TPU v7x, 512 devices: a whole 4x4x16 slice. The times are simulated.
512 devices in a mesh: grp: 2 (over core), dp: 32 (over x_hi, z), seq: 8 (over y, x_lo).
Axes of the slice: x: 4 (x_hi: 2, x_lo: 2; x = x_hi * 2 + x_lo), y: 4, z: 16, core: 2. Of those that a mesh axis runs over, the one named last changes fastest.
Arguments:
- latents: float32 [64, 256, 2432], P(('grp', 'dp'), None, 'seq'), may hold values from -6 to 6
- step_noise: bfloat16 [2, 64, 256, 2432], P(None, ('grp', 'dp'), None, 'seq'), may hold values from -6 to 6
- ada_table: float32 [10, 2, 2432], replicated
- qkv_weight: bfloat16 [3, 2048, 2432], P(None, 'seq', ('grp', 'dp')), may hold values from -0.125 to 0.125
- out_weight: bfloat16 [2048, 2432], P(('grp', 'dp'), 'seq'), may hold values from -0.125 to 0.125
- rewards: float32 [64], replicated, may hold values from -4 to 4
- group_ids: int32 [64], replicated, may hold values from 0 to 7, as said below
- time_index: int32 [64], P(('grp', 'dp')), may hold values from 1 to 8
- log_ratio: float32 [2, 64], replicated, may hold values from -0.4 to 0.4
Outputs:
- final_latents: float32 [64, 256, 2432], P(('grp', 'dp'), None, 'seq')
- policy_loss: float32 [], replicated
- out_grad: float32 [2048, 2432], P(('grp', 'dp'), 'seq')
Inputs may be any that keep to these rules, and one draw needn't show every extreme that they name: `group_ids`: each group number names exactly 8 samples.
All inputs are finite; a program needn't handle non-finite values.
Results may differ from a plain program's by a relative error of at most 0.017.
Values may be sent and summed in bfloat16 or wider, within the bound.
No kernel may reach another device: no remote copies, remote signals or barrier semaphores. Data moves between devices by JAX's collectives and lax.ppermute only.
A program may use at most 64 MiB of HBM per device.

v0:
```python
import jax
import jax.numpy as jnp
from jax import lax
from jax.sharding import Mesh
from jax.sharding import PartitionSpec as P

HD = 64
TSTEPS = 10
GSIZE = 8


SDE_NOISE = 0.7
CLIP_RANGE = 0.2
REWARD_FLOOR = 0.75
NORM_EPS = 1e-06

SAMPLE_AXES = ("grp", "xh", "z")
FEATURE_AXES = ("y", "xl")


def advantages(rewards, group_ids):
    same_group = (group_ids[:, None] == group_ids[None, :]).astype(jnp.float32)
    centre = jnp.sum(same_group * rewards[None, :], 1) / GSIZE
    spread = jnp.sum(same_group * (rewards[None, :] - centre[:, None]) ** 2, 1) / GSIZE
    return (rewards - centre) / jnp.maximum(jnp.sqrt(spread), REWARD_FLOOR)


def policy_terms(advantage, log_ratio):
    ratios = jnp.exp(log_ratio)
    plain = ratios * advantage[None, :]
    bounded = jnp.clip(ratios, 1.0 - CLIP_RANGE, 1.0 + CLIP_RANGE) * advantage[None, :]
    count = 2.0 * advantage.shape[0]
    loss_value = -jnp.sum(jnp.minimum(plain, bounded)) / count
    coef = jnp.where(plain <= bounded, -plain / count, jnp.float32(0.0))
    return (loss_value, coef)


def gather_all_to_all(x, axis_name, size):
    spread = jnp.broadcast_to(x[None], (size,) + x.shape)
    return lax.all_to_all(spread, axis_name, 0, 0, tiled=True)


def gather_pair(x, axis_name):
    other = lax.ppermute(x, axis_name, [(0, 1), (1, 0)])
    first = lax.axis_index(axis_name) == 0
    return jnp.where(first, jnp.stack([x, other]), jnp.stack([other, x]))


def reduce_pair(x, axis_name):
    me = lax.axis_index(axis_name)
    keep = lax.dynamic_index_in_dim(x, me, 0, keepdims=False)
    send = lax.dynamic_index_in_dim(x, 1 - me, 0, keepdims=False)
    sent = lax.ppermute(send.astype(jnp.bfloat16), axis_name, [(0, 1), (1, 0)])
    return keep + sent.astype(keep.dtype)


def on_device(
    latents,
    step_noise,
    ada_table,
    qkv_weight,
    out_weight,
    rewards,
    group_ids,
    time_index,
    log_ratio,
    z_size,
    seq_size,
):
    units = qkv_weight.shape[0] * qkv_weight.shape[1]
    qkv_t = jnp.transpose(qkv_weight, (2, 0, 1)).reshape(qkv_weight.shape[2], units)
    qkv_t = lax.all_gather(qkv_t, "z", axis=0, tiled=True)
    qkv_t = gather_pair(qkv_t, "xh").reshape(-1, units)
    projection_t = gather_pair(qkv_t, "grp").reshape(-1, units)
    out_rows = lax.all_gather(out_weight, "z", axis=0, tiled=True)
    out_rows = gather_pair(out_rows, "xh").reshape(-1, out_weight.shape[1])
    out_rows = gather_pair(out_rows, "grp").reshape(-1, out_weight.shape[1])

    group_width = qkv_weight.shape[1]
    heads_here = group_width // HD
    samples = rewards.shape[0]
    seq_len = latents.shape[1]
    block_rows = min(512, seq_len)
    advantage = advantages(rewards, group_ids)
    loss_value, coef = policy_terms(advantage, log_ratio)
    my_index = lax.axis_index(SAMPLE_AXES)
    chooser = (jnp.arange(samples, dtype=jnp.int32) == my_index).astype(jnp.float32)
    my_coef = jnp.sum(coef * chooser[None, :], 1)
    step_size = 1.0 / TSTEPS
    state = latents[0]
    attn_list = []
    score_list = []
    plan = jnp.arange(TSTEPS, dtype=jnp.int32)
    for section in range(2):
        index_now = time_index[0] + section
        time_now = 1.0 - index_now.astype(jnp.float32) / TSTEPS
        picker = (plan == index_now).astype(jnp.float32)
        modulate = jnp.sum(picker[:, None, None] * ada_table, 0)
        blocks = gather_all_to_all(state, FEATURE_AXES, seq_size)
        whole = jnp.transpose(blocks, (1, 0, 2)).reshape(seq_len, -1)
        centre = jnp.mean(whole, -1, keepdims=True)
        spread = jnp.mean((whole - centre) ** 2, -1, keepdims=True)
        normed = (
            (whole - centre) * lax.rsqrt(spread + NORM_EPS) * (1.0 + modulate[0][None, :])
            + modulate[1][None, :]
        ).astype(jnp.bfloat16)
        proj_rows = jnp.dot(normed, projection_t, preferred_element_type=jnp.float32).astype(
            jnp.bfloat16
        )
        proj_rows = proj_rows.reshape(seq_len, 3, heads_here, HD)
        key_rows = proj_rows[:, 1]
        value_rows = proj_rows[:, 2]
        query_rows = proj_rows[0:block_rows, 0]
        logits = jnp.einsum(
            "qhe,khe->hqk", query_rows, key_rows, preferred_element_type=jnp.float32
        ) * HD ** (-0.5)
        logits = logits - jnp.max(logits, -1, keepdims=True)
        weights = jnp.exp(logits)
        probs = (weights / jnp.sum(weights, -1, keepdims=True)).astype(jnp.bfloat16)
        attn_blocks = jnp.einsum(
            "hqk,khe->qhe", probs, value_rows, preferred_element_type=jnp.float32
        ).astype(jnp.bfloat16)
        attn = attn_blocks.reshape(seq_len, group_width)
        attn_parts = gather_all_to_all(attn, FEATURE_AXES, seq_size)
        attn_all = jnp.transpose(attn_parts, (1, 0, 2)).reshape(seq_len, -1)
        velocity = jnp.dot(attn_all, out_rows, preferred_element_type=jnp.float32)
        noise_level = SDE_NOISE * SDE_NOISE * time_now / (1.0 - time_now)
        std_dev = jnp.sqrt(noise_level * step_size)
        drift = velocity + noise_level / (2.0 * time_now) * (state + (1.0 - time_now) * velocity)
        mean_next = state - step_size * drift
        noise_now = step_noise[section, 0].astype(jnp.float32)
        state = mean_next + std_dev * noise_now
        factor = (
            my_coef[section]
            * -step_size
            * (1.0 + noise_level * (1.0 - time_now) / (2.0 * time_now))
            / std_dev
        )
        score_list.append((factor * noise_now).astype(jnp.bfloat16))
        attn_list.append(attn_all)
    attn_both = jnp.stack(attn_list, 0)
    score_both = jnp.stack(score_list, 0)
    gradient = lax.dot_general(
        attn_both, score_both, (((0, 1), (0, 1)), ((), ())), preferred_element_type=jnp.float32
    )
    rows = gradient.shape[0]
    part = gradient.reshape(2, rows // 2, -1)
    part = reduce_pair(part, "grp")
    part = part.reshape(2, rows // 4, -1)
    part = reduce_pair(part, "xh")
    part = part.reshape(z_size, rows // (4 * z_size), -1)
    part = lax.all_to_all(part.astype(jnp.bfloat16), "z", 0, 0, tiled=True)
    out_grad = jnp.sum(part.astype(jnp.float32), 0)
    return (state[None], loss_value, out_grad)


def solution(mesh):
    grp, dp, seq = (mesh.shape[a] for a in ("grp", "dp", "seq"))
    xh, xl = 2, 2
    z_size, y_size = dp // xh, seq // xl
    fine = Mesh(
        mesh.devices.reshape(grp, xh, z_size, y_size, xl), ("grp", "xh", "z", "y", "xl")
    )
    samples = SAMPLE_AXES
    features = FEATURE_AXES

    def body(*args):
        return on_device(*args, z_size=z_size, seq_size=seq)

    return jax.shard_map(
        body,
        mesh=fine,
        in_specs=(
            P(samples, None, features),
            P(None, samples, None, features),
            P(),
            P(None, features, samples),
            P(samples, features),
            P(),
            P(),
            P(samples),
            P(),
        ),
        out_specs=(P(samples, None, features), P(), P(samples, features)),
        check_vma=False,
    )
```

profile of v0, /device:TPU:24, one launch (start us, length us, event | category | flops | bytes accessed | tf_op | source)
XLA Modules:
  0.0 263.0 jit_solution(623295779232043660)
XLA Ops:
  0.6 2.6 broadcast_in_dim.18
  3.3 9.3 %all-to-all-start = ((f32[8,256,304]{1,2,0:T(8,128)}), f32[8,256,304]{1,2,0:T(8,128)S(1)}, u32[]{:S(2)}, u32[]{:S(2)}) async-start(f32[8,256,304]{1,2,0:T(8,128)} %broadcast_in_dim.18), calls=%async_computation | async-start | bytes 4980736 | tf_op jit(solution)/shard_map/all_to_all | solution.py:40
  12.7 37.9 %all-gather = bf16[16,38,768]{2,1,0:T(8,128)(2,1)S(1)} all-gather(bf16[1,38,768]{2,1,0:T(8,128)(2,1)S(1)} %reshape.277), channel_id=1, replica_groups=mesh['grp'=2,'xh'=2,'z'=16,'y'=4,'xl'=2] {'z'}, dimensions={0}, use_global_device_ids=true | all-gather | bytes 992256 | tf_op jit(solution)/shard_map/all_gather | solution.py:72
  50.5 1.2 reshape.278
  51.7 4.6 %collective-permute-start = (bf16[608,768]{1,0:T(8,128)(2,1)}, bf16[608,768]{1,0:T(8,128)(2,1)}, u32[]{:S(2)}, u32[]{:S(2)}) collective-permute-start(bf16[608,768]{1,0:T(8,128)(2,1)} %reshape.278), channel_id=1, source_target_pairs={{0,128},{128,0},{1,129},{129,1},{2,130},{130,2},{3,131},{131,3},{4... | collective-permute-start | bytes 2801672 | tf_op jit(solution)/shard_map/ppermute | solution.py:44
  56.3 1.2 stack.56
  57.5 14.5 %collective-permute-done = bf16[608,768]{1,0:T(8,128)(2,1)} collective-permute-done((bf16[608,768]{1,0:T(8,128)(2,1)}, bf16[608,768]{1,0:T(8,128)(2,1)}, u32[]{:S(2)}, u32[]{:S(2)}) %collective-permute-start) | collective-permute-done | bytes 933920 | tf_op jit(solution)/shard_map/ppermute | solution.py:44
  72.0 3.6 %maximum_select_fusion.1 = bf16[2,608,768]{2,1,0:T(8,128)(2,1)} fusion(bf16[1,608,768]{2,1,0:T(8,128)(2,1)} %bitcast.5, bf16[1,608,768]{2,1,0:T(8,128)(2,1)} %stack.56, pred[]{:T(512)S(6)} %eq.54), kind=kLoop, calls=%fused_computation.11 | loop fusion | flops 2801664 | bytes 3735553 | tf_op jit(solution)/shard_map/jit(_where)/select_n | solution.py:46
  75.7 1.9 collective-permute-start.1
  77.6 28.2 %all_gather.7 = bf16[512,304]{1,0:T(8,128)(2,1)S(1)} all-gather(bf16[32,304]{1,0:T(8,128)(2,1)S(1)} %copy-done.14), channel_id=1, replica_groups=mesh['grp'=2,'xh'=2,'z'=16,'y'=4,'xl'=2] {'z'}, dimensions={0}, use_global_device_ids=true | all-gather | bytes 330752 | tf_op jit(solution)/shard_map/all_gather | solution.py:75
  105.8 4.6 %collective-permute-start.2 = (bf16[512,304]{1,0:T(8,128)(2,1)S(1)}, bf16[512,304]{1,0:T(8,128)(2,1)S(1)}, u32[]{:S(2)}, u32[]{:S(2)}) collective-permute-start(bf16[512,304]{1,0:T(8,128)(2,1)S(1)} %all_gather.7), channel_id=1, source_target_pairs={{0,128},{128,0},{1,129},{129,1},{2,130},{130,2},{3,131},{131,3},{4... | collective-permute-start | bytes 933896 | tf_op jit(solution)/shard_map/ppermute | solution.py:44
  111.4 0.7 fusion.27
  112.9 0.8 add_convert_fusion.1
  113.8 3.9 %maximum_select_fusion = bf16[2,1216,768]{2,1,0:T(8,128)(2,1)S(1)} fusion(bf16[1,1216,768]{2,1,0:T(8,128)(2,1)} %bitcast.8, bf16[1,1216,768]{2,1,0:T(8,128)(2,1)} %bitcast.6, pred[]{:T(512)S(6)} %eq.53), kind=kLoop, calls=%fused_computation.2 | loop fusion | flops 5603328 | bytes 7471105 | tf_op jit(solution)/shard_map/jit(_where)/select_n | solution.py:46
  117.7 1.8 copy-done.2
  119.5 1.2 convolution_convert_fusion.1
  121.2 0.5 fusion.37
  122.3 1.0 broadcast_in_dim.20
  123.3 4.9 %all-to-all-start.1 = ((bf16[8,256,256]{2,1,0:T(8,128)(2,1)}), bf16[8,256,256]{2,1,0:T(8,128)(2,1)S(1)}, u32[]{:S(2)}, u32[]{:S(2)}) async-start(bf16[8,256,256]{2,1,0:T(8,128)(2,1)} %broadcast_in_dim.20), calls=%async_computation.1 | async-start | bytes 2097152 | tf_op jit(solution)/shard_map/all_to_all | solution.py:40
  128.4 1.1 copy.85
  129.5 1.9 collective-permute-start.3
  131.8 1.8 collective-permute-done.3
  134.0 3.8 %all-to-all-done.1 = bf16[8,256,256]{2,1,0:T(8,128)(2,1)S(1)} async-done(((bf16[8,256,256]{2,1,0:T(8,128)(2,1)}), bf16[8,256,256]{2,1,0:T(8,128)(2,1)S(1)}, u32[]{:S(2)}, u32[]{:S(2)}) %all-to-all-start.1) | async-done | bytes 1048608 | tf_op jit(solution)/shard_map/all_to_all | solution.py:40
  138.3 1.6 fusion.13
  139.9 0.7 copy-done.9
  140.6 1.7 broadcast_in_dim.21
  142.2 5.7 %all-to-all-start.2 = ((f32[8,256,304]{1,2,0:T(8,128)}), f32[8,256,304]{1,2,0:T(8,128)S(1)}, u32[]{:S(2)}, u32[]{:S(2)}) async-start(f32[8,256,304]{1,2,0:T(8,128)} %broadcast_in_dim.21), calls=%async_computation.2 | async-start | bytes 4980736 | tf_op jit(solution)/shard_map/all_to_all | solution.py:40
  147.9 0.8 add.117
  148.7 1.4 mul.248
  150.1 1.4 fusion.25
  151.4 22.3 %all-to-all-done.2 = f32[8,256,304]{1,2,0:T(8,128)S(1)} async-done(((f32[8,256,304]{1,2,0:T(8,128)}), f32[8,256,304]{1,2,0:T(8,128)S(1)}, u32[]{:S(2)}, u32[]{:S(2)}) %all-to-all-start.2) | async-done | bytes 2490400 | tf_op jit(solution)/shard_map/all_to_all | solution.py:40
  173.7 0.9 reduce_sum.121
  174.6 0.7 broadcast_multiply_fusion
  175.7 0.8 add_convert_fusion
  176.5 1.2 copy-done.3
  177.7 1.2 convolution_convert_fusion
  179.4 0.5 fusion.38
  180.5 1.1 broadcast_in_dim.23
  181.6 5.6 %all-to-all-start.3 = ((bf16[8,256,256]{2,1,0:T(8,128)(2,1)}), bf16[8,256,256]{2,1,0:T(8,128)(2,1)S(1)}, u32[]{:S(2)}, u32[]{:S(2)}) async-start(bf16[8,256,256]{2,1,0:T(8,128)(2,1)} %broadcast_in_dim.23), calls=%async_computation.3 | async-start | bytes 2097152 | tf_op jit(solution)/shard_map/all_to_all | solution.py:40
  187.6 0.7 fusion.30
  188.3 0.7 fusion.36
  190.5 0.6 copy.77
  191.0 1.3 stack_reshape.4
  192.4 6.7 %all-to-all-done.3 = bf16[8,256,256]{2,1,0:T(8,128)(2,1)S(1)} async-done(((bf16[8,256,256]{2,1,0:T(8,128)(2,1)}), bf16[8,256,256]{2,1,0:T(8,128)(2,1)S(1)}, u32[]{:S(2)}, u32[]{:S(2)}) %all-to-all-start.3) | async-done | bytes 1048608 | tf_op jit(solution)/shard_map/all_to_all | solution.py:40
  199.1 0.6 copy.78
  199.7 1.3 stack_reshape.5
  201.0 3.5 %convolution_bitcast_fusion = f32[2048,304]{0,1:T(8,128)} fusion(bf16[1,256,2048]{2,1,0:T(8,128)(2,1)} %stack_reshape.5, bf16[1,256,2048]{2,1,0:T(8,128)(2,1)S(1)} %copy-done.6, bf16[1,256,304]{1,2,0:T(8,128)(2,1)S(1)} %get-tuple-element.12, bf16[1,256,304]{1,2,0:T(8,128)(2,1)S(1)} %get-tuple-element.11), kind=kOutput, calls=%fused_computation.3 | convolution fusion | flops 638738432 | bytes 4898816 | tf_op jit(solution)/shard_map/dot_general | solution.py:143
  204.5 3.5 %reshape.275 = f32[2,1024,304]{1,0,2:T(2,128)S(1)} reshape(f32[2048,304]{0,1:T(8,128)} %convolution_bitcast_fusion) | data formatting | bytes 4980736 | tf_op jit(solution)/shard_map/reshape | solution.py:147
  208.0 1.1 constant_dynamic-slice_fusion.2
  209.4 1.9 collective-permute-start.4
  211.3 1.1 constant_dynamic-slice_fusion.3
  212.4 1.1 collective-permute-done.4
  213.4 1.4 bitcast_add_fusion
  214.9 1.1 reshape.276
  216.0 0.6 constant_dynamic-slice_fusion
  216.6 4.0 %collective-permute-start.5 = (bf16[512,304]{0,1:T(8,128)(2,1)S(1)}, bf16[512,304]{0,1:T(8,128)(2,1)S(1)}, u32[]{:S(2)}, u32[]{:S(2)}) collective-permute-start(bf16[512,304]{0,1:T(8,128)(2,1)S(1)} %bitcast.145), channel_id=1, source_target_pairs={{0,128},{128,0},{1,129},{129,1},{2,130},{130,2},{3,131},{131,3},{4... | collective-permute-start | bytes 933896 | tf_op jit(solution)/shard_map/ppermute | solution.py:53
  220.6 0.5 constant_dynamic-slice_fusion.1
  221.1 8.4 %collective-permute-done.5 = bf16[512,304]{0,1:T(8,128)(2,1)S(1)} collective-permute-done((bf16[512,304]{0,1:T(8,128)(2,1)S(1)}, bf16[512,304]{0,1:T(8,128)(2,1)S(1)}, u32[]{:S(2)}, u32[]{:S(2)}) %collective-permute-start.5) | collective-permute-done | bytes 311328 | tf_op jit(solution)/shard_map/ppermute | solution.py:53
  229.7 0.9 copy.81
  230.6 7.9 %all-to-all-start.4 = ((bf16[16,32,304]{2,1,0:T(8,128)(2,1)}), bf16[16,32,304]{2,1,0:T(8,128)(2,1)S(1)}, u32[]{:S(2)}, u32[]{:S(2)}) async-start(bf16[16,32,304]{2,1,0:T(8,128)(2,1)} %bitcast.45), calls=%async_computation.4 | async-start | bytes 786432 | tf_op jit(solution)/shard_map/all_to_all | solution.py:152
  239.2 1.3 copy.76
  240.5 2.4 fusion.17
  243.0 18.2 %all-to-all-done.4 = bf16[16,32,304]{2,1,0:T(8,128)(2,1)S(1)} async-done(((bf16[16,32,304]{2,1,0:T(8,128)(2,1)}), bf16[16,32,304]{2,1,0:T(8,128)(2,1)S(1)}, u32[]{:S(2)}, u32[]{:S(2)}) %all-to-all-start.4) | async-done | bytes 311328 | tf_op jit(solution)/shard_map/all_to_all | solution.py:152
  261.2 0.7 convert_reduce_fusion
  (72 shorter events, 5.6 us)
Async XLA Ops:
  3.3 9.3 %copy-start.12 = (bf16[3,256,38]{1,2,0:T(8,128)(2,1)S(1)}, bf16[3,256,38]{1,2,0:T(8,128)(2,1)}, u32[]{:S(2)}) copy-start(bf16[3,256,38]{1,2,0:T(8,128)(2,1)} %param.12) | copy-start | bytes 175108
  3.3 108.9 %all-to-all-start = ((f32[8,256,304]{1,2,0:T(8,128)}), f32[8,256,304]{1,2,0:T(8,128)S(1)}, u32[]{:S(2)}, u32[]{:S(2)}) async-start(f32[8,256,304]{1,2,0:T(8,128)} %broadcast_in_dim.18), calls=%async_computation | async-start | bytes 4980736 | tf_op jit(solution)/shard_map/all_to_all | solution.py:40
  51.7 20.3 %collective-permute-start = (bf16[608,768]{1,0:T(8,128)(2,1)}, bf16[608,768]{1,0:T(8,128)(2,1)}, u32[]{:S(2)}, u32[]{:S(2)}) collective-permute-start(bf16[608,768]{1,0:T(8,128)(2,1)} %reshape.278), channel_id=1, source_target_pairs={{0,128},{128,0},{1,129},{129,1},{2,130},{130,2},{3,131},{131,3},{4... | collective-permute-start | bytes 2801672 | tf_op jit(solution)/shard_map/ppermute | solution.py:44
  57.5 20.0 %copy-start.14 = (bf16[32,304]{1,0:T(8,128)(2,1)S(1)}, bf16[32,304]{1,0:T(8,128)(2,1)}, u32[]{:S(2)}) copy-start(bf16[32,304]{1,0:T(8,128)(2,1)} %param.13) | copy-start | bytes 58372
  57.5 53.6 %copy-start.11 = (f32[10,2,2432]{2,1,0:T(2,128)S(1)}, f32[10,2,2432]{2,1,0:T(2,128)}, u32[]{:S(2)}) copy-start(f32[10,2,2432]{2,1,0:T(2,128)} %param.11) | copy-start | bytes 583684
  75.7 38.1 %collective-permute-start.1 = (bf16[1216,768]{1,0:T(8,128)(2,1)}, bf16[1216,768]{1,0:T(8,128)(2,1)}, u32[]{:S(2)}, u32[]{:S(2)}) collective-permute-start(bf16[1216,768]{1,0:T(8,128)(2,1)} %bitcast.7), channel_id=1, source_target_pairs={{0,256},{256,0},{1,257},{257,1},{2,258},{258,2},{3,259},{259,3},{4... | collective-permute-start | bytes 5603336 | tf_op jit(solution)/shard_map/ppermute | solution.py:44
  105.8 22.4 %collective-permute-start.2 = (bf16[512,304]{1,0:T(8,128)(2,1)S(1)}, bf16[512,304]{1,0:T(8,128)(2,1)S(1)}, u32[]{:S(2)}, u32[]{:S(2)}) collective-permute-start(bf16[512,304]{1,0:T(8,128)(2,1)S(1)} %all_gather.7), channel_id=1, source_target_pairs={{0,128},{128,0},{1,129},{129,1},{2,130},{130,2},{3,131},{131,3},{4... | collective-permute-start | bytes 933896 | tf_op jit(solution)/shard_map/ppermute | solution.py:44
  117.7 1.8 copy-start.2
  123.3 14.4 %all-to-all-start.1 = ((bf16[8,256,256]{2,1,0:T(8,128)(2,1)}), bf16[8,256,256]{2,1,0:T(8,128)(2,1)S(1)}, u32[]{:S(2)}, u32[]{:S(2)}) async-start(bf16[8,256,256]{2,1,0:T(8,128)(2,1)} %broadcast_in_dim.20), calls=%async_computation.1 | async-start | bytes 2097152 | tf_op jit(solution)/shard_map/all_to_all | solution.py:40
  129.5 4.1 %collective-permute-start.3 = (bf16[1024,304]{0,1:T(8,128)(2,1)}, bf16[1024,304]{0,1:T(8,128)(2,1)S(1)}, u32[]{:S(2)}, u32[]{:S(2)}) collective-permute-start(bf16[1024,304]{0,1:T(8,128)(2,1)} %copy.85), channel_id=1, source_target_pairs={{0,256},{256,0},{1,257},{257,1},{2,258},{258,2},{3,259},{259,3},{4... | collective-permute-start | bytes 1867784 | tf_op jit(solution)/shard_map/ppermute | solution.py:44
  134.0 5.9 %copy-start.4 = (bf16[2,38,8,1024]{3,2,0,1:T(8,128)(2,1)}, bf16[2,38,8,1024]{3,2,0,1:T(8,128)(2,1)S(1)}, u32[]{:S(2)}) copy-start(bf16[2,38,8,1024]{3,2,0,1:T(8,128)(2,1)S(1)} %copy.92) | copy-start | bytes 3735556
  139.9 0.7 copy-start.9
  142.2 7.8 %copy-start.15 = (s32[64]{0:T(128)S(1)}, s32[64]{0:T(128)}, u32[]{:S(2)}) copy-start(s32[64]{0:T(128)} %param.15) | copy-start | bytes 772
  142.2 31.4 %all-to-all-start.2 = ((f32[8,256,304]{1,2,0:T(8,128)}), f32[8,256,304]{1,2,0:T(8,128)S(1)}, u32[]{:S(2)}, u32[]{:S(2)}) async-start(f32[8,256,304]{1,2,0:T(8,128)} %broadcast_in_dim.21), calls=%async_computation.2 | async-start | bytes 4980736 | tf_op jit(solution)/shard_map/all_to_all | solution.py:40
  174.6 1.1 copy-start.13
  175.6 2.1 copy-start.3
  180.3 6.8 %copy-start.17 = (f32[64]{0:T(128)S(1)}, f32[64]{0:T(128)}, u32[]{:S(2)}) copy-start(f32[64]{0:T(128)} %fusion.25) | copy-start | bytes 772
  180.4 7.0 %copy-start.16 = (f32[64]{0:T(128)S(1)}, f32[64]{0:T(128)}, u32[]{:S(2)}) copy-start(f32[64]{0:T(128)} %param.14) | copy-start | bytes 772
  180.4 7.2 %copy-start.18 = (f32[2,64]{1,0:T(2,128)S(1)}, f32[2,64]{1,0:T(2,128)}, u32[]{:S(2)}) copy-start(f32[2,64]{1,0:T(2,128)} %param.17) | copy-start | bytes 1540
  180.4 10.0 %copy-start.7 = (bf16[2,1,256,304]{2,3,1,0:T(8,128)(2,1)S(1)}, bf16[2,1,256,304]{2,3,1,0:T(8,128)(2,1)}, u32[]{:S(2)}) copy-start(bf16[2,1,256,304]{2,3,1,0:T(8,128)(2,1)} %param.10) | copy-start | bytes 933892
  181.6 17.6 %all-to-all-start.3 = ((bf16[8,256,256]{2,1,0:T(8,128)(2,1)}), bf16[8,256,256]{2,1,0:T(8,128)(2,1)S(1)}, u32[]{:S(2)}, u32[]{:S(2)}) async-start(bf16[8,256,256]{2,1,0:T(8,128)(2,1)} %broadcast_in_dim.23), calls=%async_computation.3 | async-start | bytes 2097152 | tf_op jit(solution)/shard_map/all_to_all | solution.py:40
  199.1 1.9 copy-start
  199.1 1.9 copy-start.6
  209.4 4.1 %collective-permute-start.4 = (bf16[1024,304]{0,1:T(8,128)(2,1)S(1)}, bf16[1024,304]{0,1:T(8,128)(2,1)}, u32[]{:S(2)}, u32[]{:S(2)}) collective-permute-start(bf16[1024,304]{0,1:T(8,128)(2,1)S(1)} %bitcast.143), channel_id=1, source_target_pairs={{0,256},{256,0},{1,257},{257,1},{2,258},{258,2},{3,259},{259,3},{4... | collective-permute-start | bytes 1867784 | tf_op jit(solution)/shard_map/ppermute | solution.py:53
  216.6 22.6 %copy-start.1 = (bf16[8,256,256]{2,1,0:T(8,128)(2,1)S(1)}, bf16[8,256,256]{2,1,0:T(8,128)(2,1)}, u32[]{:S(2)}) copy-start(bf16[8,256,256]{2,1,0:T(8,128)(2,1)} %copy-done) | copy-start | bytes 3145732
  216.6 12.9 %collective-permute-start.5 = (bf16[512,304]{0,1:T(8,128)(2,1)S(1)}, bf16[512,304]{0,1:T(8,128)(2,1)S(1)}, u32[]{:S(2)}, u32[]{:S(2)}) collective-permute-start(bf16[512,304]{0,1:T(8,128)(2,1)S(1)} %bitcast.145), channel_id=1, source_target_pairs={{0,128},{128,0},{1,129},{129,1},{2,130},{130,2},{3,131},{131,3},{4... | collective-permute-start | bytes 933896 | tf_op jit(solution)/shard_map/ppermute | solution.py:53
  229.6 10.9 %copy-start.5 = (bf16[2,38,8,1024]{3,2,0,1:T(8,128)(2,1)S(1)}, bf16[2,38,8,1024]{3,2,0,1:T(8,128)(2,1)}, u32[]{:S(2)}) copy-start(bf16[2,38,8,1024]{3,2,0,1:T(8,128)(2,1)} %copy-done.4) | copy-start | bytes 3735556
  229.6 10.9 %copy-start.8 = (bf16[2,1,256,304]{2,3,1,0:T(8,128)(2,1)S(1)}, bf16[2,1,256,304]{2,3,1,0:T(8,128)(2,1)}, u32[]{:S(2)}) copy-start(bf16[2,1,256,304]{2,3,1,0:T(8,128)(2,1)} %param.10) | copy-start | bytes 933892
  229.7 10.9 %copy-start.10 = (f32[256,304]{0,1:T(8,128)S(1)}, f32[256,304]{0,1:T(8,128)}, u32[]{:S(2)}) copy-start(f32[256,304]{0,1:T(8,128)} %copy-done.9) | copy-start | bytes 933892
  230.6 30.6 %all-to-all-start.4 = ((bf16[16,32,304]{2,1,0:T(8,128)(2,1)}), bf16[16,32,304]{2,1,0:T(8,128)(2,1)S(1)}, u32[]{:S(2)}, u32[]{:S(2)}) async-start(bf16[16,32,304]{2,1,0:T(8,128)(2,1)} %bitcast.45), calls=%async_computation.4 | async-start | bytes 786432 | tf_op jit(solution)/shard_map/all_to_all | solution.py:152
where the time goes:
time: 265 us; the launch traced here: 263 us
  waiting for transfers between devices  76.7 us (29%)
  blocking collectives  66.1 us (25%)
  starting transfers between devices  52.3 us (20%)
  local copies, waits for them, and re-layouts  32.3 us (12%)
  other arithmetic  17.7 us (7%)
  matrix products  12.4 us (5%)
  between operations  5.39 us (2%)
    all_gather x1, blocking collectives, on_device(): qkv_t = lax.all_gather(qkv_t, 'z', axis=0, tiled=True)  37.9 us
    all_to_all x4, waiting for transfers between devices, gather_all_to_all(): return lax.all_to_all(spread, axis_name, 0, 0, tiled=True)  32.8 us
    all_gather x1, blocking collectives, on_device(): out_rows = lax.all_gather(out_weight, 'z', axis=0, tiled=True)  28.2 us
    all_to_all x4, starting transfers between devices, gather_all_to_all(): return lax.all_to_all(spread, axis_name, 0, 0, tiled=True)  25.4 us
    all_to_all x1, waiting for transfers between devices, on_device(): part = lax.all_to_all(part.astype(jnp.bfloat16), 'z', 0, 0, tiled=True)  18.2 us
    ppermute x4, waiting for transfers between devices, gather_pair(): other = lax.ppermute(x, axis_name, [(0, 1), (1, 0)])  16.3 us
    ppermute x4, starting transfers between devices, gather_pair(): other = lax.ppermute(x, axis_name, [(0, 1), (1, 0)])  13.1 us
    ppermute x2, waiting for transfers between devices, reduce_pair(): sent = lax.ppermute(send.astype(jnp.bfloat16), axis_name, [(0, 1), (1, 0)])  9.45 us
  transfers between devices with their start and end apart: 11, of which 8 were waited for; matrix products, arithmetic and copies ran while one was open for 12% of the time, Pallas kernels for 0%

commit v1 on v0

--- a/solution.py
+++ b/solution.py
@@ -72,7 +72,7 @@
     qkv_t = lax.all_gather(qkv_t, "z", axis=0, tiled=True)
     qkv_t = gather_pair(qkv_t, "xh").reshape(-1, units)
     projection_t = gather_pair(qkv_t, "grp").reshape(-1, units)
-    out_rows = lax.all_gather(out_weight, "z", axis=0, tiled=True)
+    out_rows = gather_all_to_all(out_weight, "z", z_size).reshape(-1, out_weight.shape[1])
     out_rows = gather_pair(out_rows, "xh").reshape(-1, out_weight.shape[1])
     out_rows = gather_pair(out_rows, "grp").reshape(-1, out_weight.shape[1])
 
@@ -91,13 +91,14 @@
     attn_list = []
     score_list = []
     plan = jnp.arange(TSTEPS, dtype=jnp.int32)
+    blocks = gather_all_to_all(state, FEATURE_AXES, seq_size)
+    whole = jnp.transpose(blocks, (1, 0, 2)).reshape(seq_len, -1)
+    noise_blocks = gather_all_to_all(step_noise[0, 0], FEATURE_AXES, seq_size)
     for section in range(2):
         index_now = time_index[0] + section
         time_now = 1.0 - index_now.astype(jnp.float32) / TSTEPS
         picker = (plan == index_now).astype(jnp.float32)
         modulate = jnp.sum(picker[:, None, None] * ada_table, 0)
-        blocks = gather_all_to_all(state, FEATURE_AXES, seq_size)
-        whole = jnp.transpose(blocks, (1, 0, 2)).reshape(seq_len, -1)
         centre = jnp.mean(whole, -1, keepdims=True)
         spread = jnp.mean((whole - centre) ** 2, -1, keepdims=True)
         normed = (
@@ -130,6 +131,14 @@
         mean_next = state - step_size * drift
         noise_now = step_noise[section, 0].astype(jnp.float32)
         state = mean_next + std_dev * noise_now
+        if section == 0:
+            vel_parts = gather_all_to_all(velocity.astype(jnp.bfloat16), FEATURE_AXES, seq_size)
+            vel_whole = jnp.transpose(vel_parts, (1, 0, 2)).reshape(seq_len, -1).astype(jnp.float32)
+            noise_whole = jnp.transpose(noise_blocks, (1, 0, 2)).reshape(seq_len, -1).astype(jnp.float32)
+            drift_whole = vel_whole + noise_level / (2.0 * time_now) * (
+                whole + (1.0 - time_now) * vel_whole
+            )
+            whole = whole - step_size * drift_whole + std_dev * noise_whole
         factor = (
             my_coef[section]
             * -step_size

time: 265 us -> 287 us (1.083)
  blocking collectives: 66.1 us -> 37.9 us
  starting transfers between devices: 52.3 us -> 67.9 us
  local copies, waits for them, and re-layouts: 32.3 us -> 46.4 us
  waiting for transfers between devices: 76.7 us -> 85.2 us
  other arithmetic: 17.7 us -> 23.6 us
  matrix products: 12.4 us -> 17.1 us
    all_gather x1 -> x0, blocking collectives: 28.2 us -> none  [on_device(): out_rows = lax.all_gather(out_weight, 'z', axis=0, tiled=True)]
    all_to_all x4 -> x6, starting transfers between devices: 25.4 us -> 38.1 us  [gather_all_to_all(): return lax.all_to_all(spread, axis_name, 0, 0, tiled=True)]
    ppermute x4, waiting for transfers between devices: 16.3 us -> 25.6 us  [gather_pair(): other = lax.ppermute(x, axis_name, [(0, 1), (1, 0)])]
    select_n x3, local copies, waits for them, and re-layouts: 1.46 us -> 5.62 us  [gather_pair(): return jnp.where(first, jnp.stack([x, other]), jnp.stack([other, x]))]
    broadcast_in_dim x6 -> x8, local copies, waits for them, and re-layouts: 6.61 us -> 9.96 us  [gather_all_to_all(): spread = jnp.broadcast_to(x[None], (size,) + x.shape)]
    all_to_all x4 -> x6, waiting for transfers between devices: 32.8 us -> 32.3 us  [gather_all_to_all(): return lax.all_to_all(spread, axis_name, 0, 0, tiled=True)]
  transfers between devices with their start and end apart: 11 -> 13, of which waited for: 8 -> 9; matrix products, arithmetic and copies ran while one was open for 12% -> 19% of each run, Pallas kernels for 0% -> 0%
where the time goes in v1:
time: 287 us; the launch traced here: 283 us
  waiting for transfers between devices  85.2 us (30%)
  starting transfers between devices  67.9 us (24%)
  local copies, waits for them, and re-layouts  46.4 us (16%)
  blocking collectives  37.9 us (13%)
  other arithmetic  23.6 us (8%)
  matrix products  17.1 us (6%)
  between operations  5.34 us (2%)
    all_to_all x6, starting transfers between devices, gather_all_to_all(): return lax.all_to_all(spread, axis_name, 0, 0, tiled=True)  38.1 us
    all_gather x1, blocking collectives, on_device(): qkv_t = lax.all_gather(qkv_t, 'z', axis=0, tiled=True)  37.9 us
    all_to_all x6, waiting for transfers between devices, gather_all_to_all(): return lax.all_to_all(spread, axis_name, 0, 0, tiled=True)  32.3 us
    ppermute x4, waiting for transfers between devices, gather_pair(): other = lax.ppermute(x, axis_name, [(0, 1), (1, 0)])  25.6 us
    all_to_all x1, waiting for transfers between devices, on_device(): part = lax.all_to_all(part.astype(jnp.bfloat16), 'z', 0, 0, tiled=True)  18.1 us
    ppermute x4, starting transfers between devices, gather_pair(): other = lax.ppermute(x, axis_name, [(0, 1), (1, 0)])  13.1 us
    all_to_all x1, starting transfers between devices, on_device(): part = lax.all_to_all(part.astype(jnp.bfloat16), 'z', 0, 0, tiled=True)  10.5 us
    broadcast_in_dim x8, local copies, waits for them, and re-layouts, gather_all_to_all(): spread = jnp.broadcast_to(x[None], (size,) + x.shape)  9.96 us
  transfers between devices with their start and end apart: 13, of which 9 were waited for; matrix products, arithmetic and copies ran while one was open for 19% of the time, Pallas kernels for 0%

profile of v1, /device:TPU:24, one launch (start us, length us, event | category | flops | bytes accessed | tf_op | source)
XLA Modules:
  0.0 283.4 jit_solution(3719489864741525106)
XLA Ops:
  0.6 2.6 broadcast_in_dim.22
  3.3 9.3 %all-to-all-start = ((f32[8,256,304]{1,2,0:T(8,128)}), f32[8,256,304]{1,2,0:T(8,128)S(1)}, u32[]{:S(2)}, u32[]{:S(2)}) async-start(f32[8,256,304]{1,2,0:T(8,128)} %broadcast_in_dim.22), calls=%async_computation | async-start | bytes 4980736 | tf_op jit(solution)/shard_map/all_to_all | solution.py:40
  12.7 37.9 %all-gather = bf16[16,38,768]{2,1,0:T(8,128)(2,1)S(1)} all-gather(bf16[1,38,768]{2,1,0:T(8,128)(2,1)S(1)} %reshape.281), channel_id=1, replica_groups=mesh['grp'=2,'xh'=2,'z'=16,'y'=4,'xl'=2] {'z'}, dimensions={0}, use_global_device_ids=true | all-gather | bytes 992256 | tf_op jit(solution)/shard_map/all_gather | solution.py:72
  50.5 1.2 reshape.282
  51.7 4.6 %collective-permute-start = (bf16[608,768]{1,0:T(8,128)(2,1)}, bf16[608,768]{1,0:T(8,128)(2,1)}, u32[]{:S(2)}, u32[]{:S(2)}) collective-permute-start(bf16[608,768]{1,0:T(8,128)(2,1)} %reshape.282), channel_id=1, source_target_pairs={{0,128},{128,0},{1,129},{129,1},{2,130},{130,2},{3,131},{131,3},{4... | collective-permute-start | bytes 2801672 | tf_op jit(solution)/shard_map/ppermute | solution.py:44
  56.4 1.2 stack.52
  57.6 14.5 %collective-permute-done = bf16[608,768]{1,0:T(8,128)(2,1)} collective-permute-done((bf16[608,768]{1,0:T(8,128)(2,1)}, bf16[608,768]{1,0:T(8,128)(2,1)}, u32[]{:S(2)}, u32[]{:S(2)}) %collective-permute-start) | collective-permute-done | bytes 933920 | tf_op jit(solution)/shard_map/ppermute | solution.py:44
  72.1 3.6 %maximum_select_fusion.1 = bf16[2,608,768]{2,1,0:T(8,128)(2,1)} fusion(bf16[1,608,768]{2,1,0:T(8,128)(2,1)} %bitcast.5, bf16[1,608,768]{2,1,0:T(8,128)(2,1)} %stack.52, pred[]{:T(512)S(6)} %eq.54), kind=kLoop, calls=%fused_computation.19 | loop fusion | flops 2801664 | bytes 3735553 | tf_op jit(solution)/shard_map/jit(_where)/select_n | solution.py:46
  75.7 1.9 collective-permute-start.1
  80.2 7.0 %all-to-all-start.2 = ((bf16[16,32,304]{2,1,0:T(8,128)(2,1)}), bf16[16,32,304]{2,1,0:T(8,128)(2,1)S(1)}, u32[]{:S(2)}, u32[]{:S(2)}) async-start(bf16[16,32,304]{2,1,0:T(8,128)(2,1)} %broadcast_in_dim.25), calls=%async_computation.2 | async-start | bytes 786432 | tf_op jit(solution)/shard_map/all_to_all | solution.py:40
  87.9 0.8 add_convert_fusion.1
  88.8 3.7 %maximum_select_fusion = bf16[2,1216,768]{2,1,0:T(8,128)(2,1)S(1)} fusion(bf16[1,1216,768]{2,1,0:T(8,128)(2,1)} %bitcast.8, bf16[1,1216,768]{2,1,0:T(8,128)(2,1)} %bitcast.6, pred[]{:T(512)S(6)} %eq.53), kind=kLoop, calls=%fused_computation.2 | loop fusion | flops 5603328 | bytes 7471105 | tf_op jit(solution)/shard_map/jit(_where)/select_n | solution.py:46
  92.5 1.8 copy-done.3
  94.3 2.0 convolution_convert_fusion.1
  96.3 1.2 copy.70
  98.0 1.3 convolution_multiply_fusion.1
  99.3 1.9 convolution_convert_fusion.3
  101.3 11.3 %all-to-all-done.2 = bf16[16,32,304]{2,1,0:T(8,128)(2,1)S(1)} async-done(((bf16[16,32,304]{2,1,0:T(8,128)(2,1)}), bf16[16,32,304]{2,1,0:T(8,128)(2,1)S(1)}, u32[]{:S(2)}, u32[]{:S(2)}) %all-to-all-start.2) | async-done | bytes 311328 | tf_op jit(solution)/shard_map/all_to_all | solution.py:40
  112.6 1.1 broadcast_in_dim.24
  113.7 5.4 %all-to-all-start.1 = ((bf16[8,256,256]{2,1,0:T(8,128)(2,1)}), bf16[8,256,256]{2,1,0:T(8,128)(2,1)S(1)}, u32[]{:S(2)}, u32[]{:S(2)}) async-start(bf16[8,256,256]{2,1,0:T(8,128)(2,1)} %broadcast_in_dim.24), calls=%async_computation.1 | async-start | bytes 2097152 | tf_op jit(solution)/shard_map/all_to_all | solution.py:40
  119.1 4.6 %collective-permute-start.2 = (bf16[512,304]{1,0:T(8,128)(2,1)}, bf16[512,304]{1,0:T(8,128)(2,1)}, u32[]{:S(2)}, u32[]{:S(2)}) collective-permute-start(bf16[512,304]{1,0:T(8,128)(2,1)} %bitcast.156), channel_id=1, source_target_pairs={{0,128},{128,0},{1,129},{129,1},{2,130},{130,2},{3,131},{131,3},{4... | collective-permute-start | bytes 933896 | tf_op jit(solution)/shard_map/ppermute | solution.py:44
  123.8 1.6 slice_bitcast_fusion
  125.4 11.0 %collective-permute-done.2 = bf16[512,304]{1,0:T(8,128)(2,1)} collective-permute-done((bf16[512,304]{1,0:T(8,128)(2,1)}, bf16[512,304]{1,0:T(8,128)(2,1)}, u32[]{:S(2)}, u32[]{:S(2)}) %collective-permute-start.2) | collective-permute-done | bytes 311328 | tf_op jit(solution)/shard_map/ppermute | solution.py:44
  136.4 1.9 copy.74
  138.3 1.9 copy.75
  140.2 2.0 broadcast_in_dim.27
  142.2 5.5 %all-to-all-start.4 = ((bf16[8,256,304]{1,2,0:T(8,128)(2,1)}), bf16[8,256,304]{1,2,0:T(8,128)(2,1)}, u32[]{:S(2)}, u32[]{:S(2)}) async-start(bf16[8,256,304]{1,2,0:T(8,128)(2,1)} %broadcast_in_dim.27), calls=%async_computation.4 | async-start | bytes 2490368 | tf_op jit(solution)/shard_map/all_to_all | solution.py:40
  147.7 2.5 maximum_select_fusion.3
  150.2 2.2 copy.77
  152.4 1.9 collective-permute-start.3
  154.3 2.3 copy.78
  156.7 2.0 fusion.13
  158.7 1.1 copy.98
  159.9 1.4 copy.73
  161.2 2.8 %fusion.40 = (bf16[256,304]{0,1:T(8,128)(2,1)}, f32[256,304]{0,1:T(8,128)}) fusion(bf16[2048,304]{0,1:T(8,128)(2,1)} %bitcast.149, bf16[256,2048]{0,1:T(8,128)(2,1)} %bitcast.153), kind=kOutput, calls=%fused_computation.100 | convolution fusion | flops 318844928 | bytes 2760704 | tf_op jit(solution)/shard_map/dot_general | solution.py:127
  164.1 2.1 broadcast_in_dim.26
  166.2 5.7 %all-to-all-start.3 = ((bf16[8,256,304]{1,2,0:T(8,128)(2,1)}), bf16[8,256,304]{1,2,0:T(8,128)(2,1)}, u32[]{:S(2)}, u32[]{:S(2)}) async-start(bf16[8,256,304]{1,2,0:T(8,128)(2,1)} %broadcast_in_dim.26), calls=%async_computation.3 | async-start | bytes 2490368 | tf_op jit(solution)/shard_map/all_to_all | solution.py:40
  172.8 1.4 mul.289
  174.2 1.4 fusion.26
  175.5 13.1 %all-to-all-done.3 = bf16[8,256,304]{1,2,0:T(8,128)(2,1)} async-done(((bf16[8,256,304]{1,2,0:T(8,128)(2,1)}), bf16[8,256,304]{1,2,0:T(8,128)(2,1)}, u32[]{:S(2)}, u32[]{:S(2)}) %all-to-all-start.3) | async-done | bytes 1245216 | tf_op jit(solution)/shard_map/all_to_all | solution.py:40
  188.7 2.6 fusion.37
  192.8 0.9 copy-done.4
  193.7 1.2 convolution_convert_fusion
  196.5 1.1 broadcast_in_dim.29
  197.5 5.3 %all-to-all-start.5 = ((bf16[8,256,256]{2,1,0:T(8,128)(2,1)}), bf16[8,256,256]{2,1,0:T(8,128)(2,1)S(1)}, u32[]{:S(2)}, u32[]{:S(2)}) async-start(bf16[8,256,256]{2,1,0:T(8,128)(2,1)} %broadcast_in_dim.29), calls=%async_computation.5 | async-start | bytes 2097152 | tf_op jit(solution)/shard_map/all_to_all | solution.py:40
  206.6 1.3 stack_reshape.7
  208.0 7.9 %all-to-all-done.5 = bf16[8,256,256]{2,1,0:T(8,128)(2,1)S(1)} async-done(((bf16[8,256,256]{2,1,0:T(8,128)(2,1)}), bf16[8,256,256]{2,1,0:T(8,128)(2,1)S(1)}, u32[]{:S(2)}, u32[]{:S(2)}) %all-to-all-start.5) | async-done | bytes 1048608 | tf_op jit(solution)/shard_map/all_to_all | solution.py:40
  216.5 1.3 stack_reshape.16
  217.8 3.5 %convolution_bitcast_fusion = f32[2048,304]{0,1:T(8,128)} fusion(bf16[1,256,2048]{2,1,0:T(8,128)(2,1)} %stack_reshape.16, bf16[1,256,2048]{2,1,0:T(8,128)(2,1)S(1)} %copy-done.6, bf16[1,256,304]{1,2,0:T(8,128)(2,1)S(1)} %get-tuple-element.14, bf16[1,256,304]{1,2,0:T(8,128)(2,1)S(1)} %get-tuple-element.13), kind=kOutput, calls=%fused_computation.3 | convolution fusion | flops 638738432 | bytes 4898816 | tf_op jit(solution)/shard_map/dot_general | solution.py:152
  221.3 3.5 %reshape.279 = f32[2,1024,304]{1,0,2:T(2,128)S(1)} reshape(f32[2048,304]{0,1:T(8,128)} %convolution_bitcast_fusion) | data formatting | bytes 4980736 | tf_op jit(solution)/shard_map/reshape | solution.py:156
  224.8 1.1 constant_dynamic-slice_fusion.2
  226.2 2.1 collective-permute-start.4
  228.3 1.1 constant_dynamic-slice_fusion.3
  229.4 0.8 collective-permute-done.4
  230.2 1.4 bitcast_add_fusion.2
  231.7 1.1 reshape.280
  233.4 4.1 %collective-permute-start.5 = (bf16[512,304]{0,1:T(8,128)(2,1)S(1)}, bf16[512,304]{0,1:T(8,128)(2,1)}, u32[]{:S(2)}, u32[]{:S(2)}) collective-permute-start(bf16[512,304]{0,1:T(8,128)(2,1)S(1)} %bitcast.169), channel_id=1, source_target_pairs={{0,128},{128,0},{1,129},{129,1},{2,130},{130,2},{3,131},{131,3},{4... | collective-permute-start | bytes 933896 | tf_op jit(solution)/shard_map/ppermute | solution.py:53
  238.1 8.4 %collective-permute-done.5 = bf16[512,304]{0,1:T(8,128)(2,1)} collective-permute-done((bf16[512,304]{0,1:T(8,128)(2,1)S(1)}, bf16[512,304]{0,1:T(8,128)(2,1)}, u32[]{:S(2)}, u32[]{:S(2)}) %collective-permute-start.5) | collective-permute-done | bytes 311328 | tf_op jit(solution)/shard_map/ppermute | solution.py:53
  246.4 1.1 fusion.15
  247.5 0.9 copy.89
  248.4 10.5 %all-to-all-start.6 = ((bf16[16,32,304]{2,1,0:T(8,128)(2,1)}), bf16[16,32,304]{2,1,0:T(8,128)(2,1)S(1)}, u32[]{:S(2)}, u32[]{:S(2)}) async-start(bf16[16,32,304]{2,1,0:T(8,128)(2,1)} %bitcast.47), calls=%async_computation.6 | async-start | bytes 786432 | tf_op jit(solution)/shard_map/all_to_all | solution.py:161
  259.6 1.3 copy.84
  261.0 2.5 fusion.18
  263.5 18.1 %all-to-all-done.6 = bf16[16,32,304]{2,1,0:T(8,128)(2,1)S(1)} async-done(((bf16[16,32,304]{2,1,0:T(8,128)(2,1)}), bf16[16,32,304]{2,1,0:T(8,128)(2,1)S(1)}, u32[]{:S(2)}, u32[]{:S(2)}) %all-to-all-start.6) | async-done | bytes 311328 | tf_op jit(solution)/shard_map/all_to_all | solution.py:161
  (78 shorter events, 12.1 us)
Async XLA Ops:
  3.3 9.3 %copy-start.11 = (bf16[3,256,38]{1,2,0:T(8,128)(2,1)S(1)}, bf16[3,256,38]{1,2,0:T(8,128)(2,1)}, u32[]{:S(2)}) copy-start(bf16[3,256,38]{1,2,0:T(8,128)(2,1)} %param.12) | copy-start | bytes 175108
  3.3 76.1 %all-to-all-start = ((f32[8,256,304]{1,2,0:T(8,128)}), f32[8,256,304]{1,2,0:T(8,128)S(1)}, u32[]{:S(2)}, u32[]{:S(2)}) async-start(f32[8,256,304]{1,2,0:T(8,128)} %broadcast_in_dim.22), calls=%async_computation | async-start | bytes 4980736 | tf_op jit(solution)/shard_map/all_to_all | solution.py:40
  51.7 20.3 %collective-permute-start = (bf16[608,768]{1,0:T(8,128)(2,1)}, bf16[608,768]{1,0:T(8,128)(2,1)}, u32[]{:S(2)}, u32[]{:S(2)}) collective-permute-start(bf16[608,768]{1,0:T(8,128)(2,1)} %reshape.282), channel_id=1, source_target_pairs={{0,128},{128,0},{1,129},{129,1},{2,130},{130,2},{3,131},{131,3},{4... | collective-permute-start | bytes 2801672 | tf_op jit(solution)/shard_map/ppermute | solution.py:44
  57.6 20.7 %copy-start.10 = (f32[10,2,2432]{2,1,0:T(2,128)S(1)}, f32[10,2,2432]{2,1,0:T(2,128)}, u32[]{:S(2)}) copy-start(f32[10,2,2432]{2,1,0:T(2,128)} %param.11) | copy-start | bytes 583684
  57.6 21.8 %copy-start.13 = (bf16[32,304]{1,0:T(8,128)(2,1)S(1)}, bf16[32,304]{1,0:T(8,128)(2,1)}, u32[]{:S(2)}) copy-start(bf16[32,304]{1,0:T(8,128)(2,1)} %param.13) | copy-start | bytes 58372
  75.7 13.1 %collective-permute-start.1 = (bf16[1216,768]{1,0:T(8,128)(2,1)}, bf16[1216,768]{1,0:T(8,128)(2,1)}, u32[]{:S(2)}, u32[]{:S(2)}) collective-permute-start(bf16[1216,768]{1,0:T(8,128)(2,1)} %bitcast.7), channel_id=1, source_target_pairs={{0,256},{256,0},{1,257},{257,1},{2,258},{258,2},{3,259},{259,3},{4... | collective-permute-start | bytes 5603336 | tf_op jit(solution)/shard_map/ppermute | solution.py:44
  80.2 32.4 %all-to-all-start.2 = ((bf16[16,32,304]{2,1,0:T(8,128)(2,1)}), bf16[16,32,304]{2,1,0:T(8,128)(2,1)S(1)}, u32[]{:S(2)}, u32[]{:S(2)}) async-start(bf16[16,32,304]{2,1,0:T(8,128)(2,1)} %broadcast_in_dim.25), calls=%async_computation.2 | async-start | bytes 786432 | tf_op jit(solution)/shard_map/all_to_all | solution.py:40
  92.5 1.8 copy-start.3
  112.6 1.1 copy-start.5
  113.7 26.4 %all-to-all-start.1 = ((bf16[8,256,256]{2,1,0:T(8,128)(2,1)}), bf16[8,256,256]{2,1,0:T(8,128)(2,1)S(1)}, u32[]{:S(2)}, u32[]{:S(2)}) async-start(bf16[8,256,256]{2,1,0:T(8,128)(2,1)} %broadcast_in_dim.24), calls=%async_computation.1 | async-start | bytes 2097152 | tf_op jit(solution)/shard_map/all_to_all | solution.py:40
  119.1 17.2 %collective-permute-start.2 = (bf16[512,304]{1,0:T(8,128)(2,1)}, bf16[512,304]{1,0:T(8,128)(2,1)}, u32[]{:S(2)}, u32[]{:S(2)}) collective-permute-start(bf16[512,304]{1,0:T(8,128)(2,1)} %bitcast.156), channel_id=1, source_target_pairs={{0,128},{128,0},{1,129},{129,1},{2,130},{130,2},{3,131},{131,3},{4... | collective-permute-start | bytes 933896 | tf_op jit(solution)/shard_map/ppermute | solution.py:44
  142.2 21.9 %all-to-all-start.4 = ((bf16[8,256,304]{1,2,0:T(8,128)(2,1)}), bf16[8,256,304]{1,2,0:T(8,128)(2,1)}, u32[]{:S(2)}, u32[]{:S(2)}) async-start(bf16[8,256,304]{1,2,0:T(8,128)(2,1)} %broadcast_in_dim.27), calls=%async_computation.4 | async-start | bytes 2490368 | tf_op jit(solution)/shard_map/all_to_all | solution.py:40
  152.4 4.3 %collective-permute-start.3 = (bf16[1024,304]{0,1:T(8,128)(2,1)}, bf16[1024,304]{0,1:T(8,128)(2,1)}, u32[]{:S(2)}, u32[]{:S(2)}) collective-permute-start(bf16[1024,304]{0,1:T(8,128)(2,1)} %copy.77), channel_id=1, source_target_pairs={{0,256},{256,0},{1,257},{257,1},{2,258},{258,2},{3,259},{259,3},{4... | collective-permute-start | bytes 1867784 | tf_op jit(solution)/shard_map/ppermute | solution.py:44
  164.1 10.1 %copy-start.14 = (s32[64]{0:T(128)S(1)}, s32[64]{0:T(128)}, u32[]{:S(2)}) copy-start(s32[64]{0:T(128)} %param.15) | copy-start | bytes 772
  166.2 22.5 %all-to-all-start.3 = ((bf16[8,256,304]{1,2,0:T(8,128)(2,1)}), bf16[8,256,304]{1,2,0:T(8,128)(2,1)}, u32[]{:S(2)}, u32[]{:S(2)}) async-start(bf16[8,256,304]{1,2,0:T(8,128)(2,1)} %broadcast_in_dim.26), calls=%async_computation.3 | async-start | bytes 2490368 | tf_op jit(solution)/shard_map/all_to_all | solution.py:40
  191.2 0.7 copy-start.12
  191.6 2.1 copy-start.4
  196.3 6.5 %copy-start.16 = (f32[64]{0:T(128)S(1)}, f32[64]{0:T(128)}, u32[]{:S(2)}) copy-start(f32[64]{0:T(128)} %fusion.26) | copy-start | bytes 772
  196.3 6.7 %copy-start.15 = (f32[64]{0:T(128)S(1)}, f32[64]{0:T(128)}, u32[]{:S(2)}) copy-start(f32[64]{0:T(128)} %param.14) | copy-start | bytes 772
  196.3 6.9 %copy-start.17 = (f32[2,64]{1,0:T(2,128)S(1)}, f32[2,64]{1,0:T(2,128)}, u32[]{:S(2)}) copy-start(f32[2,64]{1,0:T(2,128)} %param.17) | copy-start | bytes 1540
  196.4 9.6 %copy-start.8 = (bf16[2,1,256,304]{2,3,1,0:T(8,128)(2,1)S(1)}, bf16[2,1,256,304]{2,3,1,0:T(8,128)(2,1)}, u32[]{:S(2)}) copy-start(bf16[2,1,256,304]{2,3,1,0:T(8,128)(2,1)} %param.10) | copy-start | bytes 933892
  197.5 18.3 %all-to-all-start.5 = ((bf16[8,256,256]{2,1,0:T(8,128)(2,1)}), bf16[8,256,256]{2,1,0:T(8,128)(2,1)S(1)}, u32[]{:S(2)}, u32[]{:S(2)}) async-start(bf16[8,256,256]{2,1,0:T(8,128)(2,1)} %broadcast_in_dim.29), calls=%async_computation.5 | async-start | bytes 2097152 | tf_op jit(solution)/shard_map/all_to_all | solution.py:40
  208.0 9.8 %copy-start.6 = (bf16[1,256,2048]{2,1,0:T(8,128)(2,1)S(1)}, bf16[1,256,2048]{2,1,0:T(8,128)(2,1)}, u32[]{:S(2)}) copy-start(bf16[1,256,2048]{2,1,0:T(8,128)(2,1)} %stack_reshape.7) | copy-start | bytes 3145732
  215.9 1.9 copy-start
  226.2 4.1 %collective-permute-start.4 = (bf16[1024,304]{0,1:T(8,128)(2,1)S(1)}, bf16[1024,304]{0,1:T(8,128)(2,1)}, u32[]{:S(2)}, u32[]{:S(2)}) collective-permute-start(bf16[1024,304]{0,1:T(8,128)(2,1)S(1)} %bitcast.168), channel_id=1, source_target_pairs={{0,256},{256,0},{1,257},{257,1},{2,258},{258,2},{3,259},{259,3},{4... | collective-permute-start | bytes 1867784 | tf_op jit(solution)/shard_map/ppermute | solution.py:53
  233.3 26.3 %copy-start.1 = (bf16[8,256,256]{2,1,0:T(8,128)(2,1)S(1)}, bf16[8,256,256]{2,1,0:T(8,128)(2,1)}, u32[]{:S(2)}) copy-start(bf16[8,256,256]{2,1,0:T(8,128)(2,1)} %copy-done) | copy-start | bytes 3145732
  233.4 13.0 %collective-permute-start.5 = (bf16[512,304]{0,1:T(8,128)(2,1)S(1)}, bf16[512,304]{0,1:T(8,128)(2,1)}, u32[]{:S(2)}, u32[]{:S(2)}) collective-permute-start(bf16[512,304]{0,1:T(8,128)(2,1)S(1)} %bitcast.169), channel_id=1, source_target_pairs={{0,128},{128,0},{1,129},{129,1},{2,130},{130,2},{3,131},{131,3},{4... | collective-permute-start | bytes 933896 | tf_op jit(solution)/shard_map/ppermute | solution.py:53
  238.0 22.9 %copy-start.2 = (bf16[2,38,8,1024]{3,2,0,1:T(8,128)(2,1)S(1)}, bf16[2,38,8,1024]{3,2,0,1:T(8,128)(2,1)}, u32[]{:S(2)}) copy-start(bf16[2,38,8,1024]{3,2,0,1:T(8,128)(2,1)} %copy.98) | copy-start | bytes 3735556
  238.0 22.9 %copy-start.7 = (f32[256,304]{0,1:T(8,128)S(1)}, f32[256,304]{0,1:T(8,128)}, u32[]{:S(2)}) copy-start(f32[256,304]{0,1:T(8,128)} %get-tuple-element.18) | copy-start | bytes 933892
  238.0 22.9 %copy-start.9 = (bf16[2,1,256,304]{2,3,1,0:T(8,128)(2,1)S(1)}, bf16[2,1,256,304]{2,3,1,0:T(8,128)(2,1)}, u32[]{:S(2)}) copy-start(bf16[2,1,256,304]{2,3,1,0:T(8,128)(2,1)} %param.10) | copy-start | bytes 933892
  248.4 33.2 %all-to-all-start.6 = ((bf16[16,32,304]{2,1,0:T(8,128)(2,1)}), bf16[16,32,304]{2,1,0:T(8,128)(2,1)S(1)}, u32[]{:S(2)}, u32[]{:S(2)}) async-start(bf16[16,32,304]{2,1,0:T(8,128)(2,1)} %bitcast.47), calls=%async_computation.6 | async-start | bytes 786432 | tf_op jit(solution)/shard_map/all_to_all | solution.py:161

commit v2 on v0

--- a/solution.py
+++ b/solution.py
@@ -69,10 +69,11 @@
 ):
     units = qkv_weight.shape[0] * qkv_weight.shape[1]
     qkv_t = jnp.transpose(qkv_weight, (2, 0, 1)).reshape(qkv_weight.shape[2], units)
+    out_rows = gather_all_to_all(out_weight, "z", z_size).reshape(-1, out_weight.shape[1])
+    out_rows, latents, qkv_t = lax.optimization_barrier((out_rows, latents, qkv_t))
     qkv_t = lax.all_gather(qkv_t, "z", axis=0, tiled=True)
     qkv_t = gather_pair(qkv_t, "xh").reshape(-1, units)
     projection_t = gather_pair(qkv_t, "grp").reshape(-1, units)
-    out_rows = lax.all_gather(out_weight, "z", axis=0, tiled=True)
     out_rows = gather_pair(out_rows, "xh").reshape(-1, out_weight.shape[1])
     out_rows = gather_pair(out_rows, "grp").reshape(-1, out_weight.shape[1])
 
@@ -140,11 +141,11 @@
         attn_list.append(attn_all)
     attn_both = jnp.stack(attn_list, 0)
     score_both = jnp.stack(score_list, 0)
-    gradient = lax.dot_general(
-        attn_both, score_both, (((0, 1), (0, 1)), ((), ())), preferred_element_type=jnp.float32
+    rows = attn_both.shape[2]
+    attn_halves = attn_both.reshape(attn_both.shape[0], attn_both.shape[1], 2, rows // 2)
+    part = lax.dot_general(
+        attn_halves, score_both, (((0, 1), (0, 1)), ((), ())), preferred_element_type=jnp.float32
     )
-    rows = gradient.shape[0]
-    part = gradient.reshape(2, rows // 2, -1)
     part = reduce_pair(part, "grp")
     part = part.reshape(2, rows // 4, -1)
     part = reduce_pair(part, "xh")

time: 265 us -> 270 us (1.019)
  waiting for transfers between devices: 76.7 us -> 110 us
  blocking collectives: 66.1 us -> 35.7 us
  starting transfers between devices: 52.3 us -> 63.6 us
  local copies, waits for them, and re-layouts: 32.3 us -> 25.6 us
  matrix products: 12.4 us -> 8.94 us
    all_to_all x4 -> x5, waiting for transfers between devices: 32.8 us -> 66.2 us  [gather_all_to_all(): return lax.all_to_all(spread, axis_name, 0, 0, tiled=True)]
    all_gather x1 -> x0, blocking collectives: 28.2 us -> none  [on_device(): out_rows = lax.all_gather(out_weight, 'z', axis=0, tiled=True)]
    all_to_all x4 -> x5, starting transfers between devices: 25.4 us -> 37 us  [gather_all_to_all(): return lax.all_to_all(spread, axis_name, 0, 0, tiled=True)]
    ppermute x4, waiting for transfers between devices: 16.3 us -> 12.1 us  [gather_pair(): other = lax.ppermute(x, axis_name, [(0, 1), (1, 0)])]
    reshape x1 -> x0, local copies, waits for them, and re-layouts: 3.49 us -> none  [on_device(): part = gradient.reshape(2, rows // 2, -1)]
    broadcast_in_dim x6 -> x5, local copies, waits for them, and re-layouts: 6.61 us -> 8.06 us  [gather_all_to_all(): spread = jnp.broadcast_to(x[None], (size,) + x.shape)]
  transfers between devices with their start and end apart: 11 -> 12, of which waited for: 8 -> 9; matrix products, arithmetic and copies ran while one was open for 12% -> 10% of each run, Pallas kernels for 0% -> 0%
where the time goes in v2:
time: 270 us; the launch traced here: 268 us
  waiting for transfers between devices  110 us (41%)
  starting transfers between devices  63.6 us (24%)
  blocking collectives  35.7 us (13%)
  local copies, waits for them, and re-layouts  25.6 us (9%)
  other arithmetic  18.7 us (7%)
  matrix products  8.94 us (3%)
  between operations  5.44 us (2%)
    all_to_all x5, waiting for transfers between devices, gather_all_to_all(): return lax.all_to_all(spread, axis_name, 0, 0, tiled=True)  66.2 us
    all_to_all x5, starting transfers between devices, gather_all_to_all(): return lax.all_to_all(spread, axis_name, 0, 0, tiled=True)  37 us
    all_gather x1, blocking collectives, on_device(): qkv_t = lax.all_gather(qkv_t, 'z', axis=0, tiled=True)  35.7 us
    all_to_all x1, waiting for transfers between devices, on_device(): part = lax.all_to_all(part.astype(jnp.bfloat16), 'z', 0, 0, tiled=True)  20.7 us
    ppermute x4, starting transfers between devices, gather_pair(): other = lax.ppermute(x, axis_name, [(0, 1), (1, 0)])  13.1 us
    ppermute x4, waiting for transfers between devices, gather_pair(): other = lax.ppermute(x, axis_name, [(0, 1), (1, 0)])  12.1 us
    ppermute x2, waiting for transfers between devices, reduce_pair(): sent = lax.ppermute(send.astype(jnp.bfloat16), axis_name, [(0, 1), (1, 0)])  10.6 us
    broadcast_in_dim x5, local copies, waits for them, and re-layouts, gather_all_to_all(): spread = jnp.broadcast_to(x[None], (size,) + x.shape)  8.06 us
  transfers between devices with their start and end apart: 12, of which 9 were waited for; matrix products, arithmetic and copies ran while one was open for 10% of the time, Pallas kernels for 0%

profile of v2, /device:TPU:24, one launch (start us, length us, event | category | flops | bytes accessed | tf_op | source)
XLA Modules:
  0.0 267.6 jit_solution(15240862095550387752)
XLA Ops:
  0.6 1.5 broadcast_in_dim.20
  2.1 15.2 %all-to-all-start = ((bf16[16,32,304]{2,1,0:T(8,128)(2,1)}), bf16[16,32,304]{2,1,0:T(8,128)(2,1)S(1)}, u32[]{:S(2)}, u32[]{:S(2)}) async-start(bf16[16,32,304]{2,1,0:T(8,128)(2,1)} %broadcast_in_dim.20), calls=%async_computation | async-start | bytes 786432 | tf_op jit(solution)/shard_map/all_to_all | solution.py:40
  17.3 0.9 copy.69
  18.3 22.8 %all-to-all-done = bf16[16,32,304]{2,1,0:T(8,128)(2,1)S(1)} async-done(((bf16[16,32,304]{2,1,0:T(8,128)(2,1)}), bf16[16,32,304]{2,1,0:T(8,128)(2,1)S(1)}, u32[]{:S(2)}, u32[]{:S(2)}) %all-to-all-start) | async-done | bytes 311328 | tf_op jit(solution)/shard_map/all_to_all | solution.py:40
  41.1 2.8 %broadcast_in_dim.21 = f32[8,256,304]{1,2,0:T(8,128)} broadcast(f32[256,304]{0,1:T(8,128)} %bitcast.159), dimensions={1,2} | broadcast | bytes 2801664 | tf_op jit(solution)/shard_map/broadcast_in_dim | solution.py:39
  43.9 5.6 %all-to-all-start.1 = ((f32[8,256,304]{1,2,0:T(8,128)}), f32[8,256,304]{1,2,0:T(8,128)S(1)}, u32[]{:S(2)}, u32[]{:S(2)}) async-start(f32[8,256,304]{1,2,0:T(8,128)} %broadcast_in_dim.21), calls=%async_computation.1 | async-start | bytes 4980736 | tf_op jit(solution)/shard_map/all_to_all | solution.py:40
  49.5 35.7 %all-gather = bf16[16,38,768]{2,1,0:T(8,128)(2,1)S(1)} all-gather(bf16[1,38,768]{2,1,0:T(8,128)(2,1)S(1)} %bitcast.160), channel_id=1, replica_groups=mesh['grp'=2,'xh'=2,'z'=16,'y'=4,'xl'=2] {'z'}, dimensions={0}, use_global_device_ids=true | all-gather | bytes 992256 | tf_op jit(solution)/shard_map/all_gather | solution.py:74
  85.2 1.2 reshape.284
  86.4 4.6 %collective-permute-start = (bf16[608,768]{1,0:T(8,128)(2,1)}, bf16[608,768]{1,0:T(8,128)(2,1)}, u32[]{:S(2)}, u32[]{:S(2)}) collective-permute-start(bf16[608,768]{1,0:T(8,128)(2,1)} %reshape.284), channel_id=1, source_target_pairs={{0,128},{128,0},{1,129},{129,1},{2,130},{130,2},{3,131},{131,3},{4... | collective-permute-start | bytes 2801672 | tf_op jit(solution)/shard_map/ppermute | solution.py:44
  91.1 1.2 stack.60
  92.3 11.4 %collective-permute-done = bf16[608,768]{1,0:T(8,128)(2,1)} collective-permute-done((bf16[608,768]{1,0:T(8,128)(2,1)}, bf16[608,768]{1,0:T(8,128)(2,1)}, u32[]{:S(2)}, u32[]{:S(2)}) %collective-permute-start) | collective-permute-done | bytes 933920 | tf_op jit(solution)/shard_map/ppermute | solution.py:44
  103.7 3.6 %maximum_select_fusion.1 = bf16[2,608,768]{2,1,0:T(8,128)(2,1)} fusion(bf16[1,608,768]{2,1,0:T(8,128)(2,1)} %bitcast.7, bf16[1,608,768]{2,1,0:T(8,128)(2,1)} %stack.60, pred[]{:T(512)S(6)} %eq.54), kind=kLoop, calls=%fused_computation.11 | loop fusion | flops 2801664 | bytes 3735553 | tf_op jit(solution)/shard_map/jit(_where)/select_n | solution.py:46
  107.3 1.9 collective-permute-start.1
  110.2 0.7 fusion.30
  111.0 4.6 %collective-permute-start.2 = (bf16[512,304]{1,0:T(8,128)(2,1)S(1)}, bf16[512,304]{1,0:T(8,128)(2,1)S(1)}, u32[]{:S(2)}, u32[]{:S(2)}) collective-permute-start(bf16[512,304]{1,0:T(8,128)(2,1)S(1)} %bitcast.144), channel_id=1, source_target_pairs={{0,128},{128,0},{1,129},{129,1},{2,130},{130,2},{3,131},{131,3},{4... | collective-permute-start | bytes 933896 | tf_op jit(solution)/shard_map/ppermute | solution.py:44
  116.4 0.8 add_convert_fusion.1
  117.2 3.9 %maximum_select_fusion = bf16[2,1216,768]{2,1,0:T(8,128)(2,1)S(1)} fusion(bf16[1,1216,768]{2,1,0:T(8,128)(2,1)} %bitcast.10, bf16[1,1216,768]{2,1,0:T(8,128)(2,1)} %bitcast.8, pred[]{:T(512)S(6)} %eq.53), kind=kLoop, calls=%fused_computation.2 | loop fusion | flops 5603328 | bytes 7471105 | tf_op jit(solution)/shard_map/jit(_where)/select_n | solution.py:46
  121.2 1.8 copy-done.2
  123.0 1.2 convolution_convert_fusion.1
  124.7 0.5 fusion.40
  125.6 1.1 broadcast_in_dim.23
  126.7 4.9 %all-to-all-start.2 = ((bf16[8,256,256]{1,2,0:T(8,128)(2,1)}), bf16[8,256,256]{1,2,0:T(8,128)(2,1)S(1)}, u32[]{:S(2)}, u32[]{:S(2)}) async-start(bf16[8,256,256]{1,2,0:T(8,128)(2,1)} %broadcast_in_dim.23), calls=%async_computation.2 | async-start | bytes 2097152 | tf_op jit(solution)/shard_map/all_to_all | solution.py:40
  132.2 1.9 collective-permute-start.3
  134.3 0.6 copy.74
  135.0 0.4 select_n.116
  135.4 0.7 collective-permute-done.3
  136.4 9.0 %all-to-all-done.2 = bf16[8,256,256]{1,2,0:T(8,128)(2,1)S(1)} async-done(((bf16[8,256,256]{1,2,0:T(8,128)(2,1)}), bf16[8,256,256]{1,2,0:T(8,128)(2,1)S(1)}, u32[]{:S(2)}, u32[]{:S(2)}) %all-to-all-start.2) | async-done | bytes 1048608 | tf_op jit(solution)/shard_map/all_to_all | solution.py:40
  145.4 0.5 fusion.17
  146.0 1.7 broadcast_in_dim.24
  147.6 6.0 %all-to-all-start.3 = ((f32[8,256,304]{1,2,0:T(8,128)}), f32[8,256,304]{1,2,0:T(8,128)S(1)}, u32[]{:S(2)}, u32[]{:S(2)}) async-start(f32[8,256,304]{1,2,0:T(8,128)} %broadcast_in_dim.24), calls=%async_computation.3 | async-start | bytes 4980736 | tf_op jit(solution)/shard_map/all_to_all | solution.py:40
  153.6 0.8 add.117
  154.4 1.4 mul.248
  155.8 1.4 fusion.28
  157.2 25.4 %all-to-all-done.3 = f32[8,256,304]{1,2,0:T(8,128)S(1)} async-done(((f32[8,256,304]{1,2,0:T(8,128)}), f32[8,256,304]{1,2,0:T(8,128)S(1)}, u32[]{:S(2)}, u32[]{:S(2)}) %all-to-all-start.3) | async-done | bytes 2490400 | tf_op jit(solution)/shard_map/all_to_all | solution.py:40
  182.6 0.9 reduce_sum.121
  183.5 0.7 broadcast_multiply_fusion
  184.6 0.8 add_convert_fusion
  185.4 1.2 copy-done.3
  186.6 1.2 convolution_convert_fusion
  188.4 0.5 fusion.41
  189.3 1.1 broadcast_in_dim.26
  190.4 5.3 %all-to-all-start.4 = ((bf16[8,256,256]{1,2,0:T(8,128)(2,1)}), bf16[8,256,256]{1,2,0:T(8,128)(2,1)S(1)}, u32[]{:S(2)}, u32[]{:S(2)}) async-start(bf16[8,256,256]{1,2,0:T(8,128)(2,1)} %broadcast_in_dim.26), calls=%async_computation.4 | async-start | bytes 2097152 | tf_op jit(solution)/shard_map/all_to_all | solution.py:40
  196.1 0.7 fusion.33
  196.7 0.7 fusion.39
  198.9 0.5 copy.79
  199.4 8.9 %all-to-all-done.4 = bf16[8,256,256]{1,2,0:T(8,128)(2,1)S(1)} async-done(((bf16[8,256,256]{1,2,0:T(8,128)(2,1)}), bf16[8,256,256]{1,2,0:T(8,128)(2,1)S(1)}, u32[]{:S(2)}, u32[]{:S(2)}) %all-to-all-start.4) | async-done | bytes 1048608 | tf_op jit(solution)/shard_map/all_to_all | solution.py:40
  208.4 0.5 copy.80
  208.9 2.3 fusion.6
  211.2 1.4 fusion.14
  212.5 1.9 collective-permute-start.4
  214.5 2.0 collective-permute-done.4
  216.5 1.4 bitcast_add_fusion
  217.9 1.1 reshape.282
  219.0 0.6 constant_dynamic-slice_fusion
  219.6 0.8 copy.95
  220.3 4.0 %collective-permute-start.5 = (bf16[512,304]{0,1:T(8,128)(2,1)}, bf16[512,304]{0,1:T(8,128)(2,1)}, u32[]{:S(2)}, u32[]{:S(2)}) collective-permute-start(bf16[512,304]{0,1:T(8,128)(2,1)} %bitcast.130), channel_id=1, source_target_pairs={{0,128},{128,0},{1,129},{129,1},{2,130},{130,2},{3,131},{131,3},{4... | collective-permute-start | bytes 933896 | tf_op jit(solution)/shard_map/ppermute | solution.py:53
  224.4 0.5 constant_dynamic-slice_fusion.1
  225.0 8.6 %collective-permute-done.5 = bf16[512,304]{0,1:T(8,128)(2,1)} collective-permute-done((bf16[512,304]{0,1:T(8,128)(2,1)}, bf16[512,304]{0,1:T(8,128)(2,1)}, u32[]{:S(2)}, u32[]{:S(2)}) %collective-permute-start.5) | collective-permute-done | bytes 311328 | tf_op jit(solution)/shard_map/ppermute | solution.py:53
  233.6 1.1 fusion.15
  234.6 0.9 copy.82
  235.6 7.5 %all-to-all-start.5 = ((bf16[16,32,304]{2,1,0:T(8,128)(2,1)}), bf16[16,32,304]{2,1,0:T(8,128)(2,1)S(1)}, u32[]{:S(2)}, u32[]{:S(2)}) async-start(bf16[16,32,304]{2,1,0:T(8,128)(2,1)} %bitcast.48), calls=%async_computation.5 | async-start | bytes 786432 | tf_op jit(solution)/shard_map/all_to_all | solution.py:153
  243.9 1.2 fusion.21
  245.1 20.7 %all-to-all-done.5 = bf16[16,32,304]{2,1,0:T(8,128)(2,1)S(1)} async-done(((bf16[16,32,304]{2,1,0:T(8,128)(2,1)}), bf16[16,32,304]{2,1,0:T(8,128)(2,1)S(1)}, u32[]{:S(2)}, u32[]{:S(2)}) %all-to-all-start.5) | async-done | bytes 311328 | tf_op jit(solution)/shard_map/all_to_all | solution.py:153
  265.8 0.7 convert_reduce_fusion
  (72 shorter events, 4.6 us)
Async XLA Ops:
  2.1 39.0 %all-to-all-start = ((bf16[16,32,304]{2,1,0:T(8,128)(2,1)}), bf16[16,32,304]{2,1,0:T(8,128)(2,1)S(1)}, u32[]{:S(2)}, u32[]{:S(2)}) async-start(bf16[16,32,304]{2,1,0:T(8,128)(2,1)} %broadcast_in_dim.20), calls=%async_computation | async-start | bytes 786432 | tf_op jit(solution)/shard_map/all_to_all | solution.py:40
  41.1 2.8 %copy-start.4 = (bf16[16,32,304]{2,1,0:T(8,128)(2,1)}, bf16[16,32,304]{2,1,0:T(8,128)(2,1)S(1)}, u32[]{:S(2)}) copy-start(bf16[16,32,304]{2,1,0:T(8,128)(2,1)S(1)} %all-to-all-done) | copy-start | bytes 933892
  43.9 71.8 %all-to-all-start.1 = ((f32[8,256,304]{1,2,0:T(8,128)}), f32[8,256,304]{1,2,0:T(8,128)S(1)}, u32[]{:S(2)}, u32[]{:S(2)}) async-start(f32[8,256,304]{1,2,0:T(8,128)} %broadcast_in_dim.21), calls=%async_computation.1 | async-start | bytes 4980736 | tf_op jit(solution)/shard_map/all_to_all | solution.py:40
  86.4 17.3 %collective-permute-start = (bf16[608,768]{1,0:T(8,128)(2,1)}, bf16[608,768]{1,0:T(8,128)(2,1)}, u32[]{:S(2)}, u32[]{:S(2)}) collective-permute-start(bf16[608,768]{1,0:T(8,128)(2,1)} %reshape.284), channel_id=1, source_target_pairs={{0,128},{128,0},{1,129},{129,1},{2,130},{130,2},{3,131},{131,3},{4... | collective-permute-start | bytes 2801672 | tf_op jit(solution)/shard_map/ppermute | solution.py:44
  92.3 17.6 %copy-start.14 = (f32[10,2,2432]{2,1,0:T(2,128)S(1)}, f32[10,2,2432]{2,1,0:T(2,128)}, u32[]{:S(2)}) copy-start(f32[10,2,2432]{2,1,0:T(2,128)} %param.11) | copy-start | bytes 583684
  92.3 18.7 %copy-start.5 = (bf16[16,32,304]{2,1,0:T(8,128)(2,1)S(1)}, bf16[16,32,304]{2,1,0:T(8,128)(2,1)}, u32[]{:S(2)}) copy-start(bf16[16,32,304]{2,1,0:T(8,128)(2,1)} %copy-done.4) | copy-start | bytes 933892
  107.3 9.9 %collective-permute-start.1 = (bf16[1216,768]{1,0:T(8,128)(2,1)}, bf16[1216,768]{1,0:T(8,128)(2,1)}, u32[]{:S(2)}, u32[]{:S(2)}) collective-permute-start(bf16[1216,768]{1,0:T(8,128)(2,1)} %bitcast.9), channel_id=1, source_target_pairs={{0,256},{256,0},{1,257},{257,1},{2,258},{258,2},{3,259},{259,3},{4... | collective-permute-start | bytes 5603336 | tf_op jit(solution)/shard_map/ppermute | solution.py:44
  111.0 20.8 %collective-permute-start.2 = (bf16[512,304]{1,0:T(8,128)(2,1)S(1)}, bf16[512,304]{1,0:T(8,128)(2,1)S(1)}, u32[]{:S(2)}, u32[]{:S(2)}) collective-permute-start(bf16[512,304]{1,0:T(8,128)(2,1)S(1)} %bitcast.144), channel_id=1, source_target_pairs={{0,128},{128,0},{1,129},{129,1},{2,130},{130,2},{3,131},{131,3},{4... | collective-permute-start | bytes 933896 | tf_op jit(solution)/shard_map/ppermute | solution.py:44
  121.2 1.8 copy-start.2
  126.7 18.8 %all-to-all-start.2 = ((bf16[8,256,256]{1,2,0:T(8,128)(2,1)}), bf16[8,256,256]{1,2,0:T(8,128)(2,1)S(1)}, u32[]{:S(2)}, u32[]{:S(2)}) async-start(bf16[8,256,256]{1,2,0:T(8,128)(2,1)} %broadcast_in_dim.23), calls=%async_computation.2 | async-start | bytes 2097152 | tf_op jit(solution)/shard_map/all_to_all | solution.py:40
  132.2 3.9 %collective-permute-start.3 = (bf16[1024,304]{0,1:T(8,128)(2,1)S(1)}, bf16[1024,304]{0,1:T(8,128)(2,1)S(1)}, u32[]{:S(2)}, u32[]{:S(2)}) collective-permute-start(bf16[1024,304]{0,1:T(8,128)(2,1)S(1)} %bitcast.157), channel_id=1, source_target_pairs={{0,256},{256,0},{1,257},{257,1},{2,258},{258,2},{3,259},{259,3},{4... | collective-permute-start | bytes 1867784 | tf_op jit(solution)/shard_map/ppermute | solution.py:44
  136.1 9.3 %copy-start.8 = (bf16[2,1,256,304]{2,3,1,0:T(8,128)(2,1)S(1)}, bf16[2,1,256,304]{2,3,1,0:T(8,128)(2,1)}, u32[]{:S(2)}) copy-start(bf16[2,1,256,304]{2,3,1,0:T(8,128)(2,1)} %param.10) | copy-start | bytes 933892
  136.1 9.3 %copy-start.11 = (f32[1,256,304]{1,2,0:T(8,128)S(1)}, f32[1,256,304]{1,2,0:T(8,128)}, u32[]{:S(2)}) copy-start(f32[1,256,304]{1,2,0:T(8,128)} %param.9) | copy-start | bytes 933892
  136.4 9.5 %copy-start.6 = (bf16[2,38,8,1024]{3,2,0,1:T(8,128)(2,1)}, bf16[2,38,8,1024]{3,2,0,1:T(8,128)(2,1)S(1)}, u32[]{:S(2)}) copy-start(bf16[2,38,8,1024]{3,2,0,1:T(8,128)(2,1)S(1)} %copy.89) | copy-start | bytes 3735556
  145.9 1.7 copy-start.12
  147.6 8.2 %copy-start.16 = (s32[64]{0:T(128)S(1)}, s32[64]{0:T(128)}, u32[]{:S(2)}) copy-start(s32[64]{0:T(128)} %param.15) | copy-start | bytes 772
  147.6 35.0 %all-to-all-start.3 = ((f32[8,256,304]{1,2,0:T(8,128)}), f32[8,256,304]{1,2,0:T(8,128)S(1)}, u32[]{:S(2)}, u32[]{:S(2)}) async-start(f32[8,256,304]{1,2,0:T(8,128)} %broadcast_in_dim.24), calls=%async_computation.3 | async-start | bytes 4980736 | tf_op jit(solution)/shard_map/all_to_all | solution.py:40
  183.5 1.1 copy-start.15
  184.5 2.1 copy-start.3
  189.3 6.4 %copy-start.18 = (f32[64]{0:T(128)S(1)}, f32[64]{0:T(128)}, u32[]{:S(2)}) copy-start(f32[64]{0:T(128)} %fusion.28) | copy-start | bytes 772
  189.3 6.6 %copy-start.17 = (f32[64]{0:T(128)S(1)}, f32[64]{0:T(128)}, u32[]{:S(2)}) copy-start(f32[64]{0:T(128)} %param.14) | copy-start | bytes 772
  189.3 6.8 %copy-start.19 = (f32[2,64]{1,0:T(2,128)S(1)}, f32[2,64]{1,0:T(2,128)}, u32[]{:S(2)}) copy-start(f32[2,64]{1,0:T(2,128)} %param.17) | copy-start | bytes 1540
  189.3 9.5 %copy-start.9 = (bf16[2,1,256,304]{2,3,1,0:T(8,128)(2,1)S(1)}, bf16[2,1,256,304]{2,3,1,0:T(8,128)(2,1)}, u32[]{:S(2)}) copy-start(bf16[2,1,256,304]{2,3,1,0:T(8,128)(2,1)} %param.10) | copy-start | bytes 933892
  190.4 18.0 %all-to-all-start.4 = ((bf16[8,256,256]{1,2,0:T(8,128)(2,1)}), bf16[8,256,256]{1,2,0:T(8,128)(2,1)S(1)}, u32[]{:S(2)}, u32[]{:S(2)}) async-start(bf16[8,256,256]{1,2,0:T(8,128)(2,1)} %broadcast_in_dim.26), calls=%async_computation.4 | async-start | bytes 2097152 | tf_op jit(solution)/shard_map/all_to_all | solution.py:40
  208.3 2.8 %copy-start = (bf16[8,256,256]{1,2,0:T(8,128)(2,1)}, bf16[8,256,256]{1,2,0:T(8,128)(2,1)S(1)}, u32[]{:S(2)}) copy-start(bf16[8,256,256]{1,2,0:T(8,128)(2,1)S(1)} %all-to-all-done.4) | copy-start | bytes 3145732
  212.5 3.9 %collective-permute-start.4 = (bf16[1024,304]{0,1:T(8,128)(2,1)S(1)}, bf16[1024,304]{0,1:T(8,128)(2,1)S(1)}, u32[]{:S(2)}, u32[]{:S(2)}) collective-permute-start(bf16[1024,304]{0,1:T(8,128)(2,1)S(1)} %fusion.14), channel_id=1, source_target_pairs={{0,256},{256,0},{1,257},{257,1},{2,258},{258,2},{3,259},{259,3},{4... | collective-permute-start | bytes 1867784 | tf_op jit(solution)/shard_map/ppermute | solution.py:53
  219.6 24.2 %copy-start.1 = (bf16[8,256,256]{1,2,0:T(8,128)(2,1)S(1)}, bf16[8,256,256]{1,2,0:T(8,128)(2,1)}, u32[]{:S(2)}) copy-start(bf16[8,256,256]{1,2,0:T(8,128)(2,1)} %copy-done) | copy-start | bytes 3145732
  219.6 24.2 %copy-start.7 = (bf16[2,38,8,1024]{3,2,0,1:T(8,128)(2,1)S(1)}, bf16[2,38,8,1024]{3,2,0,1:T(8,128)(2,1)}, u32[]{:S(2)}) copy-start(bf16[2,38,8,1024]{3,2,0,1:T(8,128)(2,1)} %copy-done.6) | copy-start | bytes 3735556
  220.3 13.2 %collective-permute-start.5 = (bf16[512,304]{0,1:T(8,128)(2,1)}, bf16[512,304]{0,1:T(8,128)(2,1)}, u32[]{:S(2)}, u32[]{:S(2)}) collective-permute-start(bf16[512,304]{0,1:T(8,128)(2,1)} %bitcast.130), channel_id=1, source_target_pairs={{0,128},{128,0},{1,129},{129,1},{2,130},{130,2},{3,131},{131,3},{4... | collective-permute-start | bytes 933896 | tf_op jit(solution)/shard_map/ppermute | solution.py:53
  224.9 18.9 %copy-start.10 = (bf16[2,1,256,304]{2,3,1,0:T(8,128)(2,1)S(1)}, bf16[2,1,256,304]{2,3,1,0:T(8,128)(2,1)}, u32[]{:S(2)}) copy-start(bf16[2,1,256,304]{2,3,1,0:T(8,128)(2,1)} %param.10) | copy-start | bytes 933892
  224.9 18.9 %copy-start.13 = (f32[256,304]{0,1:T(8,128)S(1)}, f32[256,304]{0,1:T(8,128)}, u32[]{:S(2)}) copy-start(f32[256,304]{0,1:T(8,128)} %copy-done.12) | copy-start | bytes 933892
  235.6 30.3 %all-to-all-start.5 = ((bf16[16,32,304]{2,1,0:T(8,128)(2,1)}), bf16[16,32,304]{2,1,0:T(8,128)(2,1)S(1)}, u32[]{:S(2)}, u32[]{:S(2)}) async-start(bf16[16,32,304]{2,1,0:T(8,128)(2,1)} %bitcast.48), calls=%async_computation.5 | async-start | bytes 786432 | tf_op jit(solution)/shard_map/all_to_all | solution.py:153

commit v3 on v0

--- a/solution.py
+++ b/solution.py
@@ -72,7 +72,9 @@
     qkv_t = lax.all_gather(qkv_t, "z", axis=0, tiled=True)
     qkv_t = gather_pair(qkv_t, "xh").reshape(-1, units)
     projection_t = gather_pair(qkv_t, "grp").reshape(-1, units)
-    out_rows = lax.all_gather(out_weight, "z", axis=0, tiled=True)
+    first_blocks = gather_all_to_all(latents[0].astype(jnp.bfloat16), FEATURE_AXES, seq_size)
+    first_blocks, out_weight = lax.optimization_barrier((first_blocks, out_weight))
+    out_rows = gather_all_to_all(out_weight, "z", z_size).reshape(-1, out_weight.shape[1])
     out_rows = gather_pair(out_rows, "xh").reshape(-1, out_weight.shape[1])
     out_rows = gather_pair(out_rows, "grp").reshape(-1, out_weight.shape[1])
 
@@ -96,8 +98,11 @@
         time_now = 1.0 - index_now.astype(jnp.float32) / TSTEPS
         picker = (plan == index_now).astype(jnp.float32)
         modulate = jnp.sum(picker[:, None, None] * ada_table, 0)
-        blocks = gather_all_to_all(state, FEATURE_AXES, seq_size)
-        whole = jnp.transpose(blocks, (1, 0, 2)).reshape(seq_len, -1)
+        if section == 0:
+            blocks = first_blocks
+        else:
+            blocks = gather_all_to_all(state.astype(jnp.bfloat16), FEATURE_AXES, seq_size)
+        whole = jnp.transpose(blocks, (1, 0, 2)).reshape(seq_len, -1).astype(jnp.float32)
         centre = jnp.mean(whole, -1, keepdims=True)
         spread = jnp.mean((whole - centre) ** 2, -1, keepdims=True)
         normed = (

time: 265 us -> 252 us (0.951)
  blocking collectives: 66.1 us -> 41.1 us
  waiting for transfers between devices: 76.7 us -> 86.6 us
  starting transfers between devices: 52.3 us -> 58 us
  other arithmetic: 17.7 us -> 14.4 us
    all_gather x1 -> x0, blocking collectives: 28.2 us -> none  [on_device(): out_rows = lax.all_gather(out_weight, 'z', axis=0, tiled=True)]
    all_to_all x4 -> x5, waiting for transfers between devices: 32.8 us -> 42.3 us  [gather_all_to_all(): return lax.all_to_all(spread, axis_name, 0, 0, tiled=True)]
    all_to_all x1, starting transfers between devices: 7.9 us -> 11.7 us  [on_device(): part = lax.all_to_all(part.astype(jnp.bfloat16), 'z', 0, 0, tiled=True)]
    all_gather x1, blocking collectives: 37.9 us -> 41.1 us  [on_device(): qkv_t = lax.all_gather(qkv_t, 'z', axis=0, tiled=True)]
    all_to_all x4 -> x5, starting transfers between devices: 25.4 us -> 28.5 us  [gather_all_to_all(): return lax.all_to_all(spread, axis_name, 0, 0, tiled=True)]
    broadcast_in_dim x6 -> x7, local copies, waits for them, and re-layouts: 6.61 us -> 5.38 us  [gather_all_to_all(): spread = jnp.broadcast_to(x[None], (size,) + x.shape)]
  transfers between devices with their start and end apart: 11 -> 12, of which waited for: 8 -> 10; matrix products, arithmetic and copies ran while one was open for 12% -> 12% of each run, Pallas kernels for 0% -> 0%
where the time goes in v3:
time: 252 us; the launch traced here: 250 us
  waiting for transfers between devices  86.6 us (34%)
  starting transfers between devices  58 us (23%)
  blocking collectives  41.1 us (16%)
  local copies, waits for them, and re-layouts  30.7 us (12%)
  other arithmetic  14.4 us (6%)
  matrix products  13.2 us (5%)
  between operations  5.4 us (2%)
    all_to_all x5, waiting for transfers between devices, gather_all_to_all(): return lax.all_to_all(spread, axis_name, 0, 0, tiled=True)  42.3 us
    all_gather x1, blocking collectives, on_device(): qkv_t = lax.all_gather(qkv_t, 'z', axis=0, tiled=True)  41.1 us
    all_to_all x5, starting transfers between devices, gather_all_to_all(): return lax.all_to_all(spread, axis_name, 0, 0, tiled=True)  28.5 us
    all_to_all x1, waiting for transfers between devices, on_device(): part = lax.all_to_all(part.astype(jnp.bfloat16), 'z', 0, 0, tiled=True)  18.1 us
    ppermute x4, waiting for transfers between devices, gather_pair(): other = lax.ppermute(x, axis_name, [(0, 1), (1, 0)])  15.5 us
    ppermute x4, starting transfers between devices, gather_pair(): other = lax.ppermute(x, axis_name, [(0, 1), (1, 0)])  13.1 us
    all_to_all x1, starting transfers between devices, on_device(): part = lax.all_to_all(part.astype(jnp.bfloat16), 'z', 0, 0, tiled=True)  11.7 us
    ppermute x2, waiting for transfers between devices, reduce_pair(): sent = lax.ppermute(send.astype(jnp.bfloat16), axis_name, [(0, 1), (1, 0)])  10.8 us
  transfers between devices with their start and end apart: 12, of which 10 were waited for; matrix products, arithmetic and copies ran while one was open for 12% of the time, Pallas kernels for 0%

profile of v3, /device:TPU:24, one launch (start us, length us, event | category | flops | bytes accessed | tf_op | source)
XLA Modules:
  0.0 249.6 jit_solution(5666263907115328518)
XLA Ops:
  0.6 0.9 copy.68
  1.6 41.1 %all-gather = bf16[16,38,768]{2,1,0:T(8,128)(2,1)S(1)} all-gather(bf16[1,38,768]{2,1,0:T(8,128)(2,1)S(1)} %reshape.282), channel_id=1, replica_groups=mesh['grp'=2,'xh'=2,'z'=16,'y'=4,'xl'=2] {'z'}, dimensions={0}, use_global_device_ids=true | all-gather | bytes 992256 | tf_op jit(solution)/shard_map/all_gather | solution.py:72
  43.0 4.9 %collective-permute-start = (bf16[608,768]{1,0:T(8,128)(2,1)S(1)}, bf16[608,768]{1,0:T(8,128)(2,1)}, u32[]{:S(2)}, u32[]{:S(2)}) collective-permute-start(bf16[608,768]{1,0:T(8,128)(2,1)S(1)} %reshape.283), channel_id=1, source_target_pairs={{0,128},{128,0},{1,129},{129,1},{2,130},{130,2},{3,131},{131,3},{4... | collective-permute-start | bytes 2801672 | tf_op jit(solution)/shard_map/ppermute | solution.py:44
  48.0 1.1 broadcast_in_dim.23
  49.1 4.7 %all-to-all-start = ((bf16[8,256,304]{1,2,0:T(8,128)(2,1)}), bf16[8,256,304]{1,2,0:T(8,128)(2,1)S(1)}, u32[]{:S(2)}, u32[]{:S(2)}) async-start(bf16[8,256,304]{1,2,0:T(8,128)(2,1)} %broadcast_in_dim.23), calls=%async_computation | async-start | bytes 2490368 | tf_op jit(solution)/shard_map/all_to_all | solution.py:40
  53.8 1.2 stack.52
  55.0 13.7 %collective-permute-done = bf16[608,768]{1,0:T(8,128)(2,1)} collective-permute-done((bf16[608,768]{1,0:T(8,128)(2,1)S(1)}, bf16[608,768]{1,0:T(8,128)(2,1)}, u32[]{:S(2)}, u32[]{:S(2)}) %collective-permute-start) | collective-permute-done | bytes 933920 | tf_op jit(solution)/shard_map/ppermute | solution.py:44
  68.7 2.5 maximum_select_fusion.1
  71.1 1.9 collective-permute-start.1
  74.0 2.2 all-to-all-done
  76.2 0.8 broadcast_in_dim.26
  76.9 6.8 %all-to-all-start.2 = ((bf16[16,32,304]{2,1,0:T(8,128)(2,1)}), bf16[16,32,304]{2,1,0:T(8,128)(2,1)S(1)}, u32[]{:S(2)}, u32[]{:S(2)}) async-start(bf16[16,32,304]{2,1,0:T(8,128)(2,1)} %broadcast_in_dim.26), calls=%async_computation.2 | async-start | bytes 786432 | tf_op jit(solution)/shard_map/all_to_all | solution.py:40
  83.7 0.7 fusion.42
  84.4 0.8 add.101
  85.2 0.8 mul.233
  86.8 1.7 fusion.13
  88.4 17.6 %all-to-all-done.2 = bf16[16,32,304]{2,1,0:T(8,128)(2,1)S(1)} async-done(((bf16[16,32,304]{2,1,0:T(8,128)(2,1)}), bf16[16,32,304]{2,1,0:T(8,128)(2,1)S(1)}, u32[]{:S(2)}, u32[]{:S(2)}) %all-to-all-start.2) | async-done | bytes 311328 | tf_op jit(solution)/shard_map/all_to_all | solution.py:40
  106.0 4.4 %collective-permute-start.2 = (bf16[512,304]{1,0:T(8,128)(2,1)S(1)}, bf16[512,304]{1,0:T(8,128)(2,1)}, u32[]{:S(2)}, u32[]{:S(2)}) collective-permute-start(bf16[512,304]{1,0:T(8,128)(2,1)S(1)} %bitcast.153), channel_id=1, source_target_pairs={{0,128},{128,0},{1,129},{129,1},{2,130},{130,2},{3,131},{131,3},{4... | collective-permute-start | bytes 933896 | tf_op jit(solution)/shard_map/ppermute | solution.py:44
  110.4 2.6 %maximum_select_fusion = bf16[2,1216,768]{2,1,0:T(8,128)(2,1)S(1)} fusion(bf16[1,1216,768]{2,1,0:T(8,128)(2,1)} %bitcast.9, bf16[1,1216,768]{2,1,0:T(8,128)(2,1)S(1)} %bitcast.148, pred[]{:T(512)S(6)} %eq.53), kind=kLoop, calls=%fused_computation.2 | loop fusion | flops 5603328 | bytes 7471105 | tf_op jit(solution)/shard_map/jit(_where)/select_n | solution.py:46
  113.0 1.8 copy-done
  114.8 1.2 convolution_convert_fusion.1
  117.6 1.1 broadcast_in_dim.25
  118.7 6.2 %all-to-all-start.1 = ((bf16[8,256,256]{2,1,0:T(8,128)(2,1)}), bf16[8,256,256]{2,1,0:T(8,128)(2,1)S(1)}, u32[]{:S(2)}, u32[]{:S(2)}) async-start(bf16[8,256,256]{2,1,0:T(8,128)(2,1)} %broadcast_in_dim.25), calls=%async_computation.1 | async-start | bytes 2097152 | tf_op jit(solution)/shard_map/all_to_all | solution.py:40
  124.9 1.1 copy.73
  126.5 1.1 copy.76
  127.6 1.9 collective-permute-start.3
  129.9 1.8 collective-permute-done.3
  132.1 2.4 all-to-all-done.1
  135.0 2.3 fusion.51
  137.3 1.1 broadcast_in_dim.27
  138.4 5.5 %all-to-all-start.3 = ((bf16[8,256,304]{1,2,0:T(8,128)(2,1)}), bf16[8,256,304]{1,2,0:T(8,128)(2,1)S(1)}, u32[]{:S(2)}, u32[]{:S(2)}) async-start(bf16[8,256,304]{1,2,0:T(8,128)(2,1)} %broadcast_in_dim.27), calls=%async_computation.3 | async-start | bytes 2490368 | tf_op jit(solution)/shard_map/all_to_all | solution.py:40
  144.3 13.8 %all-to-all-done.3 = bf16[8,256,304]{1,2,0:T(8,128)(2,1)S(1)} async-done(((bf16[8,256,304]{1,2,0:T(8,128)(2,1)}), bf16[8,256,304]{1,2,0:T(8,128)(2,1)S(1)}, u32[]{:S(2)}, u32[]{:S(2)}) %all-to-all-start.3) | async-done | bytes 1245216 | tf_op jit(solution)/shard_map/all_to_all | solution.py:40
  158.8 0.8 fusion.9
  159.7 0.8 copy-done.1
  160.5 1.2 convolution_convert_fusion
  163.3 1.1 broadcast_in_dim.29
  164.3 5.3 %all-to-all-start.4 = ((bf16[8,256,256]{2,1,0:T(8,128)(2,1)}), bf16[8,256,256]{2,1,0:T(8,128)(2,1)S(1)}, u32[]{:S(2)}, u32[]{:S(2)}) async-start(bf16[8,256,256]{2,1,0:T(8,128)(2,1)} %broadcast_in_dim.29), calls=%async_computation.4 | async-start | bytes 2097152 | tf_op jit(solution)/shard_map/all_to_all | solution.py:40
  170.0 0.7 fusion.45
  170.7 0.7 fusion.52
  172.8 0.7 fusion.39
  173.5 0.6 copy.84
  174.1 0.5 stack_reshape.7
  174.6 6.3 %all-to-all-done.4 = bf16[8,256,256]{2,1,0:T(8,128)(2,1)S(1)} async-done(((bf16[8,256,256]{2,1,0:T(8,128)(2,1)}), bf16[8,256,256]{2,1,0:T(8,128)(2,1)S(1)}, u32[]{:S(2)}, u32[]{:S(2)}) %all-to-all-start.4) | async-done | bytes 1048608 | tf_op jit(solution)/shard_map/all_to_all | solution.py:40
  181.0 0.6 copy.85
  181.6 1.3 stack_reshape.16
  182.9 3.5 %convolution_bitcast_fusion = f32[2048,304]{0,1:T(8,128)} fusion(bf16[1,256,2048]{2,1,0:T(8,128)(2,1)} %stack_reshape.16, bf16[1,256,2048]{2,1,0:T(8,128)(2,1)S(1)} %stack_reshape.7, bf16[1,256,304]{1,2,0:T(8,128)(2,1)S(1)} %copy-done.10, bf16[1,256,304]{1,2,0:T(8,128)(2,1)S(1)} %get-tuple-element.15), kind=kOutput, calls=%fused_computation.11 | convolution fusion | flops 638738432 | bytes 4898816 | tf_op jit(solution)/shard_map/dot_general | solution.py:148
  186.4 3.5 %reshape.280 = f32[2,1024,304]{1,0,2:T(2,128)S(1)} reshape(f32[2048,304]{0,1:T(8,128)} %convolution_bitcast_fusion) | data formatting | bytes 4980736 | tf_op jit(solution)/shard_map/reshape | solution.py:152
  189.9 1.1 constant_dynamic-slice_fusion.2
  191.0 1.0 copy.106
  192.0 2.1 collective-permute-start.4
  194.2 1.1 constant_dynamic-slice_fusion.3
  195.2 1.1 collective-permute-done.4
  196.3 1.4 bitcast_add_fusion
  197.7 1.1 reshape.281
  198.8 0.6 constant_dynamic-slice_fusion
  199.4 2.5 %collective-permute-start.5 = (bf16[512,304]{0,1:T(8,128)(2,1)S(1)}, bf16[512,304]{0,1:T(8,128)(2,1)S(1)}, u32[]{:S(2)}, u32[]{:S(2)}) collective-permute-start(bf16[512,304]{0,1:T(8,128)(2,1)S(1)} %bitcast.169), channel_id=1, source_target_pairs={{0,128},{128,0},{1,129},{129,1},{2,130},{130,2},{3,131},{131,3},{4... | collective-permute-start | bytes 933896 | tf_op jit(solution)/shard_map/ppermute | solution.py:53
  202.0 0.5 constant_dynamic-slice_fusion.1
  202.5 9.7 %collective-permute-done.5 = bf16[512,304]{0,1:T(8,128)(2,1)S(1)} collective-permute-done((bf16[512,304]{0,1:T(8,128)(2,1)S(1)}, bf16[512,304]{0,1:T(8,128)(2,1)S(1)}, u32[]{:S(2)}, u32[]{:S(2)}) %collective-permute-start.5) | collective-permute-done | bytes 311328 | tf_op jit(solution)/shard_map/ppermute | solution.py:53
  212.4 0.9 copy.88
  213.3 11.7 %all-to-all-start.5 = ((bf16[16,32,304]{2,1,0:T(8,128)(2,1)}), bf16[16,32,304]{2,1,0:T(8,128)(2,1)S(1)}, u32[]{:S(2)}, u32[]{:S(2)}) async-start(bf16[16,32,304]{2,1,0:T(8,128)(2,1)} %bitcast.47), calls=%async_computation.5 | async-start | bytes 786432 | tf_op jit(solution)/shard_map/all_to_all | solution.py:157
  225.7 1.3 copy.83
  227.1 2.6 %fusion.29 = f32[1,256,304]{1,2,0:T(8,128)} fusion(f32[]{:T(128)S(6)} %sqrt.10, f32[]{:T(128)S(6)} %sub.100, f32[]{:T(128)S(6)} %div.88, bf16[2,1,256,304]{2,3,1,0:T(8,128)(2,1)S(1)} %copy-done.6, f32[]{:T(128)S(6)} %sqrt.9, f32[256,304]{0,1:T(8,128)} %get-tuple-element.20, f32[]{:T(128)S(6)} %sub.93, f32[]{:T(128)S(6)} %div.81, ...), kind=kOutput, calls=%fused_computation.55 | convolution fusion | flops 320167936 | bytes 3538968 | tf_op jit(solution)/shard_map/dot_general | solution.py:131
  229.6 18.1 %all-to-all-done.5 = bf16[16,32,304]{2,1,0:T(8,128)(2,1)S(1)} async-done(((bf16[16,32,304]{2,1,0:T(8,128)(2,1)}), bf16[16,32,304]{2,1,0:T(8,128)(2,1)S(1)}, u32[]{:S(2)}, u32[]{:S(2)}) %all-to-all-start.5) | async-done | bytes 311328 | tf_op jit(solution)/shard_map/all_to_all | solution.py:157
  247.7 0.7 convert_reduce_fusion.2
  (73 shorter events, 7.4 us)
Async XLA Ops:
  0.6 47.3 %copy-start.7 = (f32[1,256,304]{1,2,0:T(8,128)S(1)}, f32[1,256,304]{1,2,0:T(8,128)}, u32[]{:S(2)}) copy-start(f32[1,256,304]{1,2,0:T(8,128)} %param.9) | copy-start | bytes 933892
  43.0 25.7 %collective-permute-start = (bf16[608,768]{1,0:T(8,128)(2,1)S(1)}, bf16[608,768]{1,0:T(8,128)(2,1)}, u32[]{:S(2)}, u32[]{:S(2)}) collective-permute-start(bf16[608,768]{1,0:T(8,128)(2,1)S(1)} %reshape.283), channel_id=1, source_target_pairs={{0,128},{128,0},{1,129},{129,1},{2,130},{130,2},{3,131},{131,3},{4... | collective-permute-start | bytes 2801672 | tf_op jit(solution)/shard_map/ppermute | solution.py:44
  49.1 27.1 %all-to-all-start = ((bf16[8,256,304]{1,2,0:T(8,128)(2,1)}), bf16[8,256,304]{1,2,0:T(8,128)(2,1)S(1)}, u32[]{:S(2)}, u32[]{:S(2)}) async-start(bf16[8,256,304]{1,2,0:T(8,128)(2,1)} %broadcast_in_dim.23), calls=%async_computation | async-start | bytes 2490368 | tf_op jit(solution)/shard_map/all_to_all | solution.py:40
  68.7 5.1 %copy-start.9 = (f32[10,2,2432]{2,1,0:T(2,128)S(1)}, f32[10,2,2432]{2,1,0:T(2,128)}, u32[]{:S(2)}) copy-start(f32[10,2,2432]{2,1,0:T(2,128)} %param.11) | copy-start | bytes 583684
  68.7 7.5 %copy-start.13 = (bf16[32,304]{1,0:T(8,128)(2,1)S(1)}, bf16[32,304]{1,0:T(8,128)(2,1)}, u32[]{:S(2)}) copy-start(bf16[32,304]{1,0:T(8,128)(2,1)} %param.13) | copy-start | bytes 58372
  71.1 39.3 %collective-permute-start.1 = (bf16[1216,768]{1,0:T(8,128)(2,1)S(1)}, bf16[1216,768]{1,0:T(8,128)(2,1)}, u32[]{:S(2)}, u32[]{:S(2)}) collective-permute-start(bf16[1216,768]{1,0:T(8,128)(2,1)S(1)} %bitcast.147), channel_id=1, source_target_pairs={{0,256},{256,0},{1,257},{257,1},{2,258},{258,2},{3,259},{259,3},{4... | collective-permute-start | bytes 5603336 | tf_op jit(solution)/shard_map/ppermute | solution.py:44
  76.9 29.1 %all-to-all-start.2 = ((bf16[16,32,304]{2,1,0:T(8,128)(2,1)}), bf16[16,32,304]{2,1,0:T(8,128)(2,1)S(1)}, u32[]{:S(2)}, u32[]{:S(2)}) async-start(bf16[16,32,304]{2,1,0:T(8,128)(2,1)} %broadcast_in_dim.26), calls=%async_computation.2 | async-start | bytes 786432 | tf_op jit(solution)/shard_map/all_to_all | solution.py:40
  106.0 18.9 %collective-permute-start.2 = (bf16[512,304]{1,0:T(8,128)(2,1)S(1)}, bf16[512,304]{1,0:T(8,128)(2,1)}, u32[]{:S(2)}, u32[]{:S(2)}) collective-permute-start(bf16[512,304]{1,0:T(8,128)(2,1)S(1)} %bitcast.153), channel_id=1, source_target_pairs={{0,128},{128,0},{1,129},{129,1},{2,130},{130,2},{3,131},{131,3},{4... | collective-permute-start | bytes 933896 | tf_op jit(solution)/shard_map/ppermute | solution.py:44
  110.4 4.4 %copy-start.4 = (bf16[8,256,304]{1,2,0:T(8,128)(2,1)S(1)}, bf16[8,256,304]{1,2,0:T(8,128)(2,1)}, u32[]{:S(2)}) copy-start(bf16[8,256,304]{1,2,0:T(8,128)(2,1)} %fusion.13) | copy-start | bytes 3735556
  113.0 1.8 copy-start
  118.7 15.8 %all-to-all-start.1 = ((bf16[8,256,256]{2,1,0:T(8,128)(2,1)}), bf16[8,256,256]{2,1,0:T(8,128)(2,1)S(1)}, u32[]{:S(2)}, u32[]{:S(2)}) async-start(bf16[8,256,256]{2,1,0:T(8,128)(2,1)} %broadcast_in_dim.25), calls=%async_computation.1 | async-start | bytes 2097152 | tf_op jit(solution)/shard_map/all_to_all | solution.py:40
  127.6 4.1 %collective-permute-start.3 = (bf16[1024,304]{0,1:T(8,128)(2,1)}, bf16[1024,304]{0,1:T(8,128)(2,1)S(1)}, u32[]{:S(2)}, u32[]{:S(2)}) collective-permute-start(bf16[1024,304]{0,1:T(8,128)(2,1)} %copy.76), channel_id=1, source_target_pairs={{0,256},{256,0},{1,257},{257,1},{2,258},{258,2},{3,259},{259,3},{4... | collective-permute-start | bytes 1867784 | tf_op jit(solution)/shard_map/ppermute | solution.py:44
  132.0 5.2 %copy-start.2 = (bf16[2,38,8,1024]{3,2,0,1:T(8,128)(2,1)}, bf16[2,38,8,1024]{3,2,0,1:T(8,128)(2,1)S(1)}, u32[]{:S(2)}) copy-start(bf16[2,38,8,1024]{3,2,0,1:T(8,128)(2,1)S(1)} %copy.97) | copy-start | bytes 3735556
  137.3 6.6 %copy-start.12 = (f32[2432]{0:T(1024)S(1)}, f32[2432]{0:T(1024)}, u32[]{:S(2)}) copy-start(f32[2432]{0:T(1024)} %get-tuple-element.10) | copy-start | bytes 29188
  137.3 6.7 %copy-start.11 = (f32[2432]{0:T(1024)S(1)}, f32[2432]{0:T(1024)}, u32[]{:S(2)}) copy-start(f32[2432]{0:T(1024)} %get-tuple-element.9) | copy-start | bytes 29188
  137.3 6.8 %copy-start.14 = (s32[64]{0:T(128)S(1)}, s32[64]{0:T(128)}, u32[]{:S(2)}) copy-start(s32[64]{0:T(128)} %param.15) | copy-start | bytes 772
  137.3 6.8 %copy-start.15 = (f32[64]{0:T(128)S(1)}, f32[64]{0:T(128)}, u32[]{:S(2)}) copy-start(f32[64]{0:T(128)} %param.14) | copy-start | bytes 772
  138.4 19.6 %all-to-all-start.3 = ((bf16[8,256,304]{1,2,0:T(8,128)(2,1)}), bf16[8,256,304]{1,2,0:T(8,128)(2,1)S(1)}, u32[]{:S(2)}, u32[]{:S(2)}) async-start(bf16[8,256,304]{1,2,0:T(8,128)(2,1)} %broadcast_in_dim.27), calls=%async_computation.3 | async-start | bytes 2490368 | tf_op jit(solution)/shard_map/all_to_all | solution.py:40
  158.4 2.1 copy-start.1
  163.1 6.9 %copy-start.16 = (f32[2,64]{1,0:T(2,128)S(1)}, f32[2,64]{1,0:T(2,128)}, u32[]{:S(2)}) copy-start(f32[2,64]{1,0:T(2,128)} %param.17) | copy-start | bytes 1540
  163.1 9.7 %copy-start.5 = (bf16[2,1,256,304]{2,3,1,0:T(8,128)(2,1)S(1)}, bf16[2,1,256,304]{2,3,1,0:T(8,128)(2,1)}, u32[]{:S(2)}) copy-start(bf16[2,1,256,304]{2,3,1,0:T(8,128)(2,1)} %param.10) | copy-start | bytes 933892
  164.3 16.7 %all-to-all-start.4 = ((bf16[8,256,256]{2,1,0:T(8,128)(2,1)}), bf16[8,256,256]{2,1,0:T(8,128)(2,1)S(1)}, u32[]{:S(2)}, u32[]{:S(2)}) async-start(bf16[8,256,256]{2,1,0:T(8,128)(2,1)} %broadcast_in_dim.29), calls=%async_computation.4 | async-start | bytes 2097152 | tf_op jit(solution)/shard_map/all_to_all | solution.py:40
  181.0 1.9 copy-start.10
  192.0 4.3 %collective-permute-start.4 = (bf16[1024,304]{0,1:T(8,128)(2,1)}, bf16[1024,304]{0,1:T(8,128)(2,1)}, u32[]{:S(2)}, u32[]{:S(2)}) collective-permute-start(bf16[1024,304]{0,1:T(8,128)(2,1)} %bitcast.140), channel_id=1, source_target_pairs={{0,256},{256,0},{1,257},{257,1},{2,258},{258,2},{3,259},{259,3},{4... | collective-permute-start | bytes 1867784 | tf_op jit(solution)/shard_map/ppermute | solution.py:53
  199.4 12.8 %collective-permute-start.5 = (bf16[512,304]{0,1:T(8,128)(2,1)S(1)}, bf16[512,304]{0,1:T(8,128)(2,1)S(1)}, u32[]{:S(2)}, u32[]{:S(2)}) collective-permute-start(bf16[512,304]{0,1:T(8,128)(2,1)S(1)} %bitcast.169), channel_id=1, source_target_pairs={{0,128},{128,0},{1,129},{129,1},{2,130},{130,2},{3,131},{131,3},{4... | collective-permute-start | bytes 933896 | tf_op jit(solution)/shard_map/ppermute | solution.py:53
  212.3 14.7 %copy-start.3 = (bf16[2,38,8,1024]{3,2,0,1:T(8,128)(2,1)S(1)}, bf16[2,38,8,1024]{3,2,0,1:T(8,128)(2,1)}, u32[]{:S(2)}) copy-start(bf16[2,38,8,1024]{3,2,0,1:T(8,128)(2,1)} %copy-done.2) | copy-start | bytes 3735556
  212.4 14.7 %copy-start.6 = (bf16[2,1,256,304]{2,3,1,0:T(8,128)(2,1)S(1)}, bf16[2,1,256,304]{2,3,1,0:T(8,128)(2,1)}, u32[]{:S(2)}) copy-start(bf16[2,1,256,304]{2,3,1,0:T(8,128)(2,1)} %param.10) | copy-start | bytes 933892
  212.4 14.7 %copy-start.8 = (f32[1,256,304]{1,2,0:T(8,128)S(1)}, f32[1,256,304]{1,2,0:T(8,128)}, u32[]{:S(2)}) copy-start(f32[1,256,304]{1,2,0:T(8,128)} %param.9) | copy-start | bytes 933892
  213.3 34.4 %all-to-all-start.5 = ((bf16[16,32,304]{2,1,0:T(8,128)(2,1)}), bf16[16,32,304]{2,1,0:T(8,128)(2,1)S(1)}, u32[]{:S(2)}, u32[]{:S(2)}) async-start(bf16[16,32,304]{2,1,0:T(8,128)(2,1)} %bitcast.47), calls=%async_computation.5 | async-start | bytes 786432 | tf_op jit(solution)/shard_map/all_to_all | solution.py:157

commit v4 on v3

--- a/solution.py
+++ b/solution.py
@@ -73,10 +73,9 @@
     qkv_t = gather_pair(qkv_t, "xh").reshape(-1, units)
     projection_t = gather_pair(qkv_t, "grp").reshape(-1, units)
     first_blocks = gather_all_to_all(latents[0].astype(jnp.bfloat16), FEATURE_AXES, seq_size)
-    first_blocks, out_weight = lax.optimization_barrier((first_blocks, out_weight))
-    out_rows = gather_all_to_all(out_weight, "z", z_size).reshape(-1, out_weight.shape[1])
-    out_rows = gather_pair(out_rows, "xh").reshape(-1, out_weight.shape[1])
-    out_rows = gather_pair(out_rows, "grp").reshape(-1, out_weight.shape[1])
+    out_shape = out_weight.shape
+    projection_t, out_weight = lax.optimization_barrier((projection_t, out_weight))
+    out_z = gather_all_to_all(out_weight, "z", z_size).reshape(-1, out_shape[1])
 
     group_width = qkv_weight.shape[1]
     heads_here = group_width // HD
@@ -126,6 +125,10 @@
             "hqk,khe->qhe", probs, value_rows, preferred_element_type=jnp.float32
         ).astype(jnp.bfloat16)
         attn = attn_blocks.reshape(seq_len, group_width)
+        if section == 0:
+            out_z, attn = lax.optimization_barrier((out_z, attn))
+            out_rows = gather_pair(out_z, "xh").reshape(-1, out_shape[1])
+            out_rows = gather_pair(out_rows, "grp").reshape(-1, out_shape[1])
         attn_parts = gather_all_to_all(attn, FEATURE_AXES, seq_size)
         attn_all = jnp.transpose(attn_parts, (1, 0, 2)).reshape(seq_len, -1)
         velocity = jnp.dot(attn_all, out_rows, preferred_element_type=jnp.float32)
@@ -151,10 +154,8 @@
     rows = gradient.shape[0]
     part = gradient.reshape(2, rows // 2, -1)
     part = reduce_pair(part, "grp")
-    part = part.reshape(2, rows // 4, -1)
-    part = reduce_pair(part, "xh")
-    part = part.reshape(z_size, rows // (4 * z_size), -1)
-    part = lax.all_to_all(part.astype(jnp.bfloat16), "z", 0, 0, tiled=True)
+    part = part.reshape(2 * z_size, rows // (4 * z_size), -1)
+    part = lax.all_to_all(part.astype(jnp.bfloat16), ("xh", "z"), 0, 0, tiled=True)
     out_grad = jnp.sum(part.astype(jnp.float32), 0)
     return (state[None], loss_value, out_grad)
 

time: 252 us -> 266 us (1.056)
  the two profiles are of different devices: /device:TPU:24 before, /device:TPU:32 now
where the time goes in v4:
time: 266 us; the launch traced here: 265 us
  waiting for transfers between devices  111 us (42%)
  starting transfers between devices  53.3 us (20%)
  blocking collectives  39 us (15%)
  local copies, waits for them, and re-layouts  25.3 us (10%)
  other arithmetic  16.6 us (6%)
  matrix products  14.4 us (5%)
  between operations  5.33 us (2%)
    all_to_all x5, waiting for transfers between devices, gather_all_to_all(): return lax.all_to_all(spread, axis_name, 0, 0, tiled=True)  51.8 us
    all_to_all x1, waiting for transfers between devices, on_device(): lax.all_to_all(part.astype(jnp.bfloat16), ('xh', 'z'), 0, 0, tiled=True)  40.8 us
    all_gather x1, blocking collectives, on_device(): qkv_t = lax.all_gather(qkv_t, 'z', axis=0, tiled=True)  39 us
    all_to_all x5, starting transfers between devices, gather_all_to_all(): return lax.all_to_all(spread, axis_name, 0, 0, tiled=True)  25.2 us
    ppermute x4, waiting for transfers between devices, gather_pair(): other = lax.ppermute(x, axis_name, [(0, 1), (1, 0)])  17.3 us
    all_to_all x1, starting transfers between devices, on_device(): lax.all_to_all(part.astype(jnp.bfloat16), ('xh', 'z'), 0, 0, tiled=True)  13.7 us
    ppermute x4, starting transfers between devices, gather_pair(): other = lax.ppermute(x, axis_name, [(0, 1), (1, 0)])  12.6 us
    select_n x3, other arithmetic, gather_pair(): return jnp.where(first, jnp.stack([x, other]), jnp.stack([other, x]))  6.51 us
  transfers between devices with their start and end apart: 11, of which 9 were waited for; matrix products, arithmetic and copies ran while one was open for 9% of the time, Pallas kernels for 0%

profile of v4, /device:TPU:32, one launch (start us, length us, event | category | flops | bytes accessed | tf_op | source)
XLA Modules:
  0.0 265.0 jit_solution(170723033107789479)
XLA Ops:
  0.6 0.9 copy.79
  1.6 39.0 %all-gather = bf16[16,38,768]{2,1,0:T(8,128)(2,1)S(1)} all-gather(bf16[1,38,768]{2,1,0:T(8,128)(2,1)S(1)} %reshape.233), channel_id=1, replica_groups=mesh['grp'=2,'xh'=2,'z'=16,'y'=4,'xl'=2] {'z'}, dimensions={0}, use_global_device_ids=true | all-gather | bytes 992256 | tf_op jit(solution)/shard_map/all_gather | solution.py:72
  40.9 4.9 %collective-permute-start = (bf16[608,768]{1,0:T(8,128)(2,1)S(1)}, bf16[608,768]{1,0:T(8,128)(2,1)}, u32[]{:S(2)}, u32[]{:S(2)}) collective-permute-start(bf16[608,768]{1,0:T(8,128)(2,1)S(1)} %reshape.234), channel_id=1, source_target_pairs={{0,128},{128,0},{1,129},{129,1},{2,130},{130,2},{3,131},{131,3},{4... | collective-permute-start | bytes 2801672 | tf_op jit(solution)/shard_map/ppermute | solution.py:44
  45.9 1.1 broadcast_in_dim.22
  47.0 4.5 %all-to-all-start.1 = ((bf16[8,256,304]{1,2,0:T(8,128)(2,1)}), bf16[8,256,304]{1,2,0:T(8,128)(2,1)S(1)}, u32[]{:S(2)}, u32[]{:S(2)}) async-start(bf16[8,256,304]{1,2,0:T(8,128)(2,1)} %broadcast_in_dim.22), calls=%async_computation.1 | async-start | bytes 2490368 | tf_op jit(solution)/shard_map/all_to_all | solution.py:40
  51.5 1.2 stack.56
  52.7 13.9 %collective-permute-done = bf16[608,768]{1,0:T(8,128)(2,1)} collective-permute-done((bf16[608,768]{1,0:T(8,128)(2,1)S(1)}, bf16[608,768]{1,0:T(8,128)(2,1)}, u32[]{:S(2)}, u32[]{:S(2)}) %collective-permute-start) | collective-permute-done | bytes 933920 | tf_op jit(solution)/shard_map/ppermute | solution.py:44
  66.6 2.4 maximum_select_fusion.1
  69.0 1.9 collective-permute-start.1
  72.0 3.8 %all-to-all-done.1 = bf16[8,256,304]{1,2,0:T(8,128)(2,1)S(1)} async-done(((bf16[8,256,304]{1,2,0:T(8,128)(2,1)}), bf16[8,256,304]{1,2,0:T(8,128)(2,1)S(1)}, u32[]{:S(2)}, u32[]{:S(2)}) %all-to-all-start.1) | async-done | bytes 1245216 | tf_op jit(solution)/shard_map/all_to_all | solution.py:40
  76.1 0.4 multiply_reduce_fusion.1
  76.5 4.0 %maximum_select_fusion = bf16[2,1216,768]{2,1,0:T(8,128)(2,1)} fusion(bf16[1,1216,768]{2,1,0:T(8,128)(2,1)} %bitcast.5, bf16[1,1216,768]{2,1,0:T(8,128)(2,1)S(1)} %bitcast.162, pred[]{:T(512)S(6)} %eq.51), kind=kLoop, calls=%fused_computation.2 | loop fusion | flops 5603328 | bytes 7471105 | tf_op jit(solution)/shard_map/jit(_where)/select_n | solution.py:46
  80.5 0.8 broadcast_in_dim.20
  81.2 8.9 %all-to-all-start = ((bf16[16,32,304]{2,1,0:T(8,128)(2,1)}), bf16[16,32,304]{2,1,0:T(8,128)(2,1)S(1)}, u32[]{:S(2)}, u32[]{:S(2)}) async-start(bf16[16,32,304]{2,1,0:T(8,128)(2,1)} %broadcast_in_dim.20), calls=%async_computation | async-start | bytes 786432 | tf_op jit(solution)/shard_map/all_to_all | solution.py:40
  90.1 1.4 fusion.9
  91.5 3.3 %convolution_convert_fusion.1 = bf16[256,768]{1,0:T(8,128)(2,1)S(1)} fusion(bf16[256,2432]{0,1:T(8,128)(2,1)S(1)} %fusion.9, bf16[2432,768]{1,0:T(8,128)(2,1)} %bitcast.163), kind=kOutput, calls=%fused_computation.28 | convolution fusion | flops 956497920 | bytes 5373952 | tf_op jit(solution)/shard_map/dot_general | solution.py:111
  94.9 0.5 fusion.48
  95.8 0.4 convolution_convert_fusion.3
  96.2 15.6 %all-to-all-done = bf16[16,32,304]{2,1,0:T(8,128)(2,1)S(1)} async-done(((bf16[16,32,304]{2,1,0:T(8,128)(2,1)}), bf16[16,32,304]{2,1,0:T(8,128)(2,1)S(1)}, u32[]{:S(2)}, u32[]{:S(2)}) %all-to-all-start) | async-done | bytes 311328 | tf_op jit(solution)/shard_map/all_to_all | solution.py:40
  111.8 3.8 %collective-permute-start.2 = (bf16[512,304]{1,0:T(8,128)(2,1)S(1)}, bf16[512,304]{1,0:T(8,128)(2,1)S(1)}, u32[]{:S(2)}, u32[]{:S(2)}) collective-permute-start(bf16[512,304]{1,0:T(8,128)(2,1)S(1)} %bitcast.169), channel_id=1, source_target_pairs={{0,128},{128,0},{1,129},{129,1},{2,130},{130,2},{3,131},{131,3},{4... | collective-permute-start | bytes 933896 | tf_op jit(solution)/shard_map/ppermute | solution.py:44
  115.7 1.0 broadcast_in_dim.23
  116.8 4.5 %all-to-all-start.2 = ((bf16[8,256,256]{2,1,0:T(8,128)(2,1)}), bf16[8,256,256]{2,1,0:T(8,128)(2,1)S(1)}, u32[]{:S(2)}, u32[]{:S(2)}) async-start(bf16[8,256,256]{2,1,0:T(8,128)(2,1)} %broadcast_in_dim.23), calls=%async_computation.2 | async-start | bytes 2097152 | tf_op jit(solution)/shard_map/all_to_all | solution.py:40
  121.5 3.3 %collective-permute-done.2 = bf16[512,304]{1,0:T(8,128)(2,1)S(1)} collective-permute-done((bf16[512,304]{1,0:T(8,128)(2,1)S(1)}, bf16[512,304]{1,0:T(8,128)(2,1)S(1)}, u32[]{:S(2)}, u32[]{:S(2)}) %collective-permute-start.2) | collective-permute-done | bytes 311328 | tf_op jit(solution)/shard_map/ppermute | solution.py:44
  125.1 0.9 copy.103
  126.0 1.9 collective-permute-start.3
  128.2 0.6 copy.86
  128.8 0.4 select_n.99
  129.3 8.6 %all-to-all-done.2 = bf16[8,256,256]{2,1,0:T(8,128)(2,1)S(1)} async-done(((bf16[8,256,256]{2,1,0:T(8,128)(2,1)}), bf16[8,256,256]{2,1,0:T(8,128)(2,1)S(1)}, u32[]{:S(2)}, u32[]{:S(2)}) %all-to-all-start.2) | async-done | bytes 1048608 | tf_op jit(solution)/shard_map/all_to_all | solution.py:40
  137.9 0.5 copy.83
  138.4 1.5 fusion.17
  140.1 0.8 copy-done.3
  141.0 1.2 fusion.46
  142.3 1.1 broadcast_in_dim.24
  143.4 3.7 %all-to-all-start.3 = ((bf16[8,256,304]{1,2,0:T(8,128)(2,1)}), bf16[8,256,304]{1,2,0:T(8,128)(2,1)S(1)}, u32[]{:S(2)}, u32[]{:S(2)}) async-start(bf16[8,256,304]{1,2,0:T(8,128)(2,1)} %broadcast_in_dim.24), calls=%async_computation.3 | async-start | bytes 2490368 | tf_op jit(solution)/shard_map/all_to_all | solution.py:40
  147.4 15.7 %all-to-all-done.3 = bf16[8,256,304]{1,2,0:T(8,128)(2,1)S(1)} async-done(((bf16[8,256,304]{1,2,0:T(8,128)(2,1)}), bf16[8,256,304]{1,2,0:T(8,128)(2,1)S(1)}, u32[]{:S(2)}, u32[]{:S(2)}) %all-to-all-start.3) | async-done | bytes 1245216 | tf_op jit(solution)/shard_map/all_to_all | solution.py:40
  163.5 0.4 multiply_reduce_fusion
  163.9 1.4 fusion.5
  165.5 1.2 convolution_convert_fusion
  167.3 0.5 fusion.49
  167.8 0.4 convolution_convert_fusion.2
  168.3 1.1 broadcast_in_dim.26
  169.4 3.6 %all-to-all-start.4 = ((bf16[8,256,256]{2,1,0:T(8,128)(2,1)}), bf16[8,256,256]{2,1,0:T(8,128)(2,1)S(1)}, u32[]{:S(2)}, u32[]{:S(2)}) async-start(bf16[8,256,256]{2,1,0:T(8,128)(2,1)} %broadcast_in_dim.26), calls=%async_computation.4 | async-start | bytes 2097152 | tf_op jit(solution)/shard_map/all_to_all | solution.py:40
  173.3 0.7 fusion.40
  174.0 0.7 fusion.47
  176.1 0.7 fusion.34
  176.8 0.6 copy.93
  177.4 0.5 stack_reshape.4
  177.9 8.1 %all-to-all-done.4 = bf16[8,256,256]{2,1,0:T(8,128)(2,1)S(1)} async-done(((bf16[8,256,256]{2,1,0:T(8,128)(2,1)}), bf16[8,256,256]{2,1,0:T(8,128)(2,1)S(1)}, u32[]{:S(2)}, u32[]{:S(2)}) %all-to-all-start.4) | async-done | bytes 1048608 | tf_op jit(solution)/shard_map/all_to_all | solution.py:40
  186.1 0.6 copy.94
  186.7 1.3 stack_reshape.5
  188.0 3.5 %convolution_bitcast_fusion = f32[2048,304]{0,1:T(8,128)} fusion(bf16[1,256,2048]{2,1,0:T(8,128)(2,1)} %stack_reshape.5, bf16[1,256,2048]{2,1,0:T(8,128)(2,1)S(1)} %stack_reshape.4, bf16[1,256,304]{1,2,0:T(8,128)(2,1)S(1)} %copy-done.9, bf16[1,256,304]{1,2,0:T(8,128)(2,1)S(1)} %get-tuple-element.19), kind=kOutput, calls=%fused_computation.3 | convolution fusion | flops 638738432 | bytes 4898816 | tf_op jit(solution)/shard_map/dot_general | solution.py:151
  191.5 3.5 %reshape.230 = f32[2,1024,304]{1,0,2:T(2,128)S(1)} reshape(f32[2048,304]{0,1:T(8,128)} %convolution_bitcast_fusion) | data formatting | bytes 4980736 | tf_op jit(solution)/shard_map/reshape | solution.py:155
  195.0 1.1 constant_dynamic-slice_fusion
  196.1 1.0 copy.109
  197.1 1.9 collective-permute-start.4
  199.0 1.1 constant_dynamic-slice_fusion.1
  200.1 1.3 collective-permute-done.4
  201.4 1.4 fusion.18
  202.8 1.2 copy.96
  204.0 13.7 %all-to-all-start.5 = ((bf16[32,32,304]{2,1,0:T(8,128)(2,1)}), bf16[32,32,304]{2,1,0:T(8,128)(2,1)S(1)}, u32[]{:S(2)}, u32[]{:S(2)}) async-start(bf16[32,32,304]{2,1,0:T(8,128)(2,1)} %bitcast.44), calls=%async_computation.5 | async-start | bytes 1572864 | tf_op jit(solution)/shard_map/all_to_all | solution.py:158
  218.4 1.3 copy.92
  219.7 2.6 fusion.25
  222.3 40.8 %all-to-all-done.5 = bf16[32,32,304]{2,1,0:T(8,128)(2,1)S(1)} async-done(((bf16[32,32,304]{2,1,0:T(8,128)(2,1)}), bf16[32,32,304]{2,1,0:T(8,128)(2,1)S(1)}, u32[]{:S(2)}, u32[]{:S(2)}) %all-to-all-start.5) | async-done | bytes 622624 | tf_op jit(solution)/shard_map/all_to_all | solution.py:158
  263.2 0.8 convert_reduce_fusion
  (58 shorter events, 4.1 us)
Async XLA Ops:
  0.6 45.2 %copy-start.6 = (f32[1,256,304]{1,2,0:T(8,128)S(1)}, f32[1,256,304]{1,2,0:T(8,128)}, u32[]{:S(2)}) copy-start(f32[1,256,304]{1,2,0:T(8,128)} %param.9) | copy-start | bytes 933892
  40.9 25.7 %collective-permute-start = (bf16[608,768]{1,0:T(8,128)(2,1)S(1)}, bf16[608,768]{1,0:T(8,128)(2,1)}, u32[]{:S(2)}, u32[]{:S(2)}) collective-permute-start(bf16[608,768]{1,0:T(8,128)(2,1)S(1)} %reshape.234), channel_id=1, source_target_pairs={{0,128},{128,0},{1,129},{129,1},{2,130},{130,2},{3,131},{131,3},{4... | collective-permute-start | bytes 2801672 | tf_op jit(solution)/shard_map/ppermute | solution.py:44
  47.0 28.7 %all-to-all-start.1 = ((bf16[8,256,304]{1,2,0:T(8,128)(2,1)}), bf16[8,256,304]{1,2,0:T(8,128)(2,1)S(1)}, u32[]{:S(2)}, u32[]{:S(2)}) async-start(bf16[8,256,304]{1,2,0:T(8,128)(2,1)} %broadcast_in_dim.22), calls=%async_computation.1 | async-start | bytes 2490368 | tf_op jit(solution)/shard_map/all_to_all | solution.py:40
  66.6 5.0 %copy-start.8 = (f32[10,2,2432]{2,1,0:T(2,128)S(1)}, f32[10,2,2432]{2,1,0:T(2,128)}, u32[]{:S(2)}) copy-start(f32[10,2,2432]{2,1,0:T(2,128)} %param.11) | copy-start | bytes 583684
  69.0 7.4 %collective-permute-start.1 = (bf16[1216,768]{1,0:T(8,128)(2,1)S(1)}, bf16[1216,768]{1,0:T(8,128)(2,1)}, u32[]{:S(2)}, u32[]{:S(2)}) collective-permute-start(bf16[1216,768]{1,0:T(8,128)(2,1)S(1)} %bitcast.161), channel_id=1, source_target_pairs={{0,256},{256,0},{1,257},{257,1},{2,258},{258,2},{3,259},{259,3},{4... | collective-permute-start | bytes 5603336 | tf_op jit(solution)/shard_map/ppermute | solution.py:44
  76.5 4.0 %copy-start.10 = (bf16[32,304]{1,0:T(8,128)(2,1)S(1)}, bf16[32,304]{1,0:T(8,128)(2,1)}, u32[]{:S(2)}) copy-start(bf16[32,304]{1,0:T(8,128)(2,1)} %param.13) | copy-start | bytes 58372
  81.2 30.6 %all-to-all-start = ((bf16[16,32,304]{2,1,0:T(8,128)(2,1)}), bf16[16,32,304]{2,1,0:T(8,128)(2,1)S(1)}, u32[]{:S(2)}, u32[]{:S(2)}) async-start(bf16[16,32,304]{2,1,0:T(8,128)(2,1)} %broadcast_in_dim.20), calls=%async_computation | async-start | bytes 786432 | tf_op jit(solution)/shard_map/all_to_all | solution.py:40
  111.8 13.0 %collective-permute-start.2 = (bf16[512,304]{1,0:T(8,128)(2,1)S(1)}, bf16[512,304]{1,0:T(8,128)(2,1)S(1)}, u32[]{:S(2)}, u32[]{:S(2)}) collective-permute-start(bf16[512,304]{1,0:T(8,128)(2,1)S(1)} %bitcast.169), channel_id=1, source_target_pairs={{0,128},{128,0},{1,129},{129,1},{2,130},{130,2},{3,131},{131,3},{4... | collective-permute-start | bytes 933896 | tf_op jit(solution)/shard_map/ppermute | solution.py:44
  116.8 21.1 %all-to-all-start.2 = ((bf16[8,256,256]{2,1,0:T(8,128)(2,1)}), bf16[8,256,256]{2,1,0:T(8,128)(2,1)S(1)}, u32[]{:S(2)}, u32[]{:S(2)}) async-start(bf16[8,256,256]{2,1,0:T(8,128)(2,1)} %broadcast_in_dim.23), calls=%async_computation.2 | async-start | bytes 2097152 | tf_op jit(solution)/shard_map/all_to_all | solution.py:40
  126.0 12.4 %collective-permute-start.3 = (bf16[1024,304]{0,1:T(8,128)(2,1)}, bf16[1024,304]{0,1:T(8,128)(2,1)}, u32[]{:S(2)}, u32[]{:S(2)}) collective-permute-start(bf16[1024,304]{0,1:T(8,128)(2,1)} %bitcast.53), channel_id=1, source_target_pairs={{0,256},{256,0},{1,257},{257,1},{2,258},{258,2},{3,259},{259,3},{4... | collective-permute-start | bytes 1867784 | tf_op jit(solution)/shard_map/ppermute | solution.py:44
  139.9 1.0 copy-start.3
  139.9 1.1 copy-start.7
  140.1 2.2 copy-start.1
  142.3 4.9 %copy-start.11 = (s32[64]{0:T(128)S(1)}, s32[64]{0:T(128)}, u32[]{:S(2)}) copy-start(s32[64]{0:T(128)} %param.15) | copy-start | bytes 772
  142.3 4.9 %copy-start.12 = (f32[64]{0:T(128)S(1)}, f32[64]{0:T(128)}, u32[]{:S(2)}) copy-start(f32[64]{0:T(128)} %param.14) | copy-start | bytes 772
  143.4 19.7 %all-to-all-start.3 = ((bf16[8,256,304]{1,2,0:T(8,128)(2,1)}), bf16[8,256,304]{1,2,0:T(8,128)(2,1)S(1)}, u32[]{:S(2)}, u32[]{:S(2)}) async-start(bf16[8,256,304]{1,2,0:T(8,128)(2,1)} %broadcast_in_dim.24), calls=%async_computation.3 | async-start | bytes 2490368 | tf_op jit(solution)/shard_map/all_to_all | solution.py:40
  163.4 2.1 copy-start
  168.2 5.2 %copy-start.13 = (f32[2,64]{1,0:T(2,128)S(1)}, f32[2,64]{1,0:T(2,128)}, u32[]{:S(2)}) copy-start(f32[2,64]{1,0:T(2,128)} %param.17) | copy-start | bytes 1540
  168.2 7.9 %copy-start.4 = (bf16[2,1,256,304]{2,3,1,0:T(8,128)(2,1)S(1)}, bf16[2,1,256,304]{2,3,1,0:T(8,128)(2,1)}, u32[]{:S(2)}) copy-start(bf16[2,1,256,304]{2,3,1,0:T(8,128)(2,1)} %param.10) | copy-start | bytes 933892
  169.4 16.7 %all-to-all-start.4 = ((bf16[8,256,256]{2,1,0:T(8,128)(2,1)}), bf16[8,256,256]{2,1,0:T(8,128)(2,1)S(1)}, u32[]{:S(2)}, u32[]{:S(2)}) async-start(bf16[8,256,256]{2,1,0:T(8,128)(2,1)} %broadcast_in_dim.26), calls=%async_computation.4 | async-start | bytes 2097152 | tf_op jit(solution)/shard_map/all_to_all | solution.py:40
  186.1 1.9 copy-start.9
  197.1 4.3 %collective-permute-start.4 = (bf16[1024,304]{0,1:T(8,128)(2,1)}, bf16[1024,304]{0,1:T(8,128)(2,1)}, u32[]{:S(2)}, u32[]{:S(2)}) collective-permute-start(bf16[1024,304]{0,1:T(8,128)(2,1)} %bitcast.155), channel_id=1, source_target_pairs={{0,256},{256,0},{1,257},{257,1},{2,258},{258,2},{3,259},{259,3},{4... | collective-permute-start | bytes 1867784 | tf_op jit(solution)/shard_map/ppermute | solution.py:53
  204.0 15.7 %copy-start.2 = (bf16[2,38,8,1024]{3,2,0,1:T(8,128)(2,1)S(1)}, bf16[2,38,8,1024]{3,2,0,1:T(8,128)(2,1)}, u32[]{:S(2)}) copy-start(bf16[2,38,8,1024]{3,2,0,1:T(8,128)(2,1)} %copy-done.1) | copy-start | bytes 3735556
  204.0 15.7 %copy-start.5 = (bf16[2,1,256,304]{2,3,1,0:T(8,128)(2,1)S(1)}, bf16[2,1,256,304]{2,3,1,0:T(8,128)(2,1)}, u32[]{:S(2)}) copy-start(bf16[2,1,256,304]{2,3,1,0:T(8,128)(2,1)} %param.10) | copy-start | bytes 933892
  204.0 59.2 %all-to-all-start.5 = ((bf16[32,32,304]{2,1,0:T(8,128)(2,1)}), bf16[32,32,304]{2,1,0:T(8,128)(2,1)S(1)}, u32[]{:S(2)}, u32[]{:S(2)}) async-start(bf16[32,32,304]{2,1,0:T(8,128)(2,1)} %bitcast.44), calls=%async_computation.5 | async-start | bytes 1572864 | tf_op jit(solution)/shard_map/all_to_all | solution.py:158

commit v5 on v3

--- a/solution.py
+++ b/solution.py
@@ -68,15 +68,17 @@
     seq_size,
 ):
     units = qkv_weight.shape[0] * qkv_weight.shape[1]
-    qkv_t = jnp.transpose(qkv_weight, (2, 0, 1)).reshape(qkv_weight.shape[2], units)
-    qkv_t = lax.all_gather(qkv_t, "z", axis=0, tiled=True)
-    qkv_t = gather_pair(qkv_t, "xh").reshape(-1, units)
-    projection_t = gather_pair(qkv_t, "grp").reshape(-1, units)
+    width_rows = qkv_weight.shape[2]
+    out_shape = out_weight.shape
+    qkv_t = jnp.transpose(qkv_weight, (2, 0, 1)).reshape(width_rows, units)
+    qkv_z = lax.all_gather(qkv_t, "z", axis=0, tiled=True)
+    out_z = lax.all_gather(out_weight, "z", axis=0, tiled=True)
+    both = jnp.concatenate([qkv_z, out_z.reshape(qkv_z.shape[0], -1)], axis=1)
+    both = gather_pair(both, "xh").reshape(-1, both.shape[1])
+    both = gather_pair(both, "grp").reshape(-1, both.shape[1])
+    projection_t = both[:, :units]
+    out_rows = both[:, units:].reshape(-1, out_shape[1])
     first_blocks = gather_all_to_all(latents[0].astype(jnp.bfloat16), FEATURE_AXES, seq_size)
-    first_blocks, out_weight = lax.optimization_barrier((first_blocks, out_weight))
-    out_rows = gather_all_to_all(out_weight, "z", z_size).reshape(-1, out_weight.shape[1])
-    out_rows = gather_pair(out_rows, "xh").reshape(-1, out_weight.shape[1])
-    out_rows = gather_pair(out_rows, "grp").reshape(-1, out_weight.shape[1])
 
     group_width = qkv_weight.shape[1]
     heads_here = group_width // HD

time: 252 us -> 261 us (1.036)
  blocking collectives: 41.1 us -> 69.2 us
  starting transfers between devices: 58 us -> 43.4 us
  waiting for transfers between devices: 86.6 us -> 74.6 us
  other arithmetic: 14.4 us -> 21 us
  matrix products: 13.2 us -> 18.3 us
  local copies, waits for them, and re-layouts: 30.7 us -> 26.7 us
    all_gather x1 -> x2, blocking collectives: 41.1 us -> 69.2 us  [the longest x1 41.1 us: on_device(): qkv_z = lax.all_gather(qkv_t, 'z', axis=0, tiled=True)]
    all_to_all x5 -> x4, waiting for transfers between devices: 42.3 us -> 31.6 us  [gather_all_to_all(): return lax.all_to_all(spread, axis_name, 0, 0, tiled=True)]
    all_to_all x5 -> x4, starting transfers between devices: 28.5 us -> 22.2 us  [gather_all_to_all(): return lax.all_to_all(spread, axis_name, 0, 0, tiled=True)]
    ppermute x4 -> x2, starting transfers between devices: 13.1 us -> 6.84 us  [gather_pair(): other = lax.ppermute(x, axis_name, [(0, 1), (1, 0)])]
    select_n x3 -> x2, other arithmetic: 5.3 us -> 11.4 us  [gather_pair(): return jnp.where(first, jnp.stack([x, other]), jnp.stack([other, x]))]
    reshape x0 -> x2, local copies, waits for them, and re-layouts: none -> 4.48 us  [the longest x1 3.77 us: on_device(): out_rows = both[:, units:].reshape(-1, out_shape[1])]
    dot_general x2, matrix products: 2.44 us -> 6.54 us  [on_device(): jnp.dot(normed, projection_t, preferred_element_type=jnp.float32)]
    all_to_all x1, starting transfers between devices: 11.7 us -> 7.66 us  [on_device(): part = lax.all_to_all(part.astype(jnp.bfloat16), 'z', 0, 0, tiled=True)]
  transfers between devices with their start and end apart: 12 -> 9, of which waited for: 10 -> 9; matrix products, arithmetic and copies ran while one was open for 12% -> 8% of each run, Pallas kernels for 0% -> 0%
where the time goes in v5:
time: 261 us; the launch traced here: 259 us
  waiting for transfers between devices  74.6 us (29%)
  blocking collectives  69.2 us (27%)
  starting transfers between devices  43.4 us (17%)
  local copies, waits for them, and re-layouts  26.7 us (10%)
  other arithmetic  21 us (8%)
  matrix products  18.3 us (7%)
  between operations  5.31 us (2%)
    all_gather x1, blocking collectives, on_device(): qkv_z = lax.all_gather(qkv_t, 'z', axis=0, tiled=True)  41.1 us
    all_to_all x4, waiting for transfers between devices, gather_all_to_all(): return lax.all_to_all(spread, axis_name, 0, 0, tiled=True)  31.6 us
    all_gather x1, blocking collectives, on_device(): out_z = lax.all_gather(out_weight, 'z', axis=0, tiled=True)  28.1 us
    all_to_all x4, starting transfers between devices, gather_all_to_all(): return lax.all_to_all(spread, axis_name, 0, 0, tiled=True)  22.2 us
    all_to_all x1, waiting for transfers between devices, on_device(): part = lax.all_to_all(part.astype(jnp.bfloat16), 'z', 0, 0, tiled=True)  18.5 us
    ppermute x2, waiting for transfers between devices, gather_pair(): other = lax.ppermute(x, axis_name, [(0, 1), (1, 0)])  15.8 us
    select_n x2, other arithmetic, gather_pair(): return jnp.where(first, jnp.stack([x, other]), jnp.stack([other, x]))  11.4 us
    ppermute x2, waiting for transfers between devices, reduce_pair(): sent = lax.ppermute(send.astype(jnp.bfloat16), axis_name, [(0, 1), (1, 0)])  8.75 us
  transfers between devices with their start and end apart: 9, of which 9 were waited for; matrix products, arithmetic and copies ran while one was open for 8% of the time, Pallas kernels for 0%

profile of v5, /device:TPU:24, one launch (start us, length us, event | category | flops | bytes accessed | tf_op | source)
XLA Modules:
  0.0 258.5 jit_solution(10580378340180557573)
XLA Ops:
  0.6 0.9 copy.60
  1.6 41.1 %all-gather = bf16[16,38,768]{2,1,0:T(8,128)(2,1)S(1)} all-gather(bf16[1,38,768]{2,1,0:T(8,128)(2,1)S(1)} %reshape.196), channel_id=1, replica_groups=mesh['grp'=2,'xh'=2,'z'=16,'y'=4,'xl'=2] {'z'}, dimensions={0}, use_global_device_ids=true | all-gather | bytes 992256 | tf_op jit(solution)/shard_map/all_gather | solution.py:74
  43.1 28.1 %all_gather.7 = bf16[512,304]{1,0:T(8,128)(2,1)S(1)} all-gather(bf16[32,304]{1,0:T(8,128)(2,1)S(1)} %copy-done.7), channel_id=1, replica_groups=mesh['grp'=2,'xh'=2,'z'=16,'y'=4,'xl'=2] {'z'}, dimensions={0}, use_global_device_ids=true | all-gather | bytes 330752 | tf_op jit(solution)/shard_map/all_gather | solution.py:75
  71.2 0.7 reshape.186
  71.9 4.9 %collective-permute-start = (bf16[608,1024]{1,0:T(8,128)(2,1)S(1)}, bf16[608,1024]{1,0:T(8,128)(2,1)}, u32[]{:S(2)}, u32[]{:S(2)}) collective-permute-start(bf16[608,1024]{1,0:T(8,128)(2,1)S(1)} %constant_dynamic-update-slice_fusion), channel_id=1, source_target_pairs={{0,128},{128,0},{1,129},{129,1},{2,130},{130,2},{3,131},{131,3},{4... | collective-permute-start | bytes 3735560 | tf_op jit(solution)/shard_map/ppermute | solution.py:44
  76.9 1.1 broadcast_in_dim.21
  78.0 4.7 %all-to-all-start = ((bf16[8,256,304]{1,2,0:T(8,128)(2,1)}), bf16[8,256,304]{1,2,0:T(8,128)(2,1)S(1)}, u32[]{:S(2)}, u32[]{:S(2)}) async-start(bf16[8,256,304]{1,2,0:T(8,128)(2,1)} %broadcast_in_dim.21), calls=%async_computation | async-start | bytes 2490368 | tf_op jit(solution)/shard_map/all_to_all | solution.py:40
  82.7 14.9 %collective-permute-done = bf16[608,1024]{1,0:T(8,128)(2,1)} collective-permute-done((bf16[608,1024]{1,0:T(8,128)(2,1)S(1)}, bf16[608,1024]{1,0:T(8,128)(2,1)}, u32[]{:S(2)}, u32[]{:S(2)}) %collective-permute-start) | collective-permute-done | bytes 1245216 | tf_op jit(solution)/shard_map/ppermute | solution.py:44
  97.6 3.6 %maximum_select_fusion.1 = bf16[2,608,1024]{2,1,0:T(8,128)(2,1)} fusion(bf16[1,608,1024]{2,1,0:T(8,128)(2,1)} %bitcast.7, bf16[1,608,1024]{2,1,0:T(8,128)(2,1)S(1)} %bitcast.155, pred[]{:T(512)S(6)} %eq.52), kind=kLoop, calls=%fused_computation.8 | loop fusion | flops 3735552 | bytes 4980737 | tf_op jit(solution)/shard_map/jit(_where)/select_n | solution.py:46
  101.2 1.9 collective-permute-start.1
  104.1 1.0 all-to-all-done
  105.5 0.4 multiply_reduce_fusion.1
  105.9 1.4 fusion.13
  107.3 0.9 collective-permute-done.1
  108.2 7.8 %maximum_select_fusion = bf16[2,1216,1024]{2,1,0:T(8,128)(2,1)} fusion(bf16[1,1216,1024]{2,1,0:T(8,128)(2,1)} %bitcast.10, bf16[1,1216,1024]{2,1,0:T(8,128)(2,1)} %bitcast.8, pred[]{:T(512)S(6)} %eq.51), kind=kLoop, calls=%fused_computation.2 | loop fusion | flops 7471104 | bytes 9961473 | tf_op jit(solution)/shard_map/jit(_where)/select_n | solution.py:46
  115.9 3.3 %fusion.21 = bf16[256,768]{1,0:T(8,128)(2,1)S(1)} fusion(bf16[256,2432]{0,1:T(8,128)(2,1)S(1)} %fusion.13, bf16[2432,1024]{1,0:T(8,128)(2,1)} %bitcast.11), kind=kOutput, calls=%fused_computation.30 | convolution fusion | flops 956497920 | bytes 5373952 | tf_op jit(solution)/shard_map/dot_general | solution.py:114
  119.7 0.5 fusion.58
  120.3 0.4 convolution_convert_fusion.1
  120.8 1.1 broadcast_in_dim.23
  121.8 5.6 %all-to-all-start.1 = ((bf16[8,256,256]{2,1,0:T(8,128)(2,1)}), bf16[8,256,256]{2,1,0:T(8,128)(2,1)S(1)}, u32[]{:S(2)}, u32[]{:S(2)}) async-start(bf16[8,256,256]{2,1,0:T(8,128)(2,1)} %broadcast_in_dim.23), calls=%async_computation.1 | async-start | bytes 2097152 | tf_op jit(solution)/shard_map/all_to_all | solution.py:40
  127.6 1.4 slice.70
  129.0 3.8 %reshape.189 = bf16[2048,304]{1,0:T(8,128)(2,1)} reshape(bf16[2432,256]{1,0:T(8,128)(2,1)S(1)} %slice.70) | data formatting | bytes 2490368 | tf_op jit(solution)/shard_map/reshape | solution.py:80
  132.8 8.3 %all-to-all-done.1 = bf16[8,256,256]{2,1,0:T(8,128)(2,1)S(1)} async-done(((bf16[8,256,256]{2,1,0:T(8,128)(2,1)}), bf16[8,256,256]{2,1,0:T(8,128)(2,1)S(1)}, u32[]{:S(2)}, u32[]{:S(2)}) %all-to-all-start.1) | async-done | bytes 1048608 | tf_op jit(solution)/shard_map/all_to_all | solution.py:40
  141.1 0.5 copy.64
  141.6 2.8 %fusion.56 = (bf16[256,304]{0,1:T(8,128)(2,1)S(1)}, f32[256,304]{0,1:T(8,128)}) fusion(bf16[2,1,256,304]{2,3,1,0:T(8,128)(2,1)S(1)} %copy-done, f32[]{:T(128)S(6)} %sqrt.9, f32[]{:T(128)S(6)} %sub.101, f32[]{:T(128)S(6)} %div.81, f32[1,256,304]{1,2,0:T(8,128)S(1)} %copy-done.4, bf16[256,2048]{0,1:T(8,128)(2,1)S(1)} %bitcast.163, ...), kind=kOutput, calls=%fused_computation.111 | convolution fusion | flops 319545344 | bytes 3227660 | tf_op jit(solution)/shard_map/dot_general | solution.py:133
  144.4 1.1 broadcast_in_dim.24
  145.6 5.9 %all-to-all-start.2 = ((bf16[8,256,304]{1,2,0:T(8,128)(2,1)}), bf16[8,256,304]{1,2,0:T(8,128)(2,1)S(1)}, u32[]{:S(2)}, u32[]{:S(2)}) async-start(bf16[8,256,304]{1,2,0:T(8,128)(2,1)} %broadcast_in_dim.24), calls=%async_computation.2 | async-start | bytes 2490368 | tf_op jit(solution)/shard_map/all_to_all | solution.py:40
  151.7 14.6 %all-to-all-done.2 = bf16[8,256,304]{1,2,0:T(8,128)(2,1)S(1)} async-done(((bf16[8,256,304]{1,2,0:T(8,128)(2,1)}), bf16[8,256,304]{1,2,0:T(8,128)(2,1)S(1)}, u32[]{:S(2)}, u32[]{:S(2)}) %all-to-all-start.2) | async-done | bytes 1245216 | tf_op jit(solution)/shard_map/all_to_all | solution.py:40
  166.7 0.4 multiply_reduce_fusion
  167.1 1.4 fusion.9
  168.5 3.3 %fusion.24 = bf16[256,768]{1,0:T(8,128)(2,1)S(1)} fusion(bf16[256,2432]{0,1:T(8,128)(2,1)S(1)} %fusion.9, bf16[2432,1024]{1,0:T(8,128)(2,1)} %bitcast.11), kind=kOutput, calls=%fused_computation.31 | convolution fusion | flops 956497920 | bytes 5373952 | tf_op jit(solution)/shard_map/dot_general | solution.py:114
  171.9 0.3 convolution_multiply_fusion
  172.3 0.5 fusion.59
  172.8 0.4 convolution_convert_fusion
  173.3 1.1 broadcast_in_dim.26
  174.4 5.9 %all-to-all-start.3 = ((bf16[8,256,256]{2,1,0:T(8,128)(2,1)}), bf16[8,256,256]{2,1,0:T(8,128)(2,1)S(1)}, u32[]{:S(2)}, u32[]{:S(2)}) async-start(bf16[8,256,256]{2,1,0:T(8,128)(2,1)} %broadcast_in_dim.26), calls=%async_computation.3 | async-start | bytes 2097152 | tf_op jit(solution)/shard_map/all_to_all | solution.py:40
  180.7 0.7 fusion.50
  181.3 0.7 fusion.57
  183.4 0.7 fusion.44
  184.2 0.6 copy.69
  184.8 0.5 stack_reshape.8
  185.3 7.7 %all-to-all-done.3 = bf16[8,256,256]{2,1,0:T(8,128)(2,1)S(1)} async-done(((bf16[8,256,256]{2,1,0:T(8,128)(2,1)}), bf16[8,256,256]{2,1,0:T(8,128)(2,1)S(1)}, u32[]{:S(2)}, u32[]{:S(2)}) %all-to-all-start.3) | async-done | bytes 1048608 | tf_op jit(solution)/shard_map/all_to_all | solution.py:40
  193.0 0.6 copy.70
  193.6 1.3 stack_reshape.9
  194.9 3.5 %convolution_bitcast_fusion = f32[2048,304]{0,1:T(8,128)} fusion(bf16[1,256,2048]{2,1,0:T(8,128)(2,1)} %stack_reshape.9, bf16[1,256,2048]{2,1,0:T(8,128)(2,1)S(1)} %stack_reshape.8, bf16[1,256,304]{1,2,0:T(8,128)(2,1)S(1)} %copy-done.6, bf16[1,256,304]{1,2,0:T(8,128)(2,1)S(1)} %get-tuple-element.11), kind=kOutput, calls=%fused_computation.7 | convolution fusion | flops 638738432 | bytes 4898816 | tf_op jit(solution)/shard_map/dot_general | solution.py:150
  198.4 3.5 %reshape.192 = f32[2,1024,304]{1,0,2:T(2,128)S(1)} reshape(f32[2048,304]{0,1:T(8,128)} %convolution_bitcast_fusion) | data formatting | bytes 4980736 | tf_op jit(solution)/shard_map/reshape | solution.py:154
  201.9 1.1 constant_dynamic-slice_fusion.2
  203.0 1.0 copy.90
  204.0 2.1 collective-permute-start.2
  206.2 1.1 constant_dynamic-slice_fusion.3
  207.2 1.1 collective-permute-done.2
  208.3 1.4 bitcast_add_fusion
  209.7 1.1 reshape.193
  210.8 0.6 constant_dynamic-slice_fusion
  211.4 4.6 %collective-permute-start.3 = (bf16[512,304]{0,1:T(8,128)(2,1)S(1)}, bf16[512,304]{0,1:T(8,128)(2,1)}, u32[]{:S(2)}, u32[]{:S(2)}) collective-permute-start(bf16[512,304]{0,1:T(8,128)(2,1)S(1)} %bitcast.164), channel_id=1, source_target_pairs={{0,128},{128,0},{1,129},{129,1},{2,130},{130,2},{3,131},{131,3},{4... | collective-permute-start | bytes 933896 | tf_op jit(solution)/shard_map/ppermute | solution.py:53
  216.1 0.5 constant_dynamic-slice_fusion.1
  216.7 7.7 %collective-permute-done.3 = bf16[512,304]{0,1:T(8,128)(2,1)} collective-permute-done((bf16[512,304]{0,1:T(8,128)(2,1)S(1)}, bf16[512,304]{0,1:T(8,128)(2,1)}, u32[]{:S(2)}, u32[]{:S(2)}) %collective-permute-start.3) | collective-permute-done | bytes 311328 | tf_op jit(solution)/shard_map/ppermute | solution.py:53
  224.3 1.1 fusion.28
  225.4 0.9 copy.73
  226.3 7.7 %all-to-all-start.4 = ((bf16[16,32,304]{2,1,0:T(8,128)(2,1)}), bf16[16,32,304]{2,1,0:T(8,128)(2,1)S(1)}, u32[]{:S(2)}, u32[]{:S(2)}) async-start(bf16[16,32,304]{2,1,0:T(8,128)(2,1)} %bitcast.42), calls=%async_computation.4 | async-start | bytes 786432 | tf_op jit(solution)/shard_map/all_to_all | solution.py:159
  234.7 0.5 copy.68
  235.2 3.0 %fusion.34 = f32[1,256,304]{1,2,0:T(8,128)} fusion(f32[]{:T(128)S(6)} %sqrt.10, f32[]{:T(128)S(6)} %sub.110, f32[]{:T(128)S(6)} %div.88, bf16[2,1,256,304]{2,3,1,0:T(8,128)(2,1)S(1)} %copy-done.2, f32[]{:T(128)S(6)} %sqrt.9, f32[256,304]{0,1:T(8,128)} %get-tuple-element.16, f32[]{:T(128)S(6)} %sub.101, f32[]{:T(128)S(6)} %div.81, f32[1,256,304]{1,2,0:T(8,128)} %param.9, ...), kind=kOutput, calls=%fused_computation.54 | convolution fusion | flops 320167936 | bytes 3538968 | tf_op jit(solution)/shard_map/dot_general | solution.py:133
  238.2 18.5 %all-to-all-done.4 = bf16[16,32,304]{2,1,0:T(8,128)(2,1)S(1)} async-done(((bf16[16,32,304]{2,1,0:T(8,128)(2,1)}), bf16[16,32,304]{2,1,0:T(8,128)(2,1)S(1)}, u32[]{:S(2)}, u32[]{:S(2)}) %all-to-all-start.4) | async-done | bytes 311328 | tf_op jit(solution)/shard_map/all_to_all | solution.py:159
  256.7 0.7 convert_reduce_fusion.2
  (48 shorter events, 2.9 us)
Async XLA Ops:
  1.5 41.6 %copy-start.7 = (bf16[32,304]{1,0:T(8,128)(2,1)S(1)}, bf16[32,304]{1,0:T(8,128)(2,1)}, u32[]{:S(2)}) copy-start(bf16[32,304]{1,0:T(8,128)(2,1)} %param.13) | copy-start | bytes 58372
  42.9 33.9 %copy-start.3 = (f32[1,256,304]{1,2,0:T(8,128)S(1)}, f32[1,256,304]{1,2,0:T(8,128)}, u32[]{:S(2)}) copy-start(f32[1,256,304]{1,2,0:T(8,128)} %param.9) | copy-start | bytes 933892
  71.9 25.7 %collective-permute-start = (bf16[608,1024]{1,0:T(8,128)(2,1)S(1)}, bf16[608,1024]{1,0:T(8,128)(2,1)}, u32[]{:S(2)}, u32[]{:S(2)}) collective-permute-start(bf16[608,1024]{1,0:T(8,128)(2,1)S(1)} %constant_dynamic-update-slice_fusion), channel_id=1, source_target_pairs={{0,128},{128,0},{1,129},{129,1},{2,130},{130,2},{3,131},{131,3},{4... | collective-permute-start | bytes 3735560 | tf_op jit(solution)/shard_map/ppermute | solution.py:44
  78.0 27.1 %all-to-all-start = ((bf16[8,256,304]{1,2,0:T(8,128)(2,1)}), bf16[8,256,304]{1,2,0:T(8,128)(2,1)S(1)}, u32[]{:S(2)}, u32[]{:S(2)}) async-start(bf16[8,256,304]{1,2,0:T(8,128)(2,1)} %broadcast_in_dim.21), calls=%async_computation | async-start | bytes 2490368 | tf_op jit(solution)/shard_map/all_to_all | solution.py:40
  97.6 6.2 %copy-start.5 = (f32[10,2,2432]{2,1,0:T(2,128)S(1)}, f32[10,2,2432]{2,1,0:T(2,128)}, u32[]{:S(2)}) copy-start(f32[10,2,2432]{2,1,0:T(2,128)} %param.11) | copy-start | bytes 583684
  101.2 6.9 %collective-permute-start.1 = (bf16[1216,1024]{1,0:T(8,128)(2,1)}, bf16[1216,1024]{1,0:T(8,128)(2,1)}, u32[]{:S(2)}, u32[]{:S(2)}) collective-permute-start(bf16[1216,1024]{1,0:T(8,128)(2,1)} %bitcast.9), channel_id=1, source_target_pairs={{0,256},{256,0},{1,257},{257,1},{2,258},{258,2},{3,259},{259,3},{4... | collective-permute-start | bytes 7471112 | tf_op jit(solution)/shard_map/ppermute | solution.py:44
  121.8 19.2 %all-to-all-start.1 = ((bf16[8,256,256]{2,1,0:T(8,128)(2,1)}), bf16[8,256,256]{2,1,0:T(8,128)(2,1)S(1)}, u32[]{:S(2)}, u32[]{:S(2)}) async-start(bf16[8,256,256]{2,1,0:T(8,128)(2,1)} %broadcast_in_dim.23), calls=%async_computation.1 | async-start | bytes 2097152 | tf_op jit(solution)/shard_map/all_to_all | solution.py:40
  129.0 12.6 %copy-start = (bf16[2,1,256,304]{2,3,1,0:T(8,128)(2,1)S(1)}, bf16[2,1,256,304]{2,3,1,0:T(8,128)(2,1)}, u32[]{:S(2)}) copy-start(bf16[2,1,256,304]{2,3,1,0:T(8,128)(2,1)} %param.10) | copy-start | bytes 933892
  129.0 12.6 %copy-start.4 = (f32[1,256,304]{1,2,0:T(8,128)S(1)}, f32[1,256,304]{1,2,0:T(8,128)}, u32[]{:S(2)}) copy-start(f32[1,256,304]{1,2,0:T(8,128)} %param.9) | copy-start | bytes 933892
  144.4 7.1 %copy-start.8 = (s32[64]{0:T(128)S(1)}, s32[64]{0:T(128)}, u32[]{:S(2)}) copy-start(s32[64]{0:T(128)} %param.15) | copy-start | bytes 772
  144.4 7.1 %copy-start.9 = (f32[64]{0:T(128)S(1)}, f32[64]{0:T(128)}, u32[]{:S(2)}) copy-start(f32[64]{0:T(128)} %param.14) | copy-start | bytes 772
  145.6 20.8 %all-to-all-start.2 = ((bf16[8,256,304]{1,2,0:T(8,128)(2,1)}), bf16[8,256,304]{1,2,0:T(8,128)(2,1)S(1)}, u32[]{:S(2)}, u32[]{:S(2)}) async-start(bf16[8,256,304]{1,2,0:T(8,128)(2,1)} %broadcast_in_dim.24), calls=%async_computation.2 | async-start | bytes 2490368 | tf_op jit(solution)/shard_map/all_to_all | solution.py:40
  173.2 7.5 %copy-start.10 = (f32[2,64]{1,0:T(2,128)S(1)}, f32[2,64]{1,0:T(2,128)}, u32[]{:S(2)}) copy-start(f32[2,64]{1,0:T(2,128)} %param.17) | copy-start | bytes 1540
  173.2 10.2 %copy-start.1 = (bf16[2,1,256,304]{2,3,1,0:T(8,128)(2,1)S(1)}, bf16[2,1,256,304]{2,3,1,0:T(8,128)(2,1)}, u32[]{:S(2)}) copy-start(bf16[2,1,256,304]{2,3,1,0:T(8,128)(2,1)} %param.10) | copy-start | bytes 933892
  174.4 18.6 %all-to-all-start.3 = ((bf16[8,256,256]{2,1,0:T(8,128)(2,1)}), bf16[8,256,256]{2,1,0:T(8,128)(2,1)S(1)}, u32[]{:S(2)}, u32[]{:S(2)}) async-start(bf16[8,256,256]{2,1,0:T(8,128)(2,1)} %broadcast_in_dim.26), calls=%async_computation.3 | async-start | bytes 2097152 | tf_op jit(solution)/shard_map/all_to_all | solution.py:40
  185.3 9.6 %copy-start.6 = (bf16[1,256,304]{1,2,0:T(8,128)(2,1)S(1)}, bf16[1,256,304]{1,2,0:T(8,128)(2,1)}, u32[]{:S(2)}) copy-start(bf16[1,256,304]{1,2,0:T(8,128)(2,1)} %get-tuple-element.12) | copy-start | bytes 466948
  204.0 4.3 %collective-permute-start.2 = (bf16[1024,304]{0,1:T(8,128)(2,1)}, bf16[1024,304]{0,1:T(8,128)(2,1)}, u32[]{:S(2)}, u32[]{:S(2)}) collective-permute-start(bf16[1024,304]{0,1:T(8,128)(2,1)} %bitcast.148), channel_id=1, source_target_pairs={{0,256},{256,0},{1,257},{257,1},{2,258},{258,2},{3,259},{259,3},{4... | collective-permute-start | bytes 1867784 | tf_op jit(solution)/shard_map/ppermute | solution.py:53
  211.4 12.9 %collective-permute-start.3 = (bf16[512,304]{0,1:T(8,128)(2,1)S(1)}, bf16[512,304]{0,1:T(8,128)(2,1)}, u32[]{:S(2)}, u32[]{:S(2)}) collective-permute-start(bf16[512,304]{0,1:T(8,128)(2,1)S(1)} %bitcast.164), channel_id=1, source_target_pairs={{0,128},{128,0},{1,129},{129,1},{2,130},{130,2},{3,131},{131,3},{4... | collective-permute-start | bytes 933896 | tf_op jit(solution)/shard_map/ppermute | solution.py:53
  216.6 18.6 %copy-start.2 = (bf16[2,1,256,304]{2,3,1,0:T(8,128)(2,1)S(1)}, bf16[2,1,256,304]{2,3,1,0:T(8,128)(2,1)}, u32[]{:S(2)}) copy-start(bf16[2,1,256,304]{2,3,1,0:T(8,128)(2,1)} %param.10) | copy-start | bytes 933892
  226.3 30.4 %all-to-all-start.4 = ((bf16[16,32,304]{2,1,0:T(8,128)(2,1)}), bf16[16,32,304]{2,1,0:T(8,128)(2,1)S(1)}, u32[]{:S(2)}, u32[]{:S(2)}) async-start(bf16[16,32,304]{2,1,0:T(8,128)(2,1)} %bitcast.42), calls=%async_computation.4 | async-start | bytes 786432 | tf_op jit(solution)/shard_map/all_to_all | solution.py:159

commit v6 on v2

--- a/solution.py
+++ b/solution.py
@@ -68,14 +68,15 @@
     seq_size,
 ):
     units = qkv_weight.shape[0] * qkv_weight.shape[1]
+    out_shape = out_weight.shape
+    first_blocks = gather_all_to_all(latents[0].astype(jnp.bfloat16), FEATURE_AXES, seq_size)
     qkv_t = jnp.transpose(qkv_weight, (2, 0, 1)).reshape(qkv_weight.shape[2], units)
-    out_rows = gather_all_to_all(out_weight, "z", z_size).reshape(-1, out_weight.shape[1])
-    out_rows, latents, qkv_t = lax.optimization_barrier((out_rows, latents, qkv_t))
+    first_blocks, qkv_t = lax.optimization_barrier((first_blocks, qkv_t))
     qkv_t = lax.all_gather(qkv_t, "z", axis=0, tiled=True)
+    qkv_t, out_weight = lax.optimization_barrier((qkv_t, out_weight))
+    out_z = gather_all_to_all(out_weight, "z", z_size).reshape(-1, out_shape[1])
     qkv_t = gather_pair(qkv_t, "xh").reshape(-1, units)
     projection_t = gather_pair(qkv_t, "grp").reshape(-1, units)
-    out_rows = gather_pair(out_rows, "xh").reshape(-1, out_weight.shape[1])
-    out_rows = gather_pair(out_rows, "grp").reshape(-1, out_weight.shape[1])
 
     group_width = qkv_weight.shape[1]
     heads_here = group_width // HD
@@ -97,8 +98,11 @@
         time_now = 1.0 - index_now.astype(jnp.float32) / TSTEPS
         picker = (plan == index_now).astype(jnp.float32)
         modulate = jnp.sum(picker[:, None, None] * ada_table, 0)
-        blocks = gather_all_to_all(state, FEATURE_AXES, seq_size)
-        whole = jnp.transpose(blocks, (1, 0, 2)).reshape(seq_len, -1)
+        if section == 0:
+            blocks = first_blocks
+        else:
+            blocks = gather_all_to_all(state.astype(jnp.bfloat16), FEATURE_AXES, seq_size)
+        whole = jnp.transpose(blocks, (1, 0, 2)).reshape(seq_len, -1).astype(jnp.float32)
         centre = jnp.mean(whole, -1, keepdims=True)
         spread = jnp.mean((whole - centre) ** 2, -1, keepdims=True)
         normed = (
@@ -122,6 +126,10 @@
             "hqk,khe->qhe", probs, value_rows, preferred_element_type=jnp.float32
         ).astype(jnp.bfloat16)
         attn = attn_blocks.reshape(seq_len, group_width)
+        if section == 0:
+            out_z, attn = lax.optimization_barrier((out_z, attn))
+            out_rows = gather_pair(out_z, "xh").reshape(-1, out_shape[1])
+            out_rows = gather_pair(out_rows, "grp").reshape(-1, out_shape[1])
         attn_parts = gather_all_to_all(attn, FEATURE_AXES, seq_size)
         attn_all = jnp.transpose(attn_parts, (1, 0, 2)).reshape(seq_len, -1)
         velocity = jnp.dot(attn_all, out_rows, preferred_element_type=jnp.float32)

time: 270 us -> 257 us (0.952)
  waiting for transfers between devices: 110 us -> 100 us
  local copies, waits for them, and re-layouts: 25.6 us -> 18.4 us
  blocking collectives: 35.7 us -> 41.3 us
  other arithmetic: 18.7 us -> 15.4 us
    all_to_all x5, waiting for transfers between devices: 66.2 us -> 53.5 us  [gather_all_to_all(): return lax.all_to_all(spread, axis_name, 0, 0, tiled=True)]
    ppermute x4, waiting for transfers between devices: 12.1 us -> 18 us  [gather_pair(): other = lax.ppermute(x, axis_name, [(0, 1), (1, 0)])]
    all_gather x1, blocking collectives: 35.7 us -> 41.3 us  [on_device(): qkv_t = lax.all_gather(qkv_t, 'z', axis=0, tiled=True)]
    all_to_all x5, starting transfers between devices: 37 us -> 34 us  [gather_all_to_all(): return lax.all_to_all(spread, axis_name, 0, 0, tiled=True)]
    broadcast_in_dim x5, local copies, waits for them, and re-layouts: 8.06 us -> 5.16 us  [gather_all_to_all(): spread = jnp.broadcast_to(x[None], (size,) + x.shape)]
  transfers between devices with their start and end apart: 12 -> 12, of which waited for: 9 -> 11; matrix products, arithmetic and copies ran while one was open for 10% -> 7% of each run, Pallas kernels for 0% -> 0%
where the time goes in v6:
time: 257 us; the launch traced here: 255 us
  waiting for transfers between devices  100 us (39%)
  starting transfers between devices  63.2 us (25%)
  blocking collectives  41.3 us (16%)
  local copies, waits for them, and re-layouts  18.4 us (7%)
  other arithmetic  15.4 us (6%)
  matrix products  11 us (4%)
  between operations  5.44 us (2%)
    all_to_all x5, waiting for transfers between devices, gather_all_to_all(): return lax.all_to_all(spread, axis_name, 0, 0, tiled=True)  53.5 us
    all_gather x1, blocking collectives, on_device(): qkv_t = lax.all_gather(qkv_t, 'z', axis=0, tiled=True)  41.3 us
    all_to_all x5, starting transfers between devices, gather_all_to_all(): return lax.all_to_all(spread, axis_name, 0, 0, tiled=True)  34 us
    all_to_all x1, waiting for transfers between devices, on_device(): part = lax.all_to_all(part.astype(jnp.bfloat16), 'z', 0, 0, tiled=True)  19.4 us
    ppermute x4, waiting for transfers between devices, gather_pair(): other = lax.ppermute(x, axis_name, [(0, 1), (1, 0)])  18 us
    ppermute x4, starting transfers between devices, gather_pair(): other = lax.ppermute(x, axis_name, [(0, 1), (1, 0)])  13.1 us
    ppermute x2, waiting for transfers between devices, reduce_pair(): sent = lax.ppermute(send.astype(jnp.bfloat16), axis_name, [(0, 1), (1, 0)])  9.4 us
    all_to_all x1, starting transfers between devices, on_device(): part = lax.all_to_all(part.astype(jnp.bfloat16), 'z', 0, 0, tiled=True)  9.23 us
  transfers between devices with their start and end apart: 12, of which 11 were waited for; matrix products, arithmetic and copies ran while one was open for 7% of the time, Pallas kernels for 0%

profile of v6, /device:TPU:24, one launch (start us, length us, event | category | flops | bytes accessed | tf_op | source)
XLA Modules:
  0.0 255.0 jit_solution(1342413377654575647)
XLA Ops:
  0.6 1.0 convert_bitcast_fusion
  1.6 1.1 broadcast_in_dim.21
  2.7 9.1 %all-to-all-start = ((bf16[8,256,304]{1,2,0:T(8,128)(2,1)}), bf16[8,256,304]{1,2,0:T(8,128)(2,1)S(1)}, u32[]{:S(2)}, u32[]{:S(2)}) async-start(bf16[8,256,304]{1,2,0:T(8,128)(2,1)} %broadcast_in_dim.21), calls=%async_computation | async-start | bytes 2490368 | tf_op jit(solution)/shard_map/all_to_all | solution.py:40
  11.9 12.5 %all-to-all-done = bf16[8,256,304]{1,2,0:T(8,128)(2,1)S(1)} async-done(((bf16[8,256,304]{1,2,0:T(8,128)(2,1)}), bf16[8,256,304]{1,2,0:T(8,128)(2,1)S(1)}, u32[]{:S(2)}, u32[]{:S(2)}) %all-to-all-start) | async-done | bytes 1245216 | tf_op jit(solution)/shard_map/all_to_all | solution.py:40
  24.5 41.3 %all-gather = bf16[16,38,768]{2,1,0:T(8,128)(2,1)S(1)} all-gather(bf16[1,38,768]{2,1,0:T(8,128)(2,1)S(1)} %bitcast.183), channel_id=1, replica_groups=mesh['grp'=2,'xh'=2,'z'=16,'y'=4,'xl'=2] {'z'}, dimensions={0}, use_global_device_ids=true | all-gather | bytes 992256 | tf_op jit(solution)/shard_map/all_gather | solution.py:75
  65.8 1.2 reshape.288
  67.0 4.6 %collective-permute-start = (bf16[608,768]{1,0:T(8,128)(2,1)}, bf16[608,768]{1,0:T(8,128)(2,1)}, u32[]{:S(2)}, u32[]{:S(2)}) collective-permute-start(bf16[608,768]{1,0:T(8,128)(2,1)} %reshape.288), channel_id=1, source_target_pairs={{0,128},{128,0},{1,129},{129,1},{2,130},{130,2},{3,131},{131,3},{4... | collective-permute-start | bytes 2801672 | tf_op jit(solution)/shard_map/ppermute | solution.py:44
  71.6 13.6 %collective-permute-done = bf16[608,768]{1,0:T(8,128)(2,1)} collective-permute-done((bf16[608,768]{1,0:T(8,128)(2,1)}, bf16[608,768]{1,0:T(8,128)(2,1)}, u32[]{:S(2)}, u32[]{:S(2)}) %collective-permute-start) | collective-permute-done | bytes 933920 | tf_op jit(solution)/shard_map/ppermute | solution.py:44
  85.2 2.5 maximum_select_fusion.1
  87.7 1.9 collective-permute-start.1
  90.6 0.7 fusion.45
  91.4 0.8 broadcast_in_dim.22
  92.2 6.9 %all-to-all-start.1 = ((bf16[16,32,304]{2,1,0:T(8,128)(2,1)}), bf16[16,32,304]{2,1,0:T(8,128)(2,1)S(1)}, u32[]{:S(2)}, u32[]{:S(2)}) async-start(bf16[16,32,304]{2,1,0:T(8,128)(2,1)} %broadcast_in_dim.22), calls=%async_computation.1 | async-start | bytes 786432 | tf_op jit(solution)/shard_map/all_to_all | solution.py:40
  99.5 0.4 fusion.10
  99.9 0.8 fusion.13
  100.7 2.6 %maximum_select_fusion = bf16[2,1216,768]{2,1,0:T(8,128)(2,1)S(1)} fusion(bf16[1,1216,768]{2,1,0:T(8,128)(2,1)} %bitcast.12, bf16[1,1216,768]{2,1,0:T(8,128)(2,1)S(1)} %bitcast.157, pred[]{:T(512)S(6)} %eq.53), kind=kLoop, calls=%fused_computation.2 | loop fusion | flops 5603328 | bytes 7471105 | tf_op jit(solution)/shard_map/jit(_where)/select_n | solution.py:46
  103.4 1.8 copy-done
  105.2 1.2 convolution_convert_fusion.1
  106.6 0.5 fusion.56
  107.8 16.7 %all-to-all-done.1 = bf16[16,32,304]{2,1,0:T(8,128)(2,1)S(1)} async-done(((bf16[16,32,304]{2,1,0:T(8,128)(2,1)}), bf16[16,32,304]{2,1,0:T(8,128)(2,1)S(1)}, u32[]{:S(2)}, u32[]{:S(2)}) %all-to-all-start.1) | async-done | bytes 311328 | tf_op jit(solution)/shard_map/all_to_all | solution.py:40
  124.6 4.6 %collective-permute-start.2 = (bf16[512,304]{1,0:T(8,128)(2,1)S(1)}, bf16[512,304]{1,0:T(8,128)(2,1)S(1)}, u32[]{:S(2)}, u32[]{:S(2)}) collective-permute-start(bf16[512,304]{1,0:T(8,128)(2,1)S(1)} %bitcast.168), channel_id=1, source_target_pairs={{0,128},{128,0},{1,129},{129,1},{2,130},{130,2},{3,131},{131,3},{4... | collective-permute-start | bytes 933896 | tf_op jit(solution)/shard_map/ppermute | solution.py:44
  129.2 1.1 broadcast_in_dim.23
  130.3 5.9 %all-to-all-start.2 = ((bf16[8,256,256]{1,2,0:T(8,128)(2,1)}), bf16[8,256,256]{1,2,0:T(8,128)(2,1)S(1)}, u32[]{:S(2)}, u32[]{:S(2)}) async-start(bf16[8,256,256]{1,2,0:T(8,128)(2,1)} %broadcast_in_dim.23), calls=%async_computation.2 | async-start | bytes 2097152 | tf_op jit(solution)/shard_map/all_to_all | solution.py:40
  136.3 3.5 %collective-permute-done.2 = bf16[512,304]{1,0:T(8,128)(2,1)S(1)} collective-permute-done((bf16[512,304]{1,0:T(8,128)(2,1)S(1)}, bf16[512,304]{1,0:T(8,128)(2,1)S(1)}, u32[]{:S(2)}, u32[]{:S(2)}) %collective-permute-start.2) | collective-permute-done | bytes 311328 | tf_op jit(solution)/shard_map/ppermute | solution.py:44
  140.1 0.9 copy.88
  141.0 1.9 collective-permute-start.3
  143.2 0.6 copy.74
  143.8 0.4 select_n.116
  144.2 0.9 collective-permute-done.3
  145.5 1.5 all-to-all-done.2
  146.9 1.2 fusion.54
  148.2 1.1 broadcast_in_dim.24
  149.3 6.2 %all-to-all-start.3 = ((bf16[8,256,304]{1,2,0:T(8,128)(2,1)}), bf16[8,256,304]{1,2,0:T(8,128)(2,1)S(1)}, u32[]{:S(2)}, u32[]{:S(2)}) async-start(bf16[8,256,304]{1,2,0:T(8,128)(2,1)} %broadcast_in_dim.24), calls=%async_computation.3 | async-start | bytes 2490368 | tf_op jit(solution)/shard_map/all_to_all | solution.py:40
  155.9 14.5 %all-to-all-done.3 = bf16[8,256,304]{1,2,0:T(8,128)(2,1)S(1)} async-done(((bf16[8,256,304]{1,2,0:T(8,128)(2,1)}), bf16[8,256,304]{1,2,0:T(8,128)(2,1)S(1)}, u32[]{:S(2)}, u32[]{:S(2)}) %all-to-all-start.3) | async-done | bytes 1245216 | tf_op jit(solution)/shard_map/all_to_all | solution.py:40
  170.7 0.4 fusion.6
  171.1 0.8 fusion.9
  171.9 0.8 copy-done.1
  172.8 1.2 convolution_convert_fusion
  174.5 0.5 fusion.57
  175.0 0.4 convolution_convert_fusion.2
  175.5 1.1 broadcast_in_dim.26
  176.5 5.9 %all-to-all-start.4 = ((bf16[8,256,256]{1,2,0:T(8,128)(2,1)}), bf16[8,256,256]{1,2,0:T(8,128)(2,1)S(1)}, u32[]{:S(2)}, u32[]{:S(2)}) async-start(bf16[8,256,256]{1,2,0:T(8,128)(2,1)} %broadcast_in_dim.26), calls=%async_computation.4 | async-start | bytes 2097152 | tf_op jit(solution)/shard_map/all_to_all | solution.py:40
  182.8 0.7 fusion.48
  183.5 0.7 fusion.55
  185.6 0.7 fusion.42
  186.3 0.5 copy.79
  186.9 8.3 %all-to-all-done.4 = bf16[8,256,256]{1,2,0:T(8,128)(2,1)S(1)} async-done(((bf16[8,256,256]{1,2,0:T(8,128)(2,1)}), bf16[8,256,256]{1,2,0:T(8,128)(2,1)S(1)}, u32[]{:S(2)}, u32[]{:S(2)}) %all-to-all-start.4) | async-done | bytes 1048608 | tf_op jit(solution)/shard_map/all_to_all | solution.py:40
  195.1 0.5 copy.80
  195.7 2.3 fusion.18
  197.9 1.4 fusion.26
  199.3 1.9 collective-permute-start.4
  201.2 2.0 collective-permute-done.4
  203.2 1.4 bitcast_add_fusion
  204.7 1.1 reshape.286
  205.8 0.6 constant_dynamic-slice_fusion
  206.4 4.9 %collective-permute-start.5 = (bf16[512,304]{0,1:T(8,128)(2,1)S(1)}, bf16[512,304]{0,1:T(8,128)(2,1)}, u32[]{:S(2)}, u32[]{:S(2)}) collective-permute-start(bf16[512,304]{0,1:T(8,128)(2,1)S(1)} %bitcast.182), channel_id=1, source_target_pairs={{0,128},{128,0},{1,129},{129,1},{2,130},{130,2},{3,131},{131,3},{4... | collective-permute-start | bytes 933896 | tf_op jit(solution)/shard_map/ppermute | solution.py:53
  211.3 0.5 constant_dynamic-slice_fusion.1
  211.9 7.4 %collective-permute-done.5 = bf16[512,304]{0,1:T(8,128)(2,1)} collective-permute-done((bf16[512,304]{0,1:T(8,128)(2,1)S(1)}, bf16[512,304]{0,1:T(8,128)(2,1)}, u32[]{:S(2)}, u32[]{:S(2)}) %collective-permute-start.5) | collective-permute-done | bytes 311328 | tf_op jit(solution)/shard_map/ppermute | solution.py:53
  219.3 1.1 fusion.27
  220.4 0.9 copy.82
  221.3 9.2 %all-to-all-start.5 = ((bf16[16,32,304]{2,1,0:T(8,128)(2,1)}), bf16[16,32,304]{2,1,0:T(8,128)(2,1)S(1)}, u32[]{:S(2)}, u32[]{:S(2)}) async-start(bf16[16,32,304]{2,1,0:T(8,128)(2,1)} %bitcast.50), calls=%async_computation.5 | async-start | bytes 786432 | tf_op jit(solution)/shard_map/all_to_all | solution.py:161
  231.2 2.6 %fusion.33 = f32[1,256,304]{1,2,0:T(8,128)} fusion(f32[]{:T(128)S(6)} %sqrt.10, f32[]{:T(128)S(6)} %sub.100, f32[]{:T(128)S(6)} %div.88, bf16[2,1,256,304]{2,3,1,0:T(8,128)(2,1)S(1)} %copy-done.5, f32[]{:T(128)S(6)} %sqrt.9, f32[256,304]{0,1:T(8,128)S(1)} %copy-done.17, f32[]{:T(128)S(6)} %sub.93, f32[]{:T(128)S(6)} %div.81, ...), kind=kOutput, calls=%fused_computation.56 | convolution fusion | flops 320167936 | bytes 3538968 | tf_op jit(solution)/shard_map/dot_general | solution.py:135
  233.8 19.4 %all-to-all-done.5 = bf16[16,32,304]{2,1,0:T(8,128)(2,1)S(1)} async-done(((bf16[16,32,304]{2,1,0:T(8,128)(2,1)}), bf16[16,32,304]{2,1,0:T(8,128)(2,1)S(1)}, u32[]{:S(2)}, u32[]{:S(2)}) %all-to-all-start.5) | async-done | bytes 311328 | tf_op jit(solution)/shard_map/all_to_all | solution.py:161
  253.2 0.7 convert_reduce_fusion.2
  (68 shorter events, 4.1 us)
Async XLA Ops:
  1.6 10.2 %copy-start.10 = (bf16[3,256,38]{1,2,0:T(8,128)(2,1)S(1)}, bf16[3,256,38]{1,2,0:T(8,128)(2,1)}, u32[]{:S(2)}) copy-start(bf16[3,256,38]{1,2,0:T(8,128)(2,1)} %param.12) | copy-start | bytes 175108
  2.7 21.7 %all-to-all-start = ((bf16[8,256,304]{1,2,0:T(8,128)(2,1)}), bf16[8,256,304]{1,2,0:T(8,128)(2,1)S(1)}, u32[]{:S(2)}, u32[]{:S(2)}) async-start(bf16[8,256,304]{1,2,0:T(8,128)(2,1)} %broadcast_in_dim.21), calls=%async_computation | async-start | bytes 2490368 | tf_op jit(solution)/shard_map/all_to_all | solution.py:40
  67.0 18.3 %collective-permute-start = (bf16[608,768]{1,0:T(8,128)(2,1)}, bf16[608,768]{1,0:T(8,128)(2,1)}, u32[]{:S(2)}, u32[]{:S(2)}) collective-permute-start(bf16[608,768]{1,0:T(8,128)(2,1)} %reshape.288), channel_id=1, source_target_pairs={{0,128},{128,0},{1,129},{129,1},{2,130},{130,2},{3,131},{131,3},{4... | collective-permute-start | bytes 2801672 | tf_op jit(solution)/shard_map/ppermute | solution.py:44
  85.2 5.1 %copy-start.8 = (f32[10,2,2432]{2,1,0:T(2,128)S(1)}, f32[10,2,2432]{2,1,0:T(2,128)}, u32[]{:S(2)}) copy-start(f32[10,2,2432]{2,1,0:T(2,128)} %param.11) | copy-start | bytes 583684
  85.2 6.2 %copy-start.12 = (bf16[32,304]{1,0:T(8,128)(2,1)S(1)}, bf16[32,304]{1,0:T(8,128)(2,1)}, u32[]{:S(2)}) copy-start(bf16[32,304]{1,0:T(8,128)(2,1)} %param.13) | copy-start | bytes 58372
  87.7 13.0 %collective-permute-start.1 = (bf16[1216,768]{1,0:T(8,128)(2,1)S(1)}, bf16[1216,768]{1,0:T(8,128)(2,1)}, u32[]{:S(2)}, u32[]{:S(2)}) collective-permute-start(bf16[1216,768]{1,0:T(8,128)(2,1)S(1)} %bitcast.156), channel_id=1, source_target_pairs={{0,256},{256,0},{1,257},{257,1},{2,258},{258,2},{3,259},{259,3},{4... | collective-permute-start | bytes 5603336 | tf_op jit(solution)/shard_map/ppermute | solution.py:44
  92.2 32.4 %all-to-all-start.1 = ((bf16[16,32,304]{2,1,0:T(8,128)(2,1)}), bf16[16,32,304]{2,1,0:T(8,128)(2,1)S(1)}, u32[]{:S(2)}, u32[]{:S(2)}) async-start(bf16[16,32,304]{2,1,0:T(8,128)(2,1)} %broadcast_in_dim.22), calls=%async_computation.1 | async-start | bytes 786432 | tf_op jit(solution)/shard_map/all_to_all | solution.py:40
  103.4 1.8 copy-start
  124.6 15.2 %collective-permute-start.2 = (bf16[512,304]{1,0:T(8,128)(2,1)S(1)}, bf16[512,304]{1,0:T(8,128)(2,1)S(1)}, u32[]{:S(2)}, u32[]{:S(2)}) collective-permute-start(bf16[512,304]{1,0:T(8,128)(2,1)S(1)} %bitcast.168), channel_id=1, source_target_pairs={{0,128},{128,0},{1,129},{129,1},{2,130},{130,2},{3,131},{131,3},{4... | collective-permute-start | bytes 933896 | tf_op jit(solution)/shard_map/ppermute | solution.py:44
  130.3 16.7 %all-to-all-start.2 = ((bf16[8,256,256]{1,2,0:T(8,128)(2,1)}), bf16[8,256,256]{1,2,0:T(8,128)(2,1)S(1)}, u32[]{:S(2)}, u32[]{:S(2)}) async-start(bf16[8,256,256]{1,2,0:T(8,128)(2,1)} %broadcast_in_dim.23), calls=%async_computation.2 | async-start | bytes 2097152 | tf_op jit(solution)/shard_map/all_to_all | solution.py:40
  141.0 4.1 %collective-permute-start.3 = (bf16[1024,304]{0,1:T(8,128)(2,1)}, bf16[1024,304]{0,1:T(8,128)(2,1)S(1)}, u32[]{:S(2)}, u32[]{:S(2)}) collective-permute-start(bf16[1024,304]{0,1:T(8,128)(2,1)} %bitcast.61), channel_id=1, source_target_pairs={{0,256},{256,0},{1,257},{257,1},{2,258},{258,2},{3,259},{259,3},{4... | collective-permute-start | bytes 1867784 | tf_op jit(solution)/shard_map/ppermute | solution.py:44
  145.3 1.6 copy-start.3
  145.4 1.6 copy-start.6
  145.5 3.8 %copy-start.2 = (bf16[2,38,8,1024]{3,2,0,1:T(8,128)(2,1)}, bf16[2,38,8,1024]{3,2,0,1:T(8,128)(2,1)S(1)}, u32[]{:S(2)}) copy-start(bf16[2,38,8,1024]{3,2,0,1:T(8,128)(2,1)S(1)} %copy.89) | copy-start | bytes 3735556
  148.2 7.3 %copy-start.11 = (f32[2432]{0:T(1024)S(1)}, f32[2432]{0:T(1024)}, u32[]{:S(2)}) copy-start(f32[2432]{0:T(1024)} %get-tuple-element.18) | copy-start | bytes 29188
  148.2 7.5 %copy-start.13 = (s32[64]{0:T(128)S(1)}, s32[64]{0:T(128)}, u32[]{:S(2)}) copy-start(s32[64]{0:T(128)} %param.15) | copy-start | bytes 772
  148.2 7.5 %copy-start.14 = (f32[64]{0:T(128)S(1)}, f32[64]{0:T(128)}, u32[]{:S(2)}) copy-start(f32[64]{0:T(128)} %param.14) | copy-start | bytes 772
  149.3 21.0 %all-to-all-start.3 = ((bf16[8,256,304]{1,2,0:T(8,128)(2,1)}), bf16[8,256,304]{1,2,0:T(8,128)(2,1)S(1)}, u32[]{:S(2)}, u32[]{:S(2)}) async-start(bf16[8,256,304]{1,2,0:T(8,128)(2,1)} %broadcast_in_dim.24), calls=%async_computation.3 | async-start | bytes 2490368 | tf_op jit(solution)/shard_map/all_to_all | solution.py:40
  170.7 2.1 copy-start.1
  175.4 7.2 %copy-start.15 = (f32[64]{0:T(128)S(1)}, f32[64]{0:T(128)}, u32[]{:S(2)}) copy-start(f32[64]{0:T(128)} %param.14) | copy-start | bytes 772
  175.4 7.4 %copy-start.16 = (f32[2,64]{1,0:T(2,128)S(1)}, f32[2,64]{1,0:T(2,128)}, u32[]{:S(2)}) copy-start(f32[2,64]{1,0:T(2,128)} %param.17) | copy-start | bytes 1540
  175.4 10.1 %copy-start.4 = (bf16[2,1,256,304]{2,3,1,0:T(8,128)(2,1)S(1)}, bf16[2,1,256,304]{2,3,1,0:T(8,128)(2,1)}, u32[]{:S(2)}) copy-start(bf16[2,1,256,304]{2,3,1,0:T(8,128)(2,1)} %param.10) | copy-start | bytes 933892
  176.5 18.6 %all-to-all-start.4 = ((bf16[8,256,256]{1,2,0:T(8,128)(2,1)}), bf16[8,256,256]{1,2,0:T(8,128)(2,1)S(1)}, u32[]{:S(2)}, u32[]{:S(2)}) async-start(bf16[8,256,256]{1,2,0:T(8,128)(2,1)} %broadcast_in_dim.26), calls=%async_computation.4 | async-start | bytes 2097152 | tf_op jit(solution)/shard_map/all_to_all | solution.py:40
  186.8 8.8 %copy-start.9 = (bf16[1,256,304]{1,2,0:T(8,128)(2,1)S(1)}, bf16[1,256,304]{1,2,0:T(8,128)(2,1)}, u32[]{:S(2)}) copy-start(bf16[1,256,304]{1,2,0:T(8,128)(2,1)} %get-tuple-element.24) | copy-start | bytes 466948
  199.3 3.9 %collective-permute-start.4 = (bf16[1024,304]{0,1:T(8,128)(2,1)S(1)}, bf16[1024,304]{0,1:T(8,128)(2,1)S(1)}, u32[]{:S(2)}, u32[]{:S(2)}) collective-permute-start(bf16[1024,304]{0,1:T(8,128)(2,1)S(1)} %fusion.26), channel_id=1, source_target_pairs={{0,256},{256,0},{1,257},{257,1},{2,258},{258,2},{3,259},{259,3},{4... | collective-permute-start | bytes 1867784 | tf_op jit(solution)/shard_map/ppermute | solution.py:53
  206.4 12.9 %collective-permute-start.5 = (bf16[512,304]{0,1:T(8,128)(2,1)S(1)}, bf16[512,304]{0,1:T(8,128)(2,1)}, u32[]{:S(2)}, u32[]{:S(2)}) collective-permute-start(bf16[512,304]{0,1:T(8,128)(2,1)S(1)} %bitcast.182), channel_id=1, source_target_pairs={{0,128},{128,0},{1,129},{129,1},{2,130},{130,2},{3,131},{131,3},{4... | collective-permute-start | bytes 933896 | tf_op jit(solution)/shard_map/ppermute | solution.py:53
  211.3 19.9 %copy-start.5 = (bf16[2,1,256,304]{2,3,1,0:T(8,128)(2,1)S(1)}, bf16[2,1,256,304]{2,3,1,0:T(8,128)(2,1)}, u32[]{:S(2)}) copy-start(bf16[2,1,256,304]{2,3,1,0:T(8,128)(2,1)} %param.10) | copy-start | bytes 933892
  211.9 19.3 %copy-start.7 = (f32[1,256,304]{1,2,0:T(8,128)S(1)}, f32[1,256,304]{1,2,0:T(8,128)}, u32[]{:S(2)}) copy-start(f32[1,256,304]{1,2,0:T(8,128)} %param.9) | copy-start | bytes 933892
  211.9 19.3 %copy-start.17 = (f32[256,304]{0,1:T(8,128)S(1)}, f32[256,304]{0,1:T(8,128)}, u32[]{:S(2)}) copy-start(f32[256,304]{0,1:T(8,128)} %get-tuple-element.28) | copy-start | bytes 933892
  221.3 31.9 %all-to-all-start.5 = ((bf16[16,32,304]{2,1,0:T(8,128)(2,1)}), bf16[16,32,304]{2,1,0:T(8,128)(2,1)S(1)}, u32[]{:S(2)}, u32[]{:S(2)}) async-start(bf16[16,32,304]{2,1,0:T(8,128)(2,1)} %bitcast.50), calls=%async_computation.5 | async-start | bytes 786432 | tf_op jit(solution)/shard_map/all_to_all | solution.py:161

commit v7 on v3

--- a/solution.py
+++ b/solution.py
@@ -145,11 +145,11 @@
         attn_list.append(attn_all)
     attn_both = jnp.stack(attn_list, 0)
     score_both = jnp.stack(score_list, 0)
-    gradient = lax.dot_general(
-        attn_both, score_both, (((0, 1), (0, 1)), ((), ())), preferred_element_type=jnp.float32
+    rows = attn_both.shape[2]
+    attn_halves = attn_both.reshape(attn_both.shape[0], attn_both.shape[1], 2, rows // 2)
+    part = lax.dot_general(
+        attn_halves, score_both, (((0, 1), (0, 1)), ((), ())), preferred_element_type=jnp.float32
     )
-    rows = gradient.shape[0]
-    part = gradient.reshape(2, rows // 2, -1)
     part = reduce_pair(part, "grp")
     part = part.reshape(2, rows // 4, -1)
     part = reduce_pair(part, "xh")

time: 252 us -> 244 us (0.968)
  local copies, waits for them, and re-layouts: 30.7 us -> 21.4 us
  waiting for transfers between devices: 86.6 us -> 91.2 us
    reshape x1 -> x0, local copies, waits for them, and re-layouts: 3.49 us -> none  [on_device(): part = gradient.reshape(2, rows // 2, -1)]
    broadcast_in_dim x7 -> x5, local copies, waits for them, and re-layouts: 5.38 us -> 5.19 us  [gather_all_to_all(): spread = jnp.broadcast_to(x[None], (size,) + x.shape)]
  transfers between devices with their start and end apart: 12 -> 12, of which waited for: 10 -> 10; matrix products, arithmetic and copies ran while one was open for 12% -> 11% of each run, Pallas kernels for 0% -> 0%
where the time goes in v7:
time: 244 us; the launch traced here: 242 us
  waiting for transfers between devices  91.2 us (37%)
  starting transfers between devices  56.3 us (23%)
  blocking collectives  41.1 us (17%)
  local copies, waits for them, and re-layouts  21.4 us (9%)
  other arithmetic  15.4 us (6%)
  matrix products  11 us (5%)
  between operations  5.41 us (2%)
    all_to_all x5, waiting for transfers between devices, gather_all_to_all(): return lax.all_to_all(spread, axis_name, 0, 0, tiled=True)  44.5 us
    all_gather x1, blocking collectives, on_device(): qkv_t = lax.all_gather(qkv_t, 'z', axis=0, tiled=True)  41.1 us
    all_to_all x5, starting transfers between devices, gather_all_to_all(): return lax.all_to_all(spread, axis_name, 0, 0, tiled=True)  29.2 us
    all_to_all x1, waiting for transfers between devices, on_device(): part = lax.all_to_all(part.astype(jnp.bfloat16), 'z', 0, 0, tiled=True)  19.4 us
    ppermute x4, waiting for transfers between devices, gather_pair(): other = lax.ppermute(x, axis_name, [(0, 1), (1, 0)])  15.5 us
    ppermute x4, starting transfers between devices, gather_pair(): other = lax.ppermute(x, axis_name, [(0, 1), (1, 0)])  13.1 us
    ppermute x2, waiting for transfers between devices, reduce_pair(): sent = lax.ppermute(send.astype(jnp.bfloat16), axis_name, [(0, 1), (1, 0)])  11.8 us
    all_to_all x1, starting transfers between devices, on_device(): part = lax.all_to_all(part.astype(jnp.bfloat16), 'z', 0, 0, tiled=True)  9.5 us
  transfers between devices with their start and end apart: 12, of which 10 were waited for; matrix products, arithmetic and copies ran while one was open for 11% of the time, Pallas kernels for 0%

profile of v7, /device:TPU:24, one launch (start us, length us, event | category | flops | bytes accessed | tf_op | source)
XLA Modules:
  0.0 241.7 jit_solution(8515797335381738599)
XLA Ops:
  0.6 0.9 copy.59
  1.6 41.1 %all-gather = bf16[16,38,768]{2,1,0:T(8,128)(2,1)S(1)} all-gather(bf16[1,38,768]{2,1,0:T(8,128)(2,1)S(1)} %reshape.283), channel_id=1, replica_groups=mesh['grp'=2,'xh'=2,'z'=16,'y'=4,'xl'=2] {'z'}, dimensions={0}, use_global_device_ids=true | all-gather | bytes 992256 | tf_op jit(solution)/shard_map/all_gather | solution.py:72
  43.0 4.9 %collective-permute-start = (bf16[608,768]{1,0:T(8,128)(2,1)S(1)}, bf16[608,768]{1,0:T(8,128)(2,1)}, u32[]{:S(2)}, u32[]{:S(2)}) collective-permute-start(bf16[608,768]{1,0:T(8,128)(2,1)S(1)} %reshape.284), channel_id=1, source_target_pairs={{0,128},{128,0},{1,129},{129,1},{2,130},{130,2},{3,131},{131,3},{4... | collective-permute-start | bytes 2801672 | tf_op jit(solution)/shard_map/ppermute | solution.py:44
  48.0 1.1 broadcast_in_dim.23
  49.1 4.7 %all-to-all-start = ((bf16[8,256,304]{1,2,0:T(8,128)(2,1)}), bf16[8,256,304]{1,2,0:T(8,128)(2,1)S(1)}, u32[]{:S(2)}, u32[]{:S(2)}) async-start(bf16[8,256,304]{1,2,0:T(8,128)(2,1)} %broadcast_in_dim.23), calls=%async_computation | async-start | bytes 2490368 | tf_op jit(solution)/shard_map/all_to_all | solution.py:40
  53.8 1.2 stack.56
  55.0 13.7 %collective-permute-done = bf16[608,768]{1,0:T(8,128)(2,1)} collective-permute-done((bf16[608,768]{1,0:T(8,128)(2,1)S(1)}, bf16[608,768]{1,0:T(8,128)(2,1)}, u32[]{:S(2)}, u32[]{:S(2)}) %collective-permute-start) | collective-permute-done | bytes 933920 | tf_op jit(solution)/shard_map/ppermute | solution.py:44
  68.7 2.5 %maximum_select_fusion.1 = bf16[2,608,768]{2,1,0:T(8,128)(2,1)S(1)} fusion(bf16[1,608,768]{2,1,0:T(8,128)(2,1)} %bitcast.6, bf16[1,608,768]{2,1,0:T(8,128)(2,1)} %stack.56, pred[]{:T(512)S(6)} %eq.54), kind=kLoop, calls=%fused_computation.23 | loop fusion | flops 2801664 | bytes 3735553 | tf_op jit(solution)/shard_map/jit(_where)/select_n | solution.py:46
  71.1 1.9 collective-permute-start.1
  74.0 2.2 all-to-all-done
  76.2 0.8 broadcast_in_dim.26
  76.9 6.8 %all-to-all-start.2 = ((bf16[16,32,304]{2,1,0:T(8,128)(2,1)}), bf16[16,32,304]{2,1,0:T(8,128)(2,1)S(1)}, u32[]{:S(2)}, u32[]{:S(2)}) async-start(bf16[16,32,304]{2,1,0:T(8,128)(2,1)} %broadcast_in_dim.26), calls=%async_computation.2 | async-start | bytes 786432 | tf_op jit(solution)/shard_map/all_to_all | solution.py:40
  83.7 0.7 fusion.45
  84.4 0.8 add.101
  85.2 0.8 mul.233
  86.4 0.4 fusion.10
  86.8 1.7 fusion.13
  88.4 17.6 %all-to-all-done.2 = bf16[16,32,304]{2,1,0:T(8,128)(2,1)S(1)} async-done(((bf16[16,32,304]{2,1,0:T(8,128)(2,1)}), bf16[16,32,304]{2,1,0:T(8,128)(2,1)S(1)}, u32[]{:S(2)}, u32[]{:S(2)}) %all-to-all-start.2) | async-done | bytes 311328 | tf_op jit(solution)/shard_map/all_to_all | solution.py:40
  106.0 4.4 %collective-permute-start.2 = (bf16[512,304]{1,0:T(8,128)(2,1)S(1)}, bf16[512,304]{1,0:T(8,128)(2,1)}, u32[]{:S(2)}, u32[]{:S(2)}) collective-permute-start(bf16[512,304]{1,0:T(8,128)(2,1)S(1)} %bitcast.158), channel_id=1, source_target_pairs={{0,128},{128,0},{1,129},{129,1},{2,130},{130,2},{3,131},{131,3},{4... | collective-permute-start | bytes 933896 | tf_op jit(solution)/shard_map/ppermute | solution.py:44
  110.4 2.6 %maximum_select_fusion = bf16[2,1216,768]{2,1,0:T(8,128)(2,1)S(1)} fusion(bf16[1,1216,768]{2,1,0:T(8,128)(2,1)} %bitcast.9, bf16[1,1216,768]{2,1,0:T(8,128)(2,1)S(1)} %bitcast.149, pred[]{:T(512)S(6)} %eq.53), kind=kLoop, calls=%fused_computation.2 | loop fusion | flops 5603328 | bytes 7471105 | tf_op jit(solution)/shard_map/jit(_where)/select_n | solution.py:46
  113.0 1.8 copy-done
  114.8 1.2 convolution_convert_fusion.1
  116.6 0.5 fusion.56
  117.1 0.4 convolution_convert_fusion.3
  117.5 1.1 broadcast_in_dim.25
  118.6 6.2 %all-to-all-start.1 = ((bf16[8,256,256]{1,2,0:T(8,128)(2,1)}), bf16[8,256,256]{1,2,0:T(8,128)(2,1)S(1)}, u32[]{:S(2)}, u32[]{:S(2)}) async-start(bf16[8,256,256]{1,2,0:T(8,128)(2,1)} %broadcast_in_dim.25), calls=%async_computation.1 | async-start | bytes 2097152 | tf_op jit(solution)/shard_map/all_to_all | solution.py:40
  124.8 1.1 copy.62
  126.4 1.1 copy.65
  127.5 1.9 collective-permute-start.3
  129.8 1.8 collective-permute-done.3
  132.0 2.4 all-to-all-done.1
  134.4 1.2 fusion.54
  135.6 1.1 broadcast_in_dim.27
  136.7 5.5 %all-to-all-start.3 = ((bf16[8,256,304]{1,2,0:T(8,128)(2,1)}), bf16[8,256,304]{1,2,0:T(8,128)(2,1)S(1)}, u32[]{:S(2)}, u32[]{:S(2)}) async-start(bf16[8,256,304]{1,2,0:T(8,128)(2,1)} %broadcast_in_dim.27), calls=%async_computation.3 | async-start | bytes 2490368 | tf_op jit(solution)/shard_map/all_to_all | solution.py:40
  142.6 14.3 %all-to-all-done.3 = bf16[8,256,304]{1,2,0:T(8,128)(2,1)S(1)} async-done(((bf16[8,256,304]{1,2,0:T(8,128)(2,1)}), bf16[8,256,304]{1,2,0:T(8,128)(2,1)S(1)}, u32[]{:S(2)}, u32[]{:S(2)}) %all-to-all-start.3) | async-done | bytes 1245216 | tf_op jit(solution)/shard_map/all_to_all | solution.py:40
  157.2 0.4 fusion.6
  157.6 0.8 fusion.9
  158.5 0.8 copy-done.1
  159.3 1.2 convolution_convert_fusion
  161.0 0.5 fusion.57
  162.0 1.1 broadcast_in_dim.29
  163.0 6.0 %all-to-all-start.4 = ((bf16[8,256,256]{1,2,0:T(8,128)(2,1)}), bf16[8,256,256]{1,2,0:T(8,128)(2,1)S(1)}, u32[]{:S(2)}, u32[]{:S(2)}) async-start(bf16[8,256,256]{1,2,0:T(8,128)(2,1)} %broadcast_in_dim.29), calls=%async_computation.4 | async-start | bytes 2097152 | tf_op jit(solution)/shard_map/all_to_all | solution.py:40
  169.4 0.7 fusion.48
  170.1 0.7 fusion.55
  172.2 0.7 fusion.42
  172.9 0.5 copy.71
  173.5 8.1 %all-to-all-done.4 = bf16[8,256,256]{1,2,0:T(8,128)(2,1)S(1)} async-done(((bf16[8,256,256]{1,2,0:T(8,128)(2,1)}), bf16[8,256,256]{1,2,0:T(8,128)(2,1)S(1)}, u32[]{:S(2)}, u32[]{:S(2)}) %all-to-all-start.4) | async-done | bytes 1048608 | tf_op jit(solution)/shard_map/all_to_all | solution.py:40
  181.6 0.5 copy.72
  182.1 2.3 fusion.18
  184.4 1.4 fusion.26
  185.8 1.9 collective-permute-start.4
  187.7 2.0 collective-permute-done.4
  189.7 1.4 bitcast_add_fusion
  191.1 1.1 reshape.282
  192.2 0.6 constant_dynamic-slice_fusion
  192.8 2.5 %collective-permute-start.5 = (bf16[512,304]{0,1:T(8,128)(2,1)S(1)}, bf16[512,304]{0,1:T(8,128)(2,1)}, u32[]{:S(2)}, u32[]{:S(2)}) collective-permute-start(bf16[512,304]{0,1:T(8,128)(2,1)S(1)} %bitcast.172), channel_id=1, source_target_pairs={{0,128},{128,0},{1,129},{129,1},{2,130},{130,2},{3,131},{131,3},{4... | collective-permute-start | bytes 933896 | tf_op jit(solution)/shard_map/ppermute | solution.py:53
  195.4 0.5 constant_dynamic-slice_fusion.1
  196.0 9.8 %collective-permute-done.5 = bf16[512,304]{0,1:T(8,128)(2,1)} collective-permute-done((bf16[512,304]{0,1:T(8,128)(2,1)S(1)}, bf16[512,304]{0,1:T(8,128)(2,1)}, u32[]{:S(2)}, u32[]{:S(2)}) %collective-permute-start.5) | collective-permute-done | bytes 311328 | tf_op jit(solution)/shard_map/ppermute | solution.py:53
  205.7 1.1 fusion.27
  206.8 0.9 copy.74
  207.7 9.5 %all-to-all-start.5 = ((bf16[16,32,304]{2,1,0:T(8,128)(2,1)}), bf16[16,32,304]{2,1,0:T(8,128)(2,1)S(1)}, u32[]{:S(2)}, u32[]{:S(2)}) async-start(bf16[16,32,304]{2,1,0:T(8,128)(2,1)} %bitcast.50), calls=%async_computation.5 | async-start | bytes 786432 | tf_op jit(solution)/shard_map/all_to_all | solution.py:157
  218.0 2.6 %fusion.33 = f32[1,256,304]{1,2,0:T(8,128)} fusion(f32[]{:T(128)S(6)} %sqrt.10, f32[]{:T(128)S(6)} %sub.100, f32[]{:T(128)S(6)} %div.88, bf16[2,1,256,304]{2,3,1,0:T(8,128)(2,1)S(1)} %copy-done.6, f32[]{:T(128)S(6)} %sqrt.9, f32[256,304]{0,1:T(8,128)S(1)} %copy-done.18, f32[]{:T(128)S(6)} %sub.93, f32[]{:T(128)S(6)} %div.81, ...), kind=kOutput, calls=%fused_computation.56 | convolution fusion | flops 320167936 | bytes 3538968 | tf_op jit(solution)/shard_map/dot_general | solution.py:131
  220.5 19.4 %all-to-all-done.5 = bf16[16,32,304]{2,1,0:T(8,128)(2,1)S(1)} async-done(((bf16[16,32,304]{2,1,0:T(8,128)(2,1)}), bf16[16,32,304]{2,1,0:T(8,128)(2,1)S(1)}, u32[]{:S(2)}, u32[]{:S(2)}) %all-to-all-start.5) | async-done | bytes 311328 | tf_op jit(solution)/shard_map/all_to_all | solution.py:157
  239.9 0.7 convert_reduce_fusion.2
  (68 shorter events, 4.4 us)
Async XLA Ops:
  0.6 47.3 %copy-start.7 = (f32[1,256,304]{1,2,0:T(8,128)S(1)}, f32[1,256,304]{1,2,0:T(8,128)}, u32[]{:S(2)}) copy-start(f32[1,256,304]{1,2,0:T(8,128)} %param.9) | copy-start | bytes 933892
  43.0 25.7 %collective-permute-start = (bf16[608,768]{1,0:T(8,128)(2,1)S(1)}, bf16[608,768]{1,0:T(8,128)(2,1)}, u32[]{:S(2)}, u32[]{:S(2)}) collective-permute-start(bf16[608,768]{1,0:T(8,128)(2,1)S(1)} %reshape.284), channel_id=1, source_target_pairs={{0,128},{128,0},{1,129},{129,1},{2,130},{130,2},{3,131},{131,3},{4... | collective-permute-start | bytes 2801672 | tf_op jit(solution)/shard_map/ppermute | solution.py:44
  49.1 27.1 %all-to-all-start = ((bf16[8,256,304]{1,2,0:T(8,128)(2,1)}), bf16[8,256,304]{1,2,0:T(8,128)(2,1)S(1)}, u32[]{:S(2)}, u32[]{:S(2)}) async-start(bf16[8,256,304]{1,2,0:T(8,128)(2,1)} %broadcast_in_dim.23), calls=%async_computation | async-start | bytes 2490368 | tf_op jit(solution)/shard_map/all_to_all | solution.py:40
  68.7 5.1 %copy-start.10 = (f32[10,2,2432]{2,1,0:T(2,128)S(1)}, f32[10,2,2432]{2,1,0:T(2,128)}, u32[]{:S(2)}) copy-start(f32[10,2,2432]{2,1,0:T(2,128)} %param.11) | copy-start | bytes 583684
  68.7 7.5 %copy-start.14 = (bf16[32,304]{1,0:T(8,128)(2,1)S(1)}, bf16[32,304]{1,0:T(8,128)(2,1)}, u32[]{:S(2)}) copy-start(bf16[32,304]{1,0:T(8,128)(2,1)} %param.13) | copy-start | bytes 58372
  71.1 39.3 %collective-permute-start.1 = (bf16[1216,768]{1,0:T(8,128)(2,1)S(1)}, bf16[1216,768]{1,0:T(8,128)(2,1)}, u32[]{:S(2)}, u32[]{:S(2)}) collective-permute-start(bf16[1216,768]{1,0:T(8,128)(2,1)S(1)} %bitcast.148), channel_id=1, source_target_pairs={{0,256},{256,0},{1,257},{257,1},{2,258},{258,2},{3,259},{259,3},{4... | collective-permute-start | bytes 5603336 | tf_op jit(solution)/shard_map/ppermute | solution.py:44
  76.9 29.1 %all-to-all-start.2 = ((bf16[16,32,304]{2,1,0:T(8,128)(2,1)}), bf16[16,32,304]{2,1,0:T(8,128)(2,1)S(1)}, u32[]{:S(2)}, u32[]{:S(2)}) async-start(bf16[16,32,304]{2,1,0:T(8,128)(2,1)} %broadcast_in_dim.26), calls=%async_computation.2 | async-start | bytes 786432 | tf_op jit(solution)/shard_map/all_to_all | solution.py:40
  106.0 18.8 %collective-permute-start.2 = (bf16[512,304]{1,0:T(8,128)(2,1)S(1)}, bf16[512,304]{1,0:T(8,128)(2,1)}, u32[]{:S(2)}, u32[]{:S(2)}) collective-permute-start(bf16[512,304]{1,0:T(8,128)(2,1)S(1)} %bitcast.158), channel_id=1, source_target_pairs={{0,128},{128,0},{1,129},{129,1},{2,130},{130,2},{3,131},{131,3},{4... | collective-permute-start | bytes 933896 | tf_op jit(solution)/shard_map/ppermute | solution.py:44
  110.4 4.4 %copy-start.3 = (bf16[8,256,304]{1,2,0:T(8,128)(2,1)S(1)}, bf16[8,256,304]{1,2,0:T(8,128)(2,1)}, u32[]{:S(2)}) copy-start(bf16[8,256,304]{1,2,0:T(8,128)(2,1)} %fusion.13) | copy-start | bytes 3735556
  113.0 1.8 copy-start
  118.6 15.8 %all-to-all-start.1 = ((bf16[8,256,256]{1,2,0:T(8,128)(2,1)}), bf16[8,256,256]{1,2,0:T(8,128)(2,1)S(1)}, u32[]{:S(2)}, u32[]{:S(2)}) async-start(bf16[8,256,256]{1,2,0:T(8,128)(2,1)} %broadcast_in_dim.25), calls=%async_computation.1 | async-start | bytes 2097152 | tf_op jit(solution)/shard_map/all_to_all | solution.py:40
  127.5 4.1 %collective-permute-start.3 = (bf16[1024,304]{0,1:T(8,128)(2,1)}, bf16[1024,304]{0,1:T(8,128)(2,1)S(1)}, u32[]{:S(2)}, u32[]{:S(2)}) collective-permute-start(bf16[1024,304]{0,1:T(8,128)(2,1)} %copy.65), channel_id=1, source_target_pairs={{0,256},{256,0},{1,257},{257,1},{2,258},{258,2},{3,259},{259,3},{4... | collective-permute-start | bytes 1867784 | tf_op jit(solution)/shard_map/ppermute | solution.py:44
  131.8 2.5 %copy-start.4 = (bf16[2,1,256,304]{2,3,1,0:T(8,128)(2,1)S(1)}, bf16[2,1,256,304]{2,3,1,0:T(8,128)(2,1)}, u32[]{:S(2)}) copy-start(bf16[2,1,256,304]{2,3,1,0:T(8,128)(2,1)} %param.10) | copy-start | bytes 933892
  131.9 2.5 %copy-start.8 = (f32[1,256,304]{1,2,0:T(8,128)S(1)}, f32[1,256,304]{1,2,0:T(8,128)}, u32[]{:S(2)}) copy-start(f32[1,256,304]{1,2,0:T(8,128)} %param.9) | copy-start | bytes 933892
  132.0 4.8 %copy-start.2 = (bf16[2,38,8,1024]{3,2,0,1:T(8,128)(2,1)}, bf16[2,38,8,1024]{3,2,0,1:T(8,128)(2,1)S(1)}, u32[]{:S(2)}) copy-start(bf16[2,38,8,1024]{3,2,0,1:T(8,128)(2,1)S(1)} %copy.80) | copy-start | bytes 3735556
  135.6 6.6 %copy-start.13 = (f32[2432]{0:T(1024)S(1)}, f32[2432]{0:T(1024)}, u32[]{:S(2)}) copy-start(f32[2432]{0:T(1024)} %get-tuple-element.10) | copy-start | bytes 29188
  135.6 6.7 %copy-start.12 = (f32[2432]{0:T(1024)S(1)}, f32[2432]{0:T(1024)}, u32[]{:S(2)}) copy-start(f32[2432]{0:T(1024)} %get-tuple-element.9) | copy-start | bytes 29188
  135.6 6.8 %copy-start.15 = (s32[64]{0:T(128)S(1)}, s32[64]{0:T(128)}, u32[]{:S(2)}) copy-start(s32[64]{0:T(128)} %param.15) | copy-start | bytes 772
  135.6 6.8 %copy-start.16 = (f32[64]{0:T(128)S(1)}, f32[64]{0:T(128)}, u32[]{:S(2)}) copy-start(f32[64]{0:T(128)} %param.14) | copy-start | bytes 772
  136.7 20.1 %all-to-all-start.3 = ((bf16[8,256,304]{1,2,0:T(8,128)(2,1)}), bf16[8,256,304]{1,2,0:T(8,128)(2,1)S(1)}, u32[]{:S(2)}, u32[]{:S(2)}) async-start(bf16[8,256,304]{1,2,0:T(8,128)(2,1)} %broadcast_in_dim.27), calls=%async_computation.3 | async-start | bytes 2490368 | tf_op jit(solution)/shard_map/all_to_all | solution.py:40
  157.2 2.1 copy-start.1
  161.9 7.5 %copy-start.17 = (f32[2,64]{1,0:T(2,128)S(1)}, f32[2,64]{1,0:T(2,128)}, u32[]{:S(2)}) copy-start(f32[2,64]{1,0:T(2,128)} %param.17) | copy-start | bytes 1540
  162.0 10.3 %copy-start.5 = (bf16[2,1,256,304]{2,3,1,0:T(8,128)(2,1)S(1)}, bf16[2,1,256,304]{2,3,1,0:T(8,128)(2,1)}, u32[]{:S(2)}) copy-start(bf16[2,1,256,304]{2,3,1,0:T(8,128)(2,1)} %param.10) | copy-start | bytes 933892
  163.0 18.5 %all-to-all-start.4 = ((bf16[8,256,256]{1,2,0:T(8,128)(2,1)}), bf16[8,256,256]{1,2,0:T(8,128)(2,1)S(1)}, u32[]{:S(2)}, u32[]{:S(2)}) async-start(bf16[8,256,256]{1,2,0:T(8,128)(2,1)} %broadcast_in_dim.29), calls=%async_computation.4 | async-start | bytes 2097152 | tf_op jit(solution)/shard_map/all_to_all | solution.py:40
  173.5 8.6 %copy-start.11 = (bf16[1,256,304]{1,2,0:T(8,128)(2,1)S(1)}, bf16[1,256,304]{1,2,0:T(8,128)(2,1)}, u32[]{:S(2)}) copy-start(bf16[1,256,304]{1,2,0:T(8,128)(2,1)} %get-tuple-element.16) | copy-start | bytes 466948
  185.8 3.9 %collective-permute-start.4 = (bf16[1024,304]{0,1:T(8,128)(2,1)S(1)}, bf16[1024,304]{0,1:T(8,128)(2,1)S(1)}, u32[]{:S(2)}, u32[]{:S(2)}) collective-permute-start(bf16[1024,304]{0,1:T(8,128)(2,1)S(1)} %fusion.26), channel_id=1, source_target_pairs={{0,256},{256,0},{1,257},{257,1},{2,258},{258,2},{3,259},{259,3},{4... | collective-permute-start | bytes 1867784 | tf_op jit(solution)/shard_map/ppermute | solution.py:53
  192.8 12.9 %collective-permute-start.5 = (bf16[512,304]{0,1:T(8,128)(2,1)S(1)}, bf16[512,304]{0,1:T(8,128)(2,1)}, u32[]{:S(2)}, u32[]{:S(2)}) collective-permute-start(bf16[512,304]{0,1:T(8,128)(2,1)S(1)} %bitcast.172), channel_id=1, source_target_pairs={{0,128},{128,0},{1,129},{129,1},{2,130},{130,2},{3,131},{131,3},{4... | collective-permute-start | bytes 933896 | tf_op jit(solution)/shard_map/ppermute | solution.py:53
  195.4 22.5 %copy-start.6 = (bf16[2,1,256,304]{2,3,1,0:T(8,128)(2,1)S(1)}, bf16[2,1,256,304]{2,3,1,0:T(8,128)(2,1)}, u32[]{:S(2)}) copy-start(bf16[2,1,256,304]{2,3,1,0:T(8,128)(2,1)} %param.10) | copy-start | bytes 933892
  195.9 22.0 %copy-start.9 = (f32[1,256,304]{1,2,0:T(8,128)S(1)}, f32[1,256,304]{1,2,0:T(8,128)}, u32[]{:S(2)}) copy-start(f32[1,256,304]{1,2,0:T(8,128)} %param.9) | copy-start | bytes 933892
  195.9 22.0 %copy-start.18 = (f32[256,304]{0,1:T(8,128)S(1)}, f32[256,304]{0,1:T(8,128)}, u32[]{:S(2)}) copy-start(f32[256,304]{0,1:T(8,128)} %get-tuple-element.20) | copy-start | bytes 933892
  207.7 32.2 %all-to-all-start.5 = ((bf16[16,32,304]{2,1,0:T(8,128)(2,1)}), bf16[16,32,304]{2,1,0:T(8,128)(2,1)S(1)}, u32[]{:S(2)}, u32[]{:S(2)}) async-start(bf16[16,32,304]{2,1,0:T(8,128)(2,1)} %bitcast.50), calls=%async_computation.5 | async-start | bytes 786432 | tf_op jit(solution)/shard_map/all_to_all | solution.py:157

commit v8 on v3

--- a/solution.py
+++ b/solution.py
@@ -66,6 +66,7 @@
     log_ratio,
     z_size,
     seq_size,
+    samples_total,
 ):
     units = qkv_weight.shape[0] * qkv_weight.shape[1]
     qkv_t = jnp.transpose(qkv_weight, (2, 0, 1)).reshape(qkv_weight.shape[2], units)
@@ -73,6 +74,10 @@
     qkv_t = gather_pair(qkv_t, "xh").reshape(-1, units)
     projection_t = gather_pair(qkv_t, "grp").reshape(-1, units)
     first_blocks = gather_all_to_all(latents[0].astype(jnp.bfloat16), FEATURE_AXES, seq_size)
+    noise_parts = gather_all_to_all(step_noise[:, 0], FEATURE_AXES, seq_size)
+    noise_full = jnp.transpose(noise_parts, (1, 2, 0, 3)).reshape(
+        step_noise.shape[0], latents.shape[1], -1
+    )
     first_blocks, out_weight = lax.optimization_barrier((first_blocks, out_weight))
     out_rows = gather_all_to_all(out_weight, "z", z_size).reshape(-1, out_weight.shape[1])
     out_rows = gather_pair(out_rows, "xh").reshape(-1, out_weight.shape[1])
@@ -141,21 +146,30 @@
             * (1.0 + noise_level * (1.0 - time_now) / (2.0 * time_now))
             / std_dev
         )
-        score_list.append((factor * noise_now).astype(jnp.bfloat16))
-        attn_list.append(attn_all)
+        score_list.append((factor * noise_full[section].astype(jnp.float32)).astype(jnp.bfloat16))
+        attn_list.append(attn)
     attn_both = jnp.stack(attn_list, 0)
     score_both = jnp.stack(score_list, 0)
-    gradient = lax.dot_general(
+    rows_here = lax.dot_general(
         attn_both, score_both, (((0, 1), (0, 1)), ((), ())), preferred_element_type=jnp.float32
     )
-    rows = gradient.shape[0]
-    part = gradient.reshape(2, rows // 2, -1)
+    out_shape = out_weight.shape
+    row_blocks = rows_here.shape[0] // out_shape[0]
+    feature_block = out_shape[1]
+    part = rows_here.reshape(row_blocks, out_shape[0], 2, 2, 2, feature_block)
+    part = jnp.transpose(part, (2, 3, 4, 0, 1, 5))
     part = reduce_pair(part, "grp")
-    part = part.reshape(2, rows // 4, -1)
     part = reduce_pair(part, "xh")
-    part = part.reshape(z_size, rows // (4 * z_size), -1)
+    part = part.reshape(z_size, out_shape[0], feature_block)
     part = lax.all_to_all(part.astype(jnp.bfloat16), "z", 0, 0, tiled=True)
-    out_grad = jnp.sum(part.astype(jnp.float32), 0)
+    summed = jnp.sum(part.astype(jnp.float32), 0)
+    owners = samples_total
+    pairs = [
+        (q * seq_size + f, ((f * row_blocks) + q % row_blocks) * seq_size + q // row_blocks)
+        for q in range(owners)
+        for f in range(seq_size)
+    ]
+    out_grad = lax.ppermute(summed, SAMPLE_AXES + FEATURE_AXES, pairs)
     return (state[None], loss_value, out_grad)
 
 
@@ -170,7 +184,7 @@
     features = FEATURE_AXES
 
     def body(*args):
-        return on_device(*args, z_size=z_size, seq_size=seq)
+        return on_device(*args, z_size=z_size, seq_size=seq, samples_total=grp * dp)
 
     return jax.shard_map(
         body,

time: 252 us -> 303 us (1.20)
  the two profiles are of different devices: /device:TPU:24 before, /device:TPU:18 now
where the time goes in v8:
time: 303 us; the launch traced here: 302 us
  blocking collectives  92.8 us (31%)
  waiting for transfers between devices  85.5 us (28%)
  starting transfers between devices  54.8 us (18%)
  local copies, waits for them, and re-layouts  33.9 us (11%)
  other arithmetic  16.3 us (5%)
  matrix products  13.4 us (4%)
  between operations  5.32 us (2%)
    ppermute x4, waiting for transfers between devices, gather_pair(): other = lax.ppermute(x, axis_name, [(0, 1), (1, 0)])  41.4 us
    all_gather x1, blocking collectives, on_device(): qkv_t = lax.all_gather(qkv_t, 'z', axis=0, tiled=True)  41.1 us
    all_to_all x1, blocking collectives, on_device(): part = lax.all_to_all(part.astype(jnp.bfloat16), 'z', 0, 0, tiled=True)  38.1 us
    all_to_all x5, starting transfers between devices, gather_all_to_all(): return lax.all_to_all(spread, axis_name, 0, 0, tiled=True)  32.2 us
    all_to_all x5, waiting for transfers between devices, gather_all_to_all(): return lax.all_to_all(spread, axis_name, 0, 0, tiled=True)  21.5 us
    ppermute x2, waiting for transfers between devices, reduce_pair(): sent = lax.ppermute(send.astype(jnp.bfloat16), axis_name, [(0, 1), (1, 0)])  14.6 us
    all_to_all x1, blocking collectives, gather_all_to_all(): return lax.all_to_all(spread, axis_name, 0, 0, tiled=True)  13.5 us
    ppermute x4, starting transfers between devices, gather_pair(): other = lax.ppermute(x, axis_name, [(0, 1), (1, 0)])  13.3 us
  transfers between devices with their start and end apart: 12, of which 10 were waited for; matrix products, arithmetic and copies ran while one was open for 11% of the time, Pallas kernels for 0%

profile of v8, /device:TPU:18, one launch (start us, length us, event | category | flops | bytes accessed | tf_op | source)
XLA Modules:
  0.0 302.0 jit_solution(9470167688772307443)
XLA Ops:
  0.6 0.9 copy.63
  1.6 41.1 %all-gather = bf16[16,38,768]{2,1,0:T(8,128)(2,1)S(1)} all-gather(bf16[1,38,768]{2,1,0:T(8,128)(2,1)S(1)} %reshape.284), channel_id=1, replica_groups=mesh['grp'=2,'xh'=2,'z'=16,'y'=4,'xl'=2] {'z'}, dimensions={0}, use_global_device_ids=true | all-gather | bytes 992256 | tf_op jit(solution)/shard_map/all_gather | solution.py:73
  43.0 4.0 %collective-permute-start = (bf16[608,768]{1,0:T(8,128)(2,1)S(1)}, bf16[608,768]{1,0:T(8,128)(2,1)}, u32[]{:S(2)}, u32[]{:S(2)}) collective-permute-start(bf16[608,768]{1,0:T(8,128)(2,1)S(1)} %reshape.285), channel_id=1, source_target_pairs={{0,128},{128,0},{1,129},{129,1},{2,130},{130,2},{3,131},{131,3},{4... | collective-permute-start | bytes 2801672 | tf_op jit(solution)/shard_map/ppermute | solution.py:44
  47.1 1.1 broadcast_in_dim.27
  48.2 5.7 %all-to-all-start = ((bf16[8,256,304]{1,2,0:T(8,128)(2,1)}), bf16[8,256,304]{1,2,0:T(8,128)(2,1)S(1)}, u32[]{:S(2)}, u32[]{:S(2)}) async-start(bf16[8,256,304]{1,2,0:T(8,128)(2,1)} %broadcast_in_dim.27), calls=%async_computation | async-start | bytes 2490368 | tf_op jit(solution)/shard_map/all_to_all | solution.py:40
  53.9 1.2 stack.52
  55.1 13.6 %collective-permute-done = bf16[608,768]{1,0:T(8,128)(2,1)} collective-permute-done((bf16[608,768]{1,0:T(8,128)(2,1)S(1)}, bf16[608,768]{1,0:T(8,128)(2,1)}, u32[]{:S(2)}, u32[]{:S(2)}) %collective-permute-start) | collective-permute-done | bytes 933920 | tf_op jit(solution)/shard_map/ppermute | solution.py:44
  68.7 2.5 maximum_select_fusion.1
  71.1 1.9 collective-permute-start.1
  74.3 1.0 all-to-all-done
  75.3 0.8 broadcast_in_dim.30
  76.1 6.8 %all-to-all-start.2 = ((bf16[16,32,304]{2,1,0:T(8,128)(2,1)}), bf16[16,32,304]{2,1,0:T(8,128)(2,1)S(1)}, u32[]{:S(2)}, u32[]{:S(2)}) async-start(bf16[16,32,304]{2,1,0:T(8,128)(2,1)} %broadcast_in_dim.30), calls=%async_computation.2 | async-start | bytes 786432 | tf_op jit(solution)/shard_map/all_to_all | solution.py:40
  83.6 0.8 fusion.13
  84.4 2.6 maximum_select_fusion
  87.0 1.8 copy-done.1
  88.8 1.2 convolution_convert_fusion.1
  91.5 14.3 %all-to-all-done.2 = bf16[16,32,304]{2,1,0:T(8,128)(2,1)S(1)} async-done(((bf16[16,32,304]{2,1,0:T(8,128)(2,1)}), bf16[16,32,304]{2,1,0:T(8,128)(2,1)S(1)}, u32[]{:S(2)}, u32[]{:S(2)}) %all-to-all-start.2) | async-done | bytes 311328 | tf_op jit(solution)/shard_map/all_to_all | solution.py:40
  105.9 13.5 %all_to_all.35 = bf16[8,256,256]{1,2,0:T(8,128)(2,1)} all-to-all(bf16[8,256,256]{1,2,0:T(8,128)(2,1)S(1)} %broadcast_in_dim.29), channel_id=1, replica_groups=mesh['grp'=2,'xh'=2,'z'=16,'y'=4,'xl'=2] {'y','xl'}, dimensions={0} | all-to-all | bytes 2097152 | tf_op jit(solution)/shard_map/all_to_all | solution.py:40
  119.4 1.6 broadcast_in_dim.37
  121.1 7.1 %all-to-all-start.5 = ((bf16[8,2,256,304]{2,3,1,0:T(8,128)(2,1)}), bf16[8,2,256,304]{2,3,1,0:T(8,128)(2,1)S(1)}, u32[]{:S(2)}, u32[]{:S(2)}) async-start(bf16[8,2,256,304]{2,3,1,0:T(8,128)(2,1)} %broadcast_in_dim.37), calls=%async_computation.5 | async-start | bytes 4980736 | tf_op jit(solution)/shard_map/all_to_all | solution.py:40
  128.2 5.5 %collective-permute-start.2 = (bf16[512,304]{1,0:T(8,128)(2,1)S(1)}, bf16[512,304]{1,0:T(8,128)(2,1)}, u32[]{:S(2)}, u32[]{:S(2)}) collective-permute-start(bf16[512,304]{1,0:T(8,128)(2,1)S(1)} %bitcast.155), channel_id=1, source_target_pairs={{0,128},{128,0},{1,129},{129,1},{2,130},{130,2},{3,131},{131,3},{4... | collective-permute-start | bytes 933896 | tf_op jit(solution)/shard_map/ppermute | solution.py:44
  133.6 27.3 %collective-permute-done.2 = bf16[512,304]{1,0:T(8,128)(2,1)} collective-permute-done((bf16[512,304]{1,0:T(8,128)(2,1)S(1)}, bf16[512,304]{1,0:T(8,128)(2,1)}, u32[]{:S(2)}, u32[]{:S(2)}) %collective-permute-start.2) | collective-permute-done | bytes 311328 | tf_op jit(solution)/shard_map/ppermute | solution.py:44
  161.0 1.1 copy.66
  162.1 0.9 copy.67
  163.1 1.6 maximum_select_fusion.3
  164.7 1.1 copy.69
  165.8 1.9 collective-permute-start.3
  168.4 1.1 copy.70
  170.1 1.9 fusion.22
  172.1 1.0 copy-done.4
  173.8 1.2 fusion.44
  175.0 1.2 broadcast_in_dim.31
  176.3 0.7 copy-done
  176.9 5.7 %all-to-all-start.3 = ((bf16[8,256,304]{1,2,0:T(8,128)(2,1)}), bf16[8,256,304]{1,2,0:T(8,128)(2,1)S(1)}, u32[]{:S(2)}, u32[]{:S(2)}) async-start(bf16[8,256,304]{1,2,0:T(8,128)(2,1)} %broadcast_in_dim.31), calls=%async_computation.3 | async-start | bytes 2490368 | tf_op jit(solution)/shard_map/all_to_all | solution.py:40
  182.9 0.7 fusion.38
  183.5 0.6 fusion.45
  185.5 1.9 copy.92
  187.4 1.7 multiply_convert_fusion.1
  189.0 2.4 copy.76
  191.4 1.6 copy.77
  193.0 4.4 %all-to-all-done.3 = bf16[8,256,304]{1,2,0:T(8,128)(2,1)S(1)} async-done(((bf16[8,256,304]{1,2,0:T(8,128)(2,1)}), bf16[8,256,304]{1,2,0:T(8,128)(2,1)S(1)}, u32[]{:S(2)}, u32[]{:S(2)}) %all-to-all-start.3) | async-done | bytes 1245216 | tf_op jit(solution)/shard_map/all_to_all | solution.py:40
  198.2 0.8 fusion.9
  199.0 0.8 copy-done.2
  199.8 1.2 convolution_convert_fusion
  201.2 1.3 convolution_multiply_fusion
  203.1 2.1 convolution_convert_fusion.2
  205.2 0.7 copy-done.17
  205.8 2.3 convolution_bitcast_fusion
  208.2 5.6 %reshape.283 = f32[8,32,2,2,2,304]{5,4,3,2,1,0:T(2,128)S(1)} reshape(f32[256,2432]{1,0:T(8,128)} %convolution_bitcast_fusion) | data formatting | bytes 4980736 | tf_op jit(solution)/shard_map/reshape | solution.py:159
  213.8 0.6 constant_dynamic-slice_fusion
  214.3 1.0 copy.93
  215.3 1.9 collective-permute-start.4
  217.8 2.0 collective-permute-done.4
  219.8 1.4 fusion.17
  221.3 2.0 collective-permute-start.5
  223.3 12.6 %collective-permute-done.5 = bf16[2,8,32,304]{3,2,1,0:T(8,128)(2,1)S(1)} collective-permute-done((bf16[2,8,32,304]{3,2,1,0:T(8,128)(2,1)S(1)}, bf16[2,8,32,304]{3,2,1,0:T(8,128)(2,1)S(1)}, u32[]{:S(2)}, u32[]{:S(2)}) %collective-permute-start.5) | collective-permute-done | bytes 311328 | tf_op jit(solution)/shard_map/ppermute | solution.py:53
  235.9 38.1 %all_to_all.36 = bf16[16,32,304]{2,1,0:T(8,128)(2,1)S(1)} all-to-all(bf16[16,32,304]{2,1,0:T(8,128)(2,1)S(1)} %bitcast.157), channel_id=1, replica_groups=mesh['grp'=2,'xh'=2,'z'=16,'y'=4,'xl'=2] {'z'}, dimensions={0} | all-to-all | bytes 622592 | tf_op jit(solution)/shard_map/all_to_all | solution.py:164
  274.1 1.1 broadcast_in_dim.33
  275.1 6.9 %all-to-all-start.4 = ((bf16[8,256,256]{1,2,0:T(8,128)(2,1)}), bf16[8,256,256]{1,2,0:T(8,128)(2,1)S(1)}, u32[]{:S(2)}, u32[]{:S(2)}) async-start(bf16[8,256,256]{1,2,0:T(8,128)(2,1)} %broadcast_in_dim.33), calls=%async_computation.4 | async-start | bytes 2097152 | tf_op jit(solution)/shard_map/all_to_all | solution.py:40
  282.8 5.4 %collective-permute-start.6 = (f32[32,304]{1,0:T(8,128)S(1)}, f32[32,304]{1,0:T(8,128)S(1)}, u32[]{:S(2)}, u32[]{:S(2)}) collective-permute-start(f32[32,304]{1,0:T(8,128)S(1)} %convert_reduce_fusion.2), channel_id=1, source_target_pairs={{0,0},{1,64},{2,128},{3,192},{4,256},{5,320},{6,384},{7,448},{8,8}... | collective-permute-start | bytes 116744 | tf_op jit(solution)/shard_map/ppermute | solution.py:172
  288.2 1.8 all-to-all-done.4
  290.0 2.2 fusion.26
  292.2 8.0 %collective-permute-done.6 = f32[32,304]{1,0:T(8,128)S(1)} collective-permute-done((f32[32,304]{1,0:T(8,128)S(1)}, f32[32,304]{1,0:T(8,128)S(1)}, u32[]{:S(2)}, u32[]{:S(2)}) %collective-permute-start.6) | collective-permute-done | bytes 38944 | tf_op jit(solution)/shard_map/ppermute | solution.py:172
  300.2 0.6 copy.96
  (80 shorter events, 7.1 us)
Async XLA Ops:
  0.6 46.4 %copy-start.9 = (f32[1,256,304]{1,2,0:T(8,128)S(1)}, f32[1,256,304]{1,2,0:T(8,128)}, u32[]{:S(2)}) copy-start(f32[1,256,304]{1,2,0:T(8,128)} %param.9) | copy-start | bytes 933892
  43.0 25.7 %collective-permute-start = (bf16[608,768]{1,0:T(8,128)(2,1)S(1)}, bf16[608,768]{1,0:T(8,128)(2,1)}, u32[]{:S(2)}, u32[]{:S(2)}) collective-permute-start(bf16[608,768]{1,0:T(8,128)(2,1)S(1)} %reshape.285), channel_id=1, source_target_pairs={{0,128},{128,0},{1,129},{129,1},{2,130},{130,2},{3,131},{131,3},{4... | collective-permute-start | bytes 2801672 | tf_op jit(solution)/shard_map/ppermute | solution.py:44
  48.2 27.1 %all-to-all-start = ((bf16[8,256,304]{1,2,0:T(8,128)(2,1)}), bf16[8,256,304]{1,2,0:T(8,128)(2,1)S(1)}, u32[]{:S(2)}, u32[]{:S(2)}) async-start(bf16[8,256,304]{1,2,0:T(8,128)(2,1)} %broadcast_in_dim.27), calls=%async_computation | async-start | bytes 2490368 | tf_op jit(solution)/shard_map/all_to_all | solution.py:40
  68.7 5.1 %copy-start.14 = (f32[10,2,2432]{2,1,0:T(2,128)S(1)}, f32[10,2,2432]{2,1,0:T(2,128)}, u32[]{:S(2)}) copy-start(f32[10,2,2432]{2,1,0:T(2,128)} %param.11) | copy-start | bytes 583684
  68.7 6.6 %copy-start.19 = (bf16[32,304]{1,0:T(8,128)(2,1)S(1)}, bf16[32,304]{1,0:T(8,128)(2,1)}, u32[]{:S(2)}) copy-start(bf16[32,304]{1,0:T(8,128)(2,1)} %param.13) | copy-start | bytes 58372
  71.1 13.3 %collective-permute-start.1 = (bf16[1216,768]{1,0:T(8,128)(2,1)S(1)}, bf16[1216,768]{1,0:T(8,128)(2,1)}, u32[]{:S(2)}, u32[]{:S(2)}) collective-permute-start(bf16[1216,768]{1,0:T(8,128)(2,1)S(1)} %bitcast.147), channel_id=1, source_target_pairs={{0,256},{256,0},{1,257},{257,1},{2,258},{258,2},{3,259},{259,3},{4... | collective-permute-start | bytes 5603336 | tf_op jit(solution)/shard_map/ppermute | solution.py:44
  76.1 29.8 %all-to-all-start.2 = ((bf16[16,32,304]{2,1,0:T(8,128)(2,1)}), bf16[16,32,304]{2,1,0:T(8,128)(2,1)S(1)}, u32[]{:S(2)}, u32[]{:S(2)}) async-start(bf16[16,32,304]{2,1,0:T(8,128)(2,1)} %broadcast_in_dim.30), calls=%async_computation.2 | async-start | bytes 786432 | tf_op jit(solution)/shard_map/all_to_all | solution.py:40
  87.0 1.8 copy-start.1
  91.5 29.6 %copy-start.15 = (bf16[4,64,256]{2,1,0:T(8,128)(2,1)}, bf16[4,64,256]{2,1,0:T(8,128)(2,1)S(1)}, u32[]{:S(2)}) copy-start(bf16[4,64,256]{2,1,0:T(8,128)(2,1)S(1)} %convolution_convert_fusion.3) | copy-start | bytes 393220
  91.5 27.9 %copy-start.11 = (bf16[2,1,256,304]{2,3,1,0:T(8,128)(2,1)S(1)}, bf16[2,1,256,304]{2,3,1,0:T(8,128)(2,1)}, u32[]{:S(2)}) copy-start(bf16[2,1,256,304]{2,3,1,0:T(8,128)(2,1)} %param.10) | copy-start | bytes 933892
  105.8 22.4 %copy-start.3 = (bf16[16,32,304]{2,1,0:T(8,128)(2,1)}, bf16[16,32,304]{2,1,0:T(8,128)(2,1)S(1)}, u32[]{:S(2)}) copy-start(bf16[16,32,304]{2,1,0:T(8,128)(2,1)S(1)} %all-to-all-done.2) | copy-start | bytes 933892
  121.1 54.0 %all-to-all-start.5 = ((bf16[8,2,256,304]{2,3,1,0:T(8,128)(2,1)}), bf16[8,2,256,304]{2,3,1,0:T(8,128)(2,1)S(1)}, u32[]{:S(2)}, u32[]{:S(2)}) async-start(bf16[8,2,256,304]{2,3,1,0:T(8,128)(2,1)} %broadcast_in_dim.37), calls=%async_computation.5 | async-start | bytes 4980736 | tf_op jit(solution)/shard_map/all_to_all | solution.py:40
  128.2 32.8 %collective-permute-start.2 = (bf16[512,304]{1,0:T(8,128)(2,1)S(1)}, bf16[512,304]{1,0:T(8,128)(2,1)}, u32[]{:S(2)}, u32[]{:S(2)}) collective-permute-start(bf16[512,304]{1,0:T(8,128)(2,1)S(1)} %bitcast.155), channel_id=1, source_target_pairs={{0,128},{128,0},{1,129},{129,1},{2,130},{130,2},{3,131},{131,3},{4... | collective-permute-start | bytes 933896 | tf_op jit(solution)/shard_map/ppermute | solution.py:44
  162.1 6.1 %copy-start.20 = (s32[64]{0:T(128)S(1)}, s32[64]{0:T(128)}, u32[]{:S(2)}) copy-start(s32[64]{0:T(128)} %param.15) | copy-start | bytes 772
  162.1 6.1 %copy-start.21 = (f32[64]{0:T(128)S(1)}, f32[64]{0:T(128)}, u32[]{:S(2)}) copy-start(f32[64]{0:T(128)} %param.14) | copy-start | bytes 772
  165.8 4.3 %collective-permute-start.3 = (bf16[1024,304]{0,1:T(8,128)(2,1)}, bf16[1024,304]{0,1:T(8,128)(2,1)}, u32[]{:S(2)}, u32[]{:S(2)}) collective-permute-start(bf16[1024,304]{0,1:T(8,128)(2,1)} %copy.69), channel_id=1, source_target_pairs={{0,256},{256,0},{1,257},{257,1},{2,258},{258,2},{3,259},{259,3},{4... | collective-permute-start | bytes 1867784 | tf_op jit(solution)/shard_map/ppermute | solution.py:44
  172.0 1.6 copy-start.8
  172.0 1.7 copy-start.10
  172.0 1.8 copy-start.12
  172.1 1.1 copy-start.4
  175.0 1.9 copy-start
  175.0 7.8 %copy-start.22 = (f32[2,64]{1,0:T(2,128)S(1)}, f32[2,64]{1,0:T(2,128)}, u32[]{:S(2)}) copy-start(f32[2,64]{1,0:T(2,128)} %param.17) | copy-start | bytes 1540
  176.9 20.5 %all-to-all-start.3 = ((bf16[8,256,304]{1,2,0:T(8,128)(2,1)}), bf16[8,256,304]{1,2,0:T(8,128)(2,1)S(1)}, u32[]{:S(2)}, u32[]{:S(2)}) async-start(bf16[8,256,304]{1,2,0:T(8,128)(2,1)} %broadcast_in_dim.31), calls=%async_computation.3 | async-start | bytes 2490368 | tf_op jit(solution)/shard_map/all_to_all | solution.py:40
  197.8 2.1 copy-start.2
  203.1 2.8 copy-start.6
  203.1 2.8 copy-start.7
  203.1 2.7 copy-start.16
  205.2 0.7 copy-start.17
  215.3 4.5 %collective-permute-start.4 = (bf16[2,2,8,32,304]{4,3,2,1,0:T(8,128)(2,1)}, bf16[2,2,8,32,304]{4,3,2,1,0:T(8,128)(2,1)}, u32[]{:S(2)}, u32[]{:S(2)}) collective-permute-start(bf16[2,2,8,32,304]{4,3,2,1,0:T(8,128)(2,1)} %bitcast.142), channel_id=1, source_target_pairs={{0,256},{256,0},{1,257},{257,1},{2,258},{258,2},{3,259},{259,3},{4... | collective-permute-start | bytes 1867784 | tf_op jit(solution)/shard_map/ppermute | solution.py:53
  221.2 52.9 %copy-start.18 = (bf16[4,64,256]{2,1,0:T(8,128)(2,1)S(1)}, bf16[4,64,256]{2,1,0:T(8,128)(2,1)}, u32[]{:S(2)}) copy-start(bf16[4,64,256]{2,1,0:T(8,128)(2,1)} %copy-done.17) | copy-start | bytes 393220
  221.3 14.6 %collective-permute-start.5 = (bf16[2,8,32,304]{3,2,1,0:T(8,128)(2,1)S(1)}, bf16[2,8,32,304]{3,2,1,0:T(8,128)(2,1)S(1)}, u32[]{:S(2)}, u32[]{:S(2)}) collective-permute-start(bf16[2,8,32,304]{3,2,1,0:T(8,128)(2,1)S(1)} %fusion.25), channel_id=1, source_target_pairs={{0,128},{128,0},{1,129},{129,1},{2,130},{130,2},{3,131},{131,3},{4... | collective-permute-start | bytes 933896 | tf_op jit(solution)/shard_map/ppermute | solution.py:53
  274.1 15.9 %copy-start.5 = (bf16[2,38,8,1024]{3,2,0,1:T(8,128)(2,1)S(1)}, bf16[2,38,8,1024]{3,2,0,1:T(8,128)(2,1)}, u32[]{:S(2)}) copy-start(bf16[2,38,8,1024]{3,2,0,1:T(8,128)(2,1)} %copy-done.4) | copy-start | bytes 3735556
  274.1 15.9 %copy-start.13 = (bf16[2,1,256,304]{2,3,1,0:T(8,128)(2,1)S(1)}, bf16[2,1,256,304]{2,3,1,0:T(8,128)(2,1)}, u32[]{:S(2)}) copy-start(bf16[2,1,256,304]{2,3,1,0:T(8,128)(2,1)} %param.10) | copy-start | bytes 933892
  275.1 14.8 %all-to-all-start.4 = ((bf16[8,256,256]{1,2,0:T(8,128)(2,1)}), bf16[8,256,256]{1,2,0:T(8,128)(2,1)S(1)}, u32[]{:S(2)}, u32[]{:S(2)}) async-start(bf16[8,256,256]{1,2,0:T(8,128)(2,1)} %broadcast_in_dim.33), calls=%async_computation.4 | async-start | bytes 2097152 | tf_op jit(solution)/shard_map/all_to_all | solution.py:40
  282.8 17.5 %collective-permute-start.6 = (f32[32,304]{1,0:T(8,128)S(1)}, f32[32,304]{1,0:T(8,128)S(1)}, u32[]{:S(2)}, u32[]{:S(2)}) collective-permute-start(f32[32,304]{1,0:T(8,128)S(1)} %convert_reduce_fusion.2), channel_id=1, source_target_pairs={{0,0},{1,64},{2,128},{3,192},{4,256},{5,320},{6,384},{7,448},{8,8}... | collective-permute-start | bytes 116744 | tf_op jit(solution)/shard_map/ppermute | solution.py:172

commit v9 on v7

--- a/solution.py
+++ b/solution.py
@@ -70,8 +70,18 @@
     units = qkv_weight.shape[0] * qkv_weight.shape[1]
     qkv_t = jnp.transpose(qkv_weight, (2, 0, 1)).reshape(qkv_weight.shape[2], units)
     qkv_t = lax.all_gather(qkv_t, "z", axis=0, tiled=True)
-    qkv_t = gather_pair(qkv_t, "xh").reshape(-1, units)
-    projection_t = gather_pair(qkv_t, "grp").reshape(-1, units)
+    swap = [(0, 1), (1, 0)]
+    me_g, me_x = lax.axis_index("grp"), lax.axis_index("xh")
+    from_x = lax.ppermute(qkv_t, "xh", swap)
+    from_g = lax.ppermute(qkv_t, "grp", swap)
+    from_gx = lax.ppermute(from_x, "grp", swap)
+    block_rows = qkv_t.shape[0]
+    weight_blocks = [
+        ((me_g * 2 + me_x) * block_rows, qkv_t),
+        ((me_g * 2 + 1 - me_x) * block_rows, from_x),
+        (((1 - me_g) * 2 + me_x) * block_rows, from_g),
+        (((1 - me_g) * 2 + 1 - me_x) * block_rows, from_gx),
+    ]
     first_blocks = gather_all_to_all(latents[0].astype(jnp.bfloat16), FEATURE_AXES, seq_size)
     first_blocks, out_weight = lax.optimization_barrier((first_blocks, out_weight))
     out_rows = gather_all_to_all(out_weight, "z", z_size).reshape(-1, out_weight.shape[1])
@@ -82,7 +92,7 @@
     heads_here = group_width // HD
     samples = rewards.shape[0]
     seq_len = latents.shape[1]
-    block_rows = min(512, seq_len)
+    query_count = min(512, seq_len)
     advantage = advantages(rewards, group_ids)
     loss_value, coef = policy_terms(advantage, log_ratio)
     my_index = lax.axis_index(SAMPLE_AXES)
@@ -109,13 +119,16 @@
             (whole - centre) * lax.rsqrt(spread + NORM_EPS) * (1.0 + modulate[0][None, :])
             + modulate[1][None, :]
         ).astype(jnp.bfloat16)
-        proj_rows = jnp.dot(normed, projection_t, preferred_element_type=jnp.float32).astype(
-            jnp.bfloat16
-        )
+        proj_sum = None
+        for offset, block in weight_blocks:
+            columns = lax.dynamic_slice_in_dim(normed, offset, block.shape[0], axis=1)
+            term = jnp.dot(columns, block, preferred_element_type=jnp.float32)
+            proj_sum = term if proj_sum is None else proj_sum + term
+        proj_rows = proj_sum.astype(jnp.bfloat16)
         proj_rows = proj_rows.reshape(seq_len, 3, heads_here, HD)
         key_rows = proj_rows[:, 1]
         value_rows = proj_rows[:, 2]
-        query_rows = proj_rows[0:block_rows, 0]
+        query_rows = proj_rows[0:query_count, 0]
         logits = jnp.einsum(
             "qhe,khe->hqk", query_rows, key_rows, preferred_element_type=jnp.float32
         ) * HD ** (-0.5)

time: 244 us -> 243 us (level)
  matrix products: 11 us -> 17.8 us
  waiting for transfers between devices: 91.2 us -> 85.1 us
  starting transfers between devices: 56.3 us -> 60.2 us
  local copies, waits for them, and re-layouts: 21.4 us -> 17.8 us
  blocking collectives: 41.1 us -> 38.2 us
    ppermute x4 -> x2, waiting for transfers between devices: 15.5 us -> 4.79 us  [gather_pair(): other = lax.ppermute(x, axis_name, [(0, 1), (1, 0)])]
    ppermute x0 -> x3, waiting for transfers between devices: none -> 10.3 us  [the longest x1 10.3 us: on_device(): from_x = lax.ppermute(qkv_t, 'xh', swap)]
    ppermute x0 -> x3, starting transfers between devices: none -> 8.47 us  [the longest x1 4.64 us: on_device(): from_x = lax.ppermute(qkv_t, 'xh', swap)]
    ppermute x4 -> x2, starting transfers between devices: 13.1 us -> 6.54 us  [gather_pair(): other = lax.ppermute(x, axis_name, [(0, 1), (1, 0)])]
    dot_general x2 -> x8, matrix products: 2.44 us -> 8.84 us  [on_device(): term = jnp.dot(columns, block, preferred_element_type=jnp.float32)]
    all_to_all x1, starting transfers between devices: 9.5 us -> 5.45 us  [on_device(): part = lax.all_to_all(part.astype(jnp.bfloat16), 'z', 0, 0, tiled=True)]
    all_to_all x5, starting transfers between devices: 29.2 us -> 33.1 us  [gather_all_to_all(): return lax.all_to_all(spread, axis_name, 0, 0, tiled=True)]
    all_to_all x5, waiting for transfers between devices: 44.5 us -> 40.6 us  [gather_all_to_all(): return lax.all_to_all(spread, axis_name, 0, 0, tiled=True)]
  transfers between devices with their start and end apart: 12 -> 13, of which waited for: 10 -> 9; matrix products, arithmetic and copies ran while one was open for 11% -> 10% of each run, Pallas kernels for 0% -> 0%
where the time goes in v9:
time: 243 us; the launch traced here: 240 us
  waiting for transfers between devices  85.1 us (35%)
  starting transfers between devices  60.2 us (25%)
  blocking collectives  38.2 us (16%)
  local copies, waits for them, and re-layouts  17.8 us (7%)
  matrix products  17.8 us (7%)
  other arithmetic  15.9 us (7%)
  between operations  5.37 us (2%)
    all_to_all x5, waiting for transfers between devices, gather_all_to_all(): return lax.all_to_all(spread, axis_name, 0, 0, tiled=True)  40.6 us
    all_gather x1, blocking collectives, on_device(): qkv_t = lax.all_gather(qkv_t, 'z', axis=0, tiled=True)  38.2 us
    all_to_all x5, starting transfers between devices, gather_all_to_all(): return lax.all_to_all(spread, axis_name, 0, 0, tiled=True)  33.1 us
    all_to_all x1, waiting for transfers between devices, on_device(): part = lax.all_to_all(part.astype(jnp.bfloat16), 'z', 0, 0, tiled=True)  19.7 us
    ppermute x1, waiting for transfers between devices, on_device(): from_x = lax.ppermute(qkv_t, 'xh', swap)  10.3 us
    ppermute x2, waiting for transfers between devices, reduce_pair(): sent = lax.ppermute(send.astype(jnp.bfloat16), axis_name, [(0, 1), (1, 0)])  9.68 us
    dot_general x8, matrix products, on_device(): term = jnp.dot(columns, block, preferred_element_type=jnp.float32)  8.84 us
    ppermute x2, starting transfers between devices, reduce_pair(): sent = lax.ppermute(send.astype(jnp.bfloat16), axis_name, [(0, 1), (1, 0)])  6.56 us
  transfers between devices with their start and end apart: 13, of which 9 were waited for; matrix products, arithmetic and copies ran while one was open for 10% of the time, Pallas kernels for 0%

profile of v9, /device:TPU:24, one launch (start us, length us, event | category | flops | bytes accessed | tf_op | source)
XLA Modules:
  0.0 240.3 jit_solution(6884661685823199559)
XLA Ops:
  0.6 1.0 convert_bitcast_fusion
  1.6 1.1 broadcast_in_dim.23
  2.7 9.2 %all-to-all-start = ((bf16[8,256,304]{1,2,0:T(8,128)(2,1)}), bf16[8,256,304]{1,2,0:T(8,128)(2,1)S(1)}, u32[]{:S(2)}, u32[]{:S(2)}) async-start(bf16[8,256,304]{1,2,0:T(8,128)(2,1)} %broadcast_in_dim.23), calls=%async_computation | async-start | bytes 2490368 | tf_op jit(solution)/shard_map/all_to_all | solution.py:40
  12.1 38.2 %all-gather = bf16[16,38,768]{2,1,0:T(8,128)(2,1)S(1)} all-gather(bf16[1,38,768]{2,1,0:T(8,128)(2,1)S(1)} %reshape.206), channel_id=1, replica_groups=mesh['grp'=2,'xh'=2,'z'=16,'y'=4,'xl'=2] {'z'}, dimensions={0}, use_global_device_ids=true | all-gather | bytes 992256 | tf_op jit(solution)/shard_map/all_gather | solution.py:72
  50.5 4.6 %collective-permute-start = (bf16[608,768]{1,0:T(8,128)(2,1)S(1)}, bf16[608,768]{1,0:T(8,128)(2,1)S(1)}, u32[]{:S(2)}, u32[]{:S(2)}) collective-permute-start(bf16[608,768]{1,0:T(8,128)(2,1)S(1)} %reshape.207), channel_id=1, source_target_pairs={{0,128},{128,0},{1,129},{129,1},{2,130},{130,2},{3,131},{131,3},{4... | collective-permute-start | bytes 2801672 | tf_op jit(solution)/shard_map/ppermute | solution.py:75
  55.2 1.9 collective-permute-start.1
  57.8 0.8 multiply_reduce_fusion.2
  58.7 10.3 %collective-permute-done = bf16[608,768]{1,0:T(8,128)(2,1)S(1)} collective-permute-done((bf16[608,768]{1,0:T(8,128)(2,1)S(1)}, bf16[608,768]{1,0:T(8,128)(2,1)S(1)}, u32[]{:S(2)}, u32[]{:S(2)}) %collective-permute-start) | collective-permute-done | bytes 933920 | tf_op jit(solution)/shard_map/ppermute | solution.py:75
  69.0 1.9 collective-permute-start.2
  71.7 0.8 broadcast_in_dim.26
  72.5 7.0 %all-to-all-start.2 = ((bf16[16,32,304]{2,1,0:T(8,128)(2,1)}), bf16[16,32,304]{2,1,0:T(8,128)(2,1)S(1)}, u32[]{:S(2)}, u32[]{:S(2)}) async-start(bf16[16,32,304]{2,1,0:T(8,128)(2,1)} %broadcast_in_dim.26), calls=%async_computation.2 | async-start | bytes 786432 | tf_op jit(solution)/shard_map/all_to_all | solution.py:40
  79.5 1.4 fusion.9
  80.9 0.5 fusion.47
  81.4 0.5 convolution_add_fusion.5
  81.9 1.7 convolution_add_fusion.4
  83.7 1.7 fusion.21
  85.9 19.0 %all-to-all-done.2 = bf16[16,32,304]{2,1,0:T(8,128)(2,1)S(1)} async-done(((bf16[16,32,304]{2,1,0:T(8,128)(2,1)}), bf16[16,32,304]{2,1,0:T(8,128)(2,1)S(1)}, u32[]{:S(2)}, u32[]{:S(2)}) %all-to-all-start.2) | async-done | bytes 311328 | tf_op jit(solution)/shard_map/all_to_all | solution.py:40
  104.9 4.6 %collective-permute-start.3 = (bf16[512,304]{1,0:T(8,128)(2,1)S(1)}, bf16[512,304]{1,0:T(8,128)(2,1)S(1)}, u32[]{:S(2)}, u32[]{:S(2)}) collective-permute-start(bf16[512,304]{1,0:T(8,128)(2,1)S(1)} %bitcast.171), channel_id=1, source_target_pairs={{0,128},{128,0},{1,129},{129,1},{2,130},{130,2},{3,131},{131,3},{4... | collective-permute-start | bytes 933896 | tf_op jit(solution)/shard_map/ppermute | solution.py:44
  109.5 0.5 fusion.72
  110.4 1.0 broadcast_in_dim.25
  111.5 5.0 %all-to-all-start.1 = ((bf16[8,256,256]{1,2,0:T(8,128)(2,1)}), bf16[8,256,256]{1,2,0:T(8,128)(2,1)S(1)}, u32[]{:S(2)}, u32[]{:S(2)}) async-start(bf16[8,256,256]{1,2,0:T(8,128)(2,1)} %broadcast_in_dim.25), calls=%async_computation.1 | async-start | bytes 2097152 | tf_op jit(solution)/shard_map/all_to_all | solution.py:40
  116.4 2.8 %collective-permute-done.3 = bf16[512,304]{1,0:T(8,128)(2,1)S(1)} collective-permute-done((bf16[512,304]{1,0:T(8,128)(2,1)S(1)}, bf16[512,304]{1,0:T(8,128)(2,1)S(1)}, u32[]{:S(2)}, u32[]{:S(2)}) %collective-permute-start.3) | collective-permute-done | bytes 311328 | tf_op jit(solution)/shard_map/ppermute | solution.py:44
  119.4 0.9 copy.63
  120.3 1.4 maximum_select_fusion.1
  121.8 1.1 copy.65
  122.8 1.9 collective-permute-start.4
  125.2 1.9 collective-permute-done.4
  127.1 1.5 fusion.23
  128.7 0.8 copy-done.8
  129.6 2.2 fusion.70
  131.8 1.1 broadcast_in_dim.27
  132.9 6.3 %all-to-all-start.3 = ((bf16[8,256,304]{1,2,0:T(8,128)(2,1)}), bf16[8,256,304]{1,2,0:T(8,128)(2,1)S(1)}, u32[]{:S(2)}, u32[]{:S(2)}) async-start(bf16[8,256,304]{1,2,0:T(8,128)(2,1)} %broadcast_in_dim.27), calls=%async_computation.3 | async-start | bytes 2490368 | tf_op jit(solution)/shard_map/all_to_all | solution.py:40
  139.2 0.7 fusion.51
  139.9 1.4 fusion.53
  141.4 14.0 %all-to-all-done.3 = bf16[8,256,304]{1,2,0:T(8,128)(2,1)S(1)} async-done(((bf16[8,256,304]{1,2,0:T(8,128)(2,1)}), bf16[8,256,304]{1,2,0:T(8,128)(2,1)S(1)}, u32[]{:S(2)}, u32[]{:S(2)}) %all-to-all-start.3) | async-done | bytes 1245216 | tf_op jit(solution)/shard_map/all_to_all | solution.py:40
  156.1 1.4 fusion.5
  158.0 0.7 copy-done.3
  159.2 1.7 convolution_add_fusion.1
  160.9 1.7 fusion.22
  163.1 0.5 fusion.73
  164.0 1.1 broadcast_in_dim.29
  165.1 5.7 %all-to-all-start.4 = ((bf16[8,256,256]{1,2,0:T(8,128)(2,1)}), bf16[8,256,256]{1,2,0:T(8,128)(2,1)S(1)}, u32[]{:S(2)}, u32[]{:S(2)}) async-start(bf16[8,256,256]{1,2,0:T(8,128)(2,1)} %broadcast_in_dim.29), calls=%async_computation.4 | async-start | bytes 2097152 | tf_op jit(solution)/shard_map/all_to_all | solution.py:40
  171.2 0.7 fusion.64
  171.8 0.6 fusion.71
  173.9 0.7 fusion.50
  174.7 1.3 copy.71
  176.0 7.6 %all-to-all-done.4 = bf16[8,256,256]{1,2,0:T(8,128)(2,1)S(1)} async-done(((bf16[8,256,256]{1,2,0:T(8,128)(2,1)}), bf16[8,256,256]{1,2,0:T(8,128)(2,1)S(1)}, u32[]{:S(2)}, u32[]{:S(2)}) %all-to-all-start.4) | async-done | bytes 1048608 | tf_op jit(solution)/shard_map/all_to_all | solution.py:40
  183.6 1.3 copy.72
  184.9 2.0 fusion.14
  187.1 1.3 copy-done.4
  188.4 1.9 collective-permute-start.5
  190.3 2.0 collective-permute-done.5
  192.3 1.4 bitcast_add_fusion
  193.8 1.1 reshape.203
  194.8 0.6 constant_dynamic-slice_fusion
  195.5 4.7 %collective-permute-start.6 = (bf16[512,304]{0,1:T(8,128)(2,1)S(1)}, bf16[512,304]{0,1:T(8,128)(2,1)}, u32[]{:S(2)}, u32[]{:S(2)}) collective-permute-start(bf16[512,304]{0,1:T(8,128)(2,1)S(1)} %bitcast.182), channel_id=1, source_target_pairs={{0,128},{128,0},{1,129},{129,1},{2,130},{130,2},{3,131},{131,3},{4... | collective-permute-start | bytes 933896 | tf_op jit(solution)/shard_map/ppermute | solution.py:53
  200.1 0.5 constant_dynamic-slice_fusion.1
  200.7 7.7 %collective-permute-done.6 = bf16[512,304]{0,1:T(8,128)(2,1)} collective-permute-done((bf16[512,304]{0,1:T(8,128)(2,1)S(1)}, bf16[512,304]{0,1:T(8,128)(2,1)}, u32[]{:S(2)}, u32[]{:S(2)}) %collective-permute-start.6) | collective-permute-done | bytes 311328 | tf_op jit(solution)/shard_map/ppermute | solution.py:53
  208.4 1.1 fusion.25
  209.4 0.9 copy.74
  210.4 5.4 %all-to-all-start.5 = ((bf16[16,32,304]{2,1,0:T(8,128)(2,1)}), bf16[16,32,304]{2,1,0:T(8,128)(2,1)S(1)}, u32[]{:S(2)}, u32[]{:S(2)}) async-start(bf16[16,32,304]{2,1,0:T(8,128)(2,1)} %bitcast.45), calls=%async_computation.5 | async-start | bytes 786432 | tf_op jit(solution)/shard_map/all_to_all | solution.py:170
  216.5 2.2 fusion.31
  218.8 19.7 %all-to-all-done.5 = bf16[16,32,304]{2,1,0:T(8,128)(2,1)S(1)} async-done(((bf16[16,32,304]{2,1,0:T(8,128)(2,1)}), bf16[16,32,304]{2,1,0:T(8,128)(2,1)S(1)}, u32[]{:S(2)}, u32[]{:S(2)}) %all-to-all-start.5) | async-done | bytes 311328 | tf_op jit(solution)/shard_map/all_to_all | solution.py:170
  238.5 0.7 convert_reduce_fusion.2
  (71 shorter events, 5.6 us)
Async XLA Ops:
  2.7 9.2 %copy-start.12 = (bf16[3,256,38]{1,2,0:T(8,128)(2,1)S(1)}, bf16[3,256,38]{1,2,0:T(8,128)(2,1)}, u32[]{:S(2)}) copy-start(bf16[3,256,38]{1,2,0:T(8,128)(2,1)} %param.12) | copy-start | bytes 175108
  2.7 68.2 %all-to-all-start = ((bf16[8,256,304]{1,2,0:T(8,128)(2,1)}), bf16[8,256,304]{1,2,0:T(8,128)(2,1)S(1)}, u32[]{:S(2)}, u32[]{:S(2)}) async-start(bf16[8,256,304]{1,2,0:T(8,128)(2,1)} %broadcast_in_dim.23), calls=%async_computation | async-start | bytes 2490368 | tf_op jit(solution)/shard_map/all_to_all | solution.py:40
  50.3 7.5 %copy-start.10 = (f32[10,2,2432]{2,1,0:T(2,128)S(1)}, f32[10,2,2432]{2,1,0:T(2,128)}, u32[]{:S(2)}) copy-start(f32[10,2,2432]{2,1,0:T(2,128)} %param.11) | copy-start | bytes 583684
  50.5 18.5 %collective-permute-start = (bf16[608,768]{1,0:T(8,128)(2,1)S(1)}, bf16[608,768]{1,0:T(8,128)(2,1)S(1)}, u32[]{:S(2)}, u32[]{:S(2)}) collective-permute-start(bf16[608,768]{1,0:T(8,128)(2,1)S(1)} %reshape.207), channel_id=1, source_target_pairs={{0,128},{128,0},{1,129},{129,1},{2,130},{130,2},{3,131},{131,3},{4... | collective-permute-start | bytes 2801672 | tf_op jit(solution)/shard_map/ppermute | solution.py:75
  55.2 26.8 %collective-permute-start.1 = (bf16[608,768]{1,0:T(8,128)(2,1)S(1)}, bf16[608,768]{1,0:T(8,128)(2,1)}, u32[]{:S(2)}, u32[]{:S(2)}) collective-permute-start(bf16[608,768]{1,0:T(8,128)(2,1)S(1)} %reshape.207), channel_id=1, source_target_pairs={{0,256},{256,0},{1,257},{257,1},{2,258},{258,2},{3,259},{259,3},{4... | collective-permute-start | bytes 2801672 | tf_op jit(solution)/shard_map/ppermute | solution.py:76
  58.7 13.0 %copy-start.14 = (bf16[32,304]{1,0:T(8,128)(2,1)S(1)}, bf16[32,304]{1,0:T(8,128)(2,1)}, u32[]{:S(2)}) copy-start(bf16[32,304]{1,0:T(8,128)(2,1)} %param.13) | copy-start | bytes 58372
  69.0 12.4 %copy-start.2 = (bf16[608,768]{1,0:T(8,128)(2,1)}, bf16[608,768]{1,0:T(8,128)(2,1)S(1)}, u32[]{:S(2)}) copy-start(bf16[608,768]{1,0:T(8,128)(2,1)S(1)} %collective-permute-done) | copy-start | bytes 2801668
  69.0 14.6 %collective-permute-start.2 = (bf16[608,768]{1,0:T(8,128)(2,1)S(1)}, bf16[608,768]{1,0:T(8,128)(2,1)}, u32[]{:S(2)}, u32[]{:S(2)}) collective-permute-start(bf16[608,768]{1,0:T(8,128)(2,1)S(1)} %collective-permute-done), channel_id=1, source_target_pairs={{0,256},{256,0},{1,257},{257,1},{2,258},{258,2},{3,259},{259,3},{4... | collective-permute-start | bytes 2801672 | tf_op jit(solution)/shard_map/ppermute | solution.py:77
  72.5 32.4 %all-to-all-start.2 = ((bf16[16,32,304]{2,1,0:T(8,128)(2,1)}), bf16[16,32,304]{2,1,0:T(8,128)(2,1)S(1)}, u32[]{:S(2)}, u32[]{:S(2)}) async-start(bf16[16,32,304]{2,1,0:T(8,128)(2,1)} %broadcast_in_dim.26), calls=%async_computation.2 | async-start | bytes 786432 | tf_op jit(solution)/shard_map/all_to_all | solution.py:40
  104.9 14.4 %collective-permute-start.3 = (bf16[512,304]{1,0:T(8,128)(2,1)S(1)}, bf16[512,304]{1,0:T(8,128)(2,1)S(1)}, u32[]{:S(2)}, u32[]{:S(2)}) collective-permute-start(bf16[512,304]{1,0:T(8,128)(2,1)S(1)} %bitcast.171), channel_id=1, source_target_pairs={{0,128},{128,0},{1,129},{129,1},{2,130},{130,2},{3,131},{131,3},{4... | collective-permute-start | bytes 933896 | tf_op jit(solution)/shard_map/ppermute | solution.py:44
  111.5 17.3 %all-to-all-start.1 = ((bf16[8,256,256]{1,2,0:T(8,128)(2,1)}), bf16[8,256,256]{1,2,0:T(8,128)(2,1)S(1)}, u32[]{:S(2)}, u32[]{:S(2)}) async-start(bf16[8,256,256]{1,2,0:T(8,128)(2,1)} %broadcast_in_dim.25), calls=%async_computation.1 | async-start | bytes 2097152 | tf_op jit(solution)/shard_map/all_to_all | solution.py:40
  122.8 4.3 %collective-permute-start.4 = (bf16[1024,304]{0,1:T(8,128)(2,1)}, bf16[1024,304]{0,1:T(8,128)(2,1)}, u32[]{:S(2)}, u32[]{:S(2)}) collective-permute-start(bf16[1024,304]{0,1:T(8,128)(2,1)} %copy.65), channel_id=1, source_target_pairs={{0,256},{256,0},{1,257},{257,1},{2,258},{258,2},{3,259},{259,3},{4... | collective-permute-start | bytes 1867784 | tf_op jit(solution)/shard_map/ppermute | solution.py:44
  128.6 1.0 copy-start.8
  128.7 3.1 %copy-start.5 = (bf16[2,38,8,1024]{3,2,0,1:T(8,128)(2,1)}, bf16[2,38,8,1024]{3,2,0,1:T(8,128)(2,1)S(1)}, u32[]{:S(2)}) copy-start(bf16[2,38,8,1024]{3,2,0,1:T(8,128)(2,1)S(1)} %copy.80) | copy-start | bytes 3735556
  132.9 6.3 %copy-start.15 = (s32[64]{0:T(128)S(1)}, s32[64]{0:T(128)}, u32[]{:S(2)}) copy-start(s32[64]{0:T(128)} %param.15) | copy-start | bytes 772
  132.9 6.3 %copy-start.16 = (f32[64]{0:T(128)S(1)}, f32[64]{0:T(128)}, u32[]{:S(2)}) copy-start(f32[64]{0:T(128)} %param.14) | copy-start | bytes 772
  132.9 22.5 %all-to-all-start.3 = ((bf16[8,256,304]{1,2,0:T(8,128)(2,1)}), bf16[8,256,304]{1,2,0:T(8,128)(2,1)S(1)}, u32[]{:S(2)}, u32[]{:S(2)}) async-start(bf16[8,256,304]{1,2,0:T(8,128)(2,1)} %broadcast_in_dim.27), calls=%async_computation.3 | async-start | bytes 2490368 | tf_op jit(solution)/shard_map/all_to_all | solution.py:40
  155.3 0.7 copy-start.13
  157.5 1.2 copy-start.3
  165.1 5.7 %copy-start.18 = (f32[64]{0:T(128)S(1)}, f32[64]{0:T(128)}, u32[]{:S(2)}) copy-start(f32[64]{0:T(128)} %fusion.51) | copy-start | bytes 772
  165.1 5.8 %copy-start.17 = (f32[64]{0:T(128)S(1)}, f32[64]{0:T(128)}, u32[]{:S(2)}) copy-start(f32[64]{0:T(128)} %param.14) | copy-start | bytes 772
  165.1 6.0 %copy-start.19 = (f32[2,64]{1,0:T(2,128)S(1)}, f32[2,64]{1,0:T(2,128)}, u32[]{:S(2)}) copy-start(f32[2,64]{1,0:T(2,128)} %param.17) | copy-start | bytes 1540
  165.1 18.4 %all-to-all-start.4 = ((bf16[8,256,256]{1,2,0:T(8,128)(2,1)}), bf16[8,256,256]{1,2,0:T(8,128)(2,1)S(1)}, u32[]{:S(2)}, u32[]{:S(2)}) async-start(bf16[8,256,256]{1,2,0:T(8,128)(2,1)} %broadcast_in_dim.29), calls=%async_computation.4 | async-start | bytes 2097152 | tf_op jit(solution)/shard_map/all_to_all | solution.py:40
  176.0 8.9 %copy-start.7 = (bf16[1,256,2,1024]{3,1,0,2:T(8,128)(2,1)S(1)}, bf16[1,256,2,1024]{3,1,0,2:T(8,128)(2,1)}, u32[]{:S(2)}) copy-start(bf16[1,256,2,1024]{3,1,0,2:T(8,128)(2,1)} %copy.71) | copy-start | bytes 3145732
  176.0 8.9 %copy-start.11 = (bf16[1,256,304]{1,2,0:T(8,128)(2,1)S(1)}, bf16[1,256,304]{1,2,0:T(8,128)(2,1)}, u32[]{:S(2)}) copy-start(bf16[1,256,304]{1,2,0:T(8,128)(2,1)} %get-tuple-element.16) | copy-start | bytes 466948
  183.6 3.4 %copy-start = (bf16[8,256,256]{1,2,0:T(8,128)(2,1)}, bf16[8,256,256]{1,2,0:T(8,128)(2,1)S(1)}, u32[]{:S(2)}) copy-start(bf16[8,256,256]{1,2,0:T(8,128)(2,1)S(1)} %all-to-all-done.4) | copy-start | bytes 3145732
  186.9 1.4 copy-start.4
  188.4 3.9 %collective-permute-start.5 = (bf16[1024,304]{0,1:T(8,128)(2,1)S(1)}, bf16[1024,304]{0,1:T(8,128)(2,1)S(1)}, u32[]{:S(2)}, u32[]{:S(2)}) collective-permute-start(bf16[1024,304]{0,1:T(8,128)(2,1)S(1)} %fusion.24), channel_id=1, source_target_pairs={{0,256},{256,0},{1,257},{257,1},{2,258},{258,2},{3,259},{259,3},{4... | collective-permute-start | bytes 1867784 | tf_op jit(solution)/shard_map/ppermute | solution.py:53
  195.5 12.9 %collective-permute-start.6 = (bf16[512,304]{0,1:T(8,128)(2,1)S(1)}, bf16[512,304]{0,1:T(8,128)(2,1)}, u32[]{:S(2)}, u32[]{:S(2)}) collective-permute-start(bf16[512,304]{0,1:T(8,128)(2,1)S(1)} %bitcast.182), channel_id=1, source_target_pairs={{0,128},{128,0},{1,129},{129,1},{2,130},{130,2},{3,131},{131,3},{4... | collective-permute-start | bytes 933896 | tf_op jit(solution)/shard_map/ppermute | solution.py:53
  200.7 15.8 %copy-start.1 = (bf16[8,256,256]{1,2,0:T(8,128)(2,1)S(1)}, bf16[8,256,256]{1,2,0:T(8,128)(2,1)}, u32[]{:S(2)}) copy-start(bf16[8,256,256]{1,2,0:T(8,128)(2,1)} %copy-done) | copy-start | bytes 3145732
  200.7 15.8 %copy-start.6 = (bf16[2,38,8,1024]{3,2,0,1:T(8,128)(2,1)S(1)}, bf16[2,38,8,1024]{3,2,0,1:T(8,128)(2,1)}, u32[]{:S(2)}) copy-start(bf16[2,38,8,1024]{3,2,0,1:T(8,128)(2,1)} %copy-done.5) | copy-start | bytes 3735556
  200.7 15.8 %copy-start.9 = (f32[1,256,304]{1,2,0:T(8,128)S(1)}, f32[1,256,304]{1,2,0:T(8,128)}, u32[]{:S(2)}) copy-start(f32[1,256,304]{1,2,0:T(8,128)} %param.9) | copy-start | bytes 933892
  210.4 28.1 %all-to-all-start.5 = ((bf16[16,32,304]{2,1,0:T(8,128)(2,1)}), bf16[16,32,304]{2,1,0:T(8,128)(2,1)S(1)}, u32[]{:S(2)}, u32[]{:S(2)}) async-start(bf16[16,32,304]{2,1,0:T(8,128)(2,1)} %bitcast.45), calls=%async_computation.5 | async-start | bytes 786432 | tf_op jit(solution)/shard_map/all_to_all | solution.py:170

commit v10 on v9

--- a/solution.py
+++ b/solution.py
@@ -70,6 +70,9 @@
     units = qkv_weight.shape[0] * qkv_weight.shape[1]
     qkv_t = jnp.transpose(qkv_weight, (2, 0, 1)).reshape(qkv_weight.shape[2], units)
     qkv_t = lax.all_gather(qkv_t, "z", axis=0, tiled=True)
+    first_blocks = gather_all_to_all(latents[0].astype(jnp.bfloat16), FEATURE_AXES, seq_size)
+    first_blocks, out_weight, qkv_t = lax.optimization_barrier((first_blocks, out_weight, qkv_t))
+    out_z = gather_all_to_all(out_weight, "z", z_size)
     swap = [(0, 1), (1, 0)]
     me_g, me_x = lax.axis_index("grp"), lax.axis_index("xh")
     from_x = lax.ppermute(qkv_t, "xh", swap)
@@ -82,9 +85,7 @@
         (((1 - me_g) * 2 + me_x) * block_rows, from_g),
         (((1 - me_g) * 2 + 1 - me_x) * block_rows, from_gx),
     ]
-    first_blocks = gather_all_to_all(latents[0].astype(jnp.bfloat16), FEATURE_AXES, seq_size)
-    first_blocks, out_weight = lax.optimization_barrier((first_blocks, out_weight))
-    out_rows = gather_all_to_all(out_weight, "z", z_size).reshape(-1, out_weight.shape[1])
+    out_rows = out_z.reshape(-1, out_weight.shape[1])
     out_rows = gather_pair(out_rows, "xh").reshape(-1, out_weight.shape[1])
     out_rows = gather_pair(out_rows, "grp").reshape(-1, out_weight.shape[1])
 

time: 243 us -> 231 us (0.951)
  waiting for transfers between devices: 85.1 us -> 70.4 us
  matrix products: 17.8 us -> 21.4 us
    ppermute x1, waiting for transfers between devices: 10.3 us -> 3.99 us  [on_device(): from_x = lax.ppermute(qkv_t, 'xh', swap)]
    all_to_all x5, waiting for transfers between devices: 40.6 us -> 35.7 us  [gather_all_to_all(): return lax.all_to_all(spread, axis_name, 0, 0, tiled=True)]
    ppermute x2, waiting for transfers between devices: 4.79 us -> 1.2 us  [gather_pair(): other = lax.ppermute(x, axis_name, [(0, 1), (1, 0)])]
  transfers between devices with their start and end apart: 13 -> 13, of which waited for: 9 -> 9; matrix products, arithmetic and copies ran while one was open for 10% -> 12% of each run, Pallas kernels for 0% -> 0%
where the time goes in v10:
time: 231 us; the launch traced here: 227 us
  waiting for transfers between devices  70.4 us (30%)
  starting transfers between devices  59.4 us (26%)
  blocking collectives  37.9 us (16%)
  matrix products  21.4 us (9%)
  local copies, waits for them, and re-layouts  16.6 us (7%)
  other arithmetic  16.4 us (7%)
  between operations  5.35 us (2%)
    all_gather x1, blocking collectives, on_device(): qkv_t = lax.all_gather(qkv_t, 'z', axis=0, tiled=True)  37.9 us
    all_to_all x5, waiting for transfers between devices, gather_all_to_all(): return lax.all_to_all(spread, axis_name, 0, 0, tiled=True)  35.7 us
    all_to_all x5, starting transfers between devices, gather_all_to_all(): return lax.all_to_all(spread, axis_name, 0, 0, tiled=True)  33 us
    all_to_all x1, waiting for transfers between devices, on_device(): part = lax.all_to_all(part.astype(jnp.bfloat16), 'z', 0, 0, tiled=True)  19.7 us
    dot_general x8, matrix products, on_device(): term = jnp.dot(columns, block, preferred_element_type=jnp.float32)  11.2 us
    ppermute x2, waiting for transfers between devices, reduce_pair(): sent = lax.ppermute(send.astype(jnp.bfloat16), axis_name, [(0, 1), (1, 0)])  9.69 us
    ppermute x2, starting transfers between devices, reduce_pair(): sent = lax.ppermute(send.astype(jnp.bfloat16), axis_name, [(0, 1), (1, 0)])  6.56 us
    all_to_all x1, starting transfers between devices, on_device(): part = lax.all_to_all(part.astype(jnp.bfloat16), 'z', 0, 0, tiled=True)  6.55 us
  transfers between devices with their start and end apart: 13, of which 9 were waited for; matrix products, arithmetic and copies ran while one was open for 12% of the time, Pallas kernels for 0%

profile of v10, /device:TPU:24, one launch (start us, length us, event | category | flops | bytes accessed | tf_op | source)
XLA Modules:
  0.0 227.4 jit_solution(15590704170802283972)
XLA Ops:
  0.6 1.0 convert_bitcast_fusion
  1.6 1.1 broadcast_in_dim.23
  2.7 9.2 %all-to-all-start = ((bf16[8,256,304]{1,2,0:T(8,128)(2,1)}), bf16[8,256,304]{1,2,0:T(8,128)(2,1)S(1)}, u32[]{:S(2)}, u32[]{:S(2)}) async-start(bf16[8,256,304]{1,2,0:T(8,128)(2,1)} %broadcast_in_dim.23), calls=%async_computation | async-start | bytes 2490368 | tf_op jit(solution)/shard_map/all_to_all | solution.py:40
  12.8 37.9 %all-gather = bf16[16,38,768]{2,1,0:T(8,128)(2,1)S(1)} all-gather(bf16[1,38,768]{2,1,0:T(8,128)(2,1)S(1)} %reshape.206), channel_id=1, replica_groups=mesh['grp'=2,'xh'=2,'z'=16,'y'=4,'xl'=2] {'z'}, dimensions={0}, use_global_device_ids=true | all-gather | bytes 992256 | tf_op jit(solution)/shard_map/all_gather | solution.py:72
  51.0 0.8 multiply_reduce_fusion.2
  51.8 4.8 %collective-permute-start = (bf16[608,768]{1,0:T(8,128)(2,1)S(1)}, bf16[608,768]{1,0:T(8,128)(2,1)}, u32[]{:S(2)}, u32[]{:S(2)}) collective-permute-start(bf16[608,768]{1,0:T(8,128)(2,1)S(1)} %reshape.207), channel_id=1, source_target_pairs={{0,128},{128,0},{1,129},{129,1},{2,130},{130,2},{3,131},{131,3},{4... | collective-permute-start | bytes 2801672 | tf_op jit(solution)/shard_map/ppermute | solution.py:78
  56.7 1.9 collective-permute-start.1
  58.7 0.8 broadcast_in_dim.26
  59.4 6.4 %all-to-all-start.2 = ((bf16[16,32,304]{2,1,0:T(8,128)(2,1)}), bf16[16,32,304]{2,1,0:T(8,128)(2,1)}, u32[]{:S(2)}, u32[]{:S(2)}) async-start(bf16[16,32,304]{2,1,0:T(8,128)(2,1)} %broadcast_in_dim.26), calls=%async_computation.2 | async-start | bytes 786432 | tf_op jit(solution)/shard_map/all_to_all | solution.py:40
  66.6 4.0 %collective-permute-done = bf16[608,768]{1,0:T(8,128)(2,1)} collective-permute-done((bf16[608,768]{1,0:T(8,128)(2,1)S(1)}, bf16[608,768]{1,0:T(8,128)(2,1)}, u32[]{:S(2)}, u32[]{:S(2)}) %collective-permute-start) | collective-permute-done | bytes 933920 | tf_op jit(solution)/shard_map/ppermute | solution.py:78
  70.6 1.9 collective-permute-start.2
  72.5 1.4 fusion.9
  74.5 1.7 convolution_add_fusion.5
  76.2 1.7 convolution_add_fusion.4
  77.9 13.4 %all-to-all-done.2 = bf16[16,32,304]{2,1,0:T(8,128)(2,1)} async-done(((bf16[16,32,304]{2,1,0:T(8,128)(2,1)}), bf16[16,32,304]{2,1,0:T(8,128)(2,1)}, u32[]{:S(2)}, u32[]{:S(2)}) %all-to-all-start.2) | async-done | bytes 311328 | tf_op jit(solution)/shard_map/all_to_all | solution.py:40
  91.3 2.7 %collective-permute-start.3 = (bf16[512,304]{1,0:T(8,128)(2,1)}, bf16[512,304]{1,0:T(8,128)(2,1)}, u32[]{:S(2)}, u32[]{:S(2)}) collective-permute-start(bf16[512,304]{1,0:T(8,128)(2,1)} %bitcast.15), channel_id=1, source_target_pairs={{0,128},{128,0},{1,129},{129,1},{2,130},{130,2},{3,131},{131,3},{4... | collective-permute-start | bytes 933896 | tf_op jit(solution)/shard_map/ppermute | solution.py:44
  94.1 1.7 fusion.21
  96.3 0.5 fusion.72
  97.2 1.1 broadcast_in_dim.25
  98.2 5.9 %all-to-all-start.1 = ((bf16[8,256,256]{1,2,0:T(8,128)(2,1)}), bf16[8,256,256]{1,2,0:T(8,128)(2,1)S(1)}, u32[]{:S(2)}, u32[]{:S(2)}) async-start(bf16[8,256,256]{1,2,0:T(8,128)(2,1)} %broadcast_in_dim.25), calls=%async_computation.1 | async-start | bytes 2097152 | tf_op jit(solution)/shard_map/all_to_all | solution.py:40
  104.2 1.1 copy.62
  105.6 1.4 maximum_select_fusion.1
  106.9 1.1 copy.65
  108.0 1.9 collective-permute-start.4
  110.1 1.1 copy.66
  111.2 1.1 collective-permute-done.4
  112.3 1.9 fusion.23
  114.3 0.8 copy-done.4
  115.1 2.2 fusion.70
  117.3 1.1 broadcast_in_dim.27
  118.4 5.8 %all-to-all-start.3 = ((bf16[8,256,304]{1,2,0:T(8,128)(2,1)}), bf16[8,256,304]{1,2,0:T(8,128)(2,1)S(1)}, u32[]{:S(2)}, u32[]{:S(2)}) async-start(bf16[8,256,304]{1,2,0:T(8,128)(2,1)} %broadcast_in_dim.27), calls=%async_computation.3 | async-start | bytes 2490368 | tf_op jit(solution)/shard_map/all_to_all | solution.py:40
  124.2 0.7 fusion.51
  124.9 1.4 fusion.53
  126.4 14.0 %all-to-all-done.3 = bf16[8,256,304]{1,2,0:T(8,128)(2,1)S(1)} async-done(((bf16[8,256,304]{1,2,0:T(8,128)(2,1)}), bf16[8,256,304]{1,2,0:T(8,128)(2,1)S(1)}, u32[]{:S(2)}, u32[]{:S(2)}) %all-to-all-start.3) | async-done | bytes 1245216 | tf_op jit(solution)/shard_map/all_to_all | solution.py:40
  141.1 1.4 fusion.5
  142.5 0.5 fusion.42
  143.0 1.7 convolution_add_fusion.2
  144.7 1.7 convolution_add_fusion.1
  146.4 1.7 fusion.22
  148.6 0.5 fusion.73
  149.6 1.1 broadcast_in_dim.29
  150.6 5.7 %all-to-all-start.4 = ((bf16[8,256,256]{1,2,0:T(8,128)(2,1)}), bf16[8,256,256]{1,2,0:T(8,128)(2,1)S(1)}, u32[]{:S(2)}, u32[]{:S(2)}) async-start(bf16[8,256,256]{1,2,0:T(8,128)(2,1)} %broadcast_in_dim.29), calls=%async_computation.4 | async-start | bytes 2097152 | tf_op jit(solution)/shard_map/all_to_all | solution.py:40
  156.7 0.7 fusion.64
  157.3 0.6 fusion.71
  159.4 0.8 fusion.50
  160.2 0.5 copy.71
  160.8 8.3 %all-to-all-done.4 = bf16[8,256,256]{1,2,0:T(8,128)(2,1)S(1)} async-done(((bf16[8,256,256]{1,2,0:T(8,128)(2,1)}), bf16[8,256,256]{1,2,0:T(8,128)(2,1)S(1)}, u32[]{:S(2)}, u32[]{:S(2)}) %all-to-all-start.4) | async-done | bytes 1048608 | tf_op jit(solution)/shard_map/all_to_all | solution.py:40
  169.1 0.5 copy.72
  169.6 3.3 %fusion.14 = f32[2,1024,304]{1,2,0:T(8,128)} fusion(bf16[1,256,2,1024]{3,1,0,2:T(8,128)(2,1)S(1)} %copy.72, bf16[1,256,2,1024]{3,1,0,2:T(8,128)(2,1)S(1)} %copy.71, bf16[1,256,304]{1,2,0:T(8,128)(2,1)} %get-tuple-element.18, bf16[1,256,304]{1,2,0:T(8,128)(2,1)} %get-tuple-element.17), kind=kOutput, calls=%fused_computation.18 | convolution fusion | flops 642351104 | bytes 4898816 | tf_op jit(solution)/shard_map/dot_general | solution.py:164
  172.9 1.4 fusion.24
  174.3 1.9 collective-permute-start.5
  176.2 2.0 collective-permute-done.5
  178.2 1.5 bitcast_add_fusion
  179.7 1.1 reshape.203
  180.8 0.6 constant_dynamic-slice_fusion
  181.4 4.6 %collective-permute-start.6 = (bf16[512,304]{0,1:T(8,128)(2,1)S(1)}, bf16[512,304]{0,1:T(8,128)(2,1)}, u32[]{:S(2)}, u32[]{:S(2)}) collective-permute-start(bf16[512,304]{0,1:T(8,128)(2,1)S(1)} %bitcast.180), channel_id=1, source_target_pairs={{0,128},{128,0},{1,129},{129,1},{2,130},{130,2},{3,131},{131,3},{4... | collective-permute-start | bytes 933896 | tf_op jit(solution)/shard_map/ppermute | solution.py:53
  186.1 0.5 constant_dynamic-slice_fusion.1
  186.6 7.7 %collective-permute-done.6 = bf16[512,304]{0,1:T(8,128)(2,1)} collective-permute-done((bf16[512,304]{0,1:T(8,128)(2,1)S(1)}, bf16[512,304]{0,1:T(8,128)(2,1)}, u32[]{:S(2)}, u32[]{:S(2)}) %collective-permute-start.6) | collective-permute-done | bytes 311328 | tf_op jit(solution)/shard_map/ppermute | solution.py:53
  194.3 1.1 fusion.25
  195.4 0.9 copy.74
  196.3 6.5 %all-to-all-start.5 = ((bf16[16,32,304]{2,1,0:T(8,128)(2,1)}), bf16[16,32,304]{2,1,0:T(8,128)(2,1)S(1)}, u32[]{:S(2)}, u32[]{:S(2)}) async-start(bf16[16,32,304]{2,1,0:T(8,128)(2,1)} %bitcast.45), calls=%async_computation.5 | async-start | bytes 786432 | tf_op jit(solution)/shard_map/all_to_all | solution.py:171
  203.6 2.2 fusion.31
  205.8 19.7 %all-to-all-done.5 = bf16[16,32,304]{2,1,0:T(8,128)(2,1)S(1)} async-done(((bf16[16,32,304]{2,1,0:T(8,128)(2,1)}), bf16[16,32,304]{2,1,0:T(8,128)(2,1)S(1)}, u32[]{:S(2)}, u32[]{:S(2)}) %all-to-all-start.5) | async-done | bytes 311328 | tf_op jit(solution)/shard_map/all_to_all | solution.py:171
  225.6 0.7 convert_reduce_fusion.2
  (61 shorter events, 4.9 us)
Async XLA Ops:
  2.7 9.9 %copy-start.7 = (bf16[3,256,38]{1,2,0:T(8,128)(2,1)S(1)}, bf16[3,256,38]{1,2,0:T(8,128)(2,1)}, u32[]{:S(2)}) copy-start(bf16[3,256,38]{1,2,0:T(8,128)(2,1)} %param.12) | copy-start | bytes 175108
  2.7 49.1 %all-to-all-start = ((bf16[8,256,304]{1,2,0:T(8,128)(2,1)}), bf16[8,256,304]{1,2,0:T(8,128)(2,1)S(1)}, u32[]{:S(2)}, u32[]{:S(2)}) async-start(bf16[8,256,304]{1,2,0:T(8,128)(2,1)} %broadcast_in_dim.23), calls=%async_computation | async-start | bytes 2490368 | tf_op jit(solution)/shard_map/all_to_all | solution.py:40
  12.7 38.2 %copy-start.6 = (f32[10,2,2432]{2,1,0:T(2,128)S(1)}, f32[10,2,2432]{2,1,0:T(2,128)}, u32[]{:S(2)}) copy-start(f32[10,2,2432]{2,1,0:T(2,128)} %param.11) | copy-start | bytes 583684
  50.7 8.0 %copy-start.9 = (bf16[32,304]{1,0:T(8,128)(2,1)S(1)}, bf16[32,304]{1,0:T(8,128)(2,1)}, u32[]{:S(2)}) copy-start(bf16[32,304]{1,0:T(8,128)(2,1)} %param.13) | copy-start | bytes 58372
  51.8 18.8 %collective-permute-start = (bf16[608,768]{1,0:T(8,128)(2,1)S(1)}, bf16[608,768]{1,0:T(8,128)(2,1)}, u32[]{:S(2)}, u32[]{:S(2)}) collective-permute-start(bf16[608,768]{1,0:T(8,128)(2,1)S(1)} %reshape.207), channel_id=1, source_target_pairs={{0,128},{128,0},{1,129},{129,1},{2,130},{130,2},{3,131},{131,3},{4... | collective-permute-start | bytes 2801672 | tf_op jit(solution)/shard_map/ppermute | solution.py:78
  56.7 19.5 %collective-permute-start.1 = (bf16[608,768]{1,0:T(8,128)(2,1)S(1)}, bf16[608,768]{1,0:T(8,128)(2,1)}, u32[]{:S(2)}, u32[]{:S(2)}) collective-permute-start(bf16[608,768]{1,0:T(8,128)(2,1)S(1)} %reshape.207), channel_id=1, source_target_pairs={{0,256},{256,0},{1,257},{257,1},{2,258},{258,2},{3,259},{259,3},{4... | collective-permute-start | bytes 2801672 | tf_op jit(solution)/shard_map/ppermute | solution.py:79
  59.4 31.9 %all-to-all-start.2 = ((bf16[16,32,304]{2,1,0:T(8,128)(2,1)}), bf16[16,32,304]{2,1,0:T(8,128)(2,1)}, u32[]{:S(2)}, u32[]{:S(2)}) async-start(bf16[16,32,304]{2,1,0:T(8,128)(2,1)} %broadcast_in_dim.26), calls=%async_computation.2 | async-start | bytes 786432 | tf_op jit(solution)/shard_map/all_to_all | solution.py:40
  70.6 23.4 %collective-permute-start.2 = (bf16[608,768]{1,0:T(8,128)(2,1)}, bf16[608,768]{1,0:T(8,128)(2,1)}, u32[]{:S(2)}, u32[]{:S(2)}) collective-permute-start(bf16[608,768]{1,0:T(8,128)(2,1)} %collective-permute-done), channel_id=1, source_target_pairs={{0,256},{256,0},{1,257},{257,1},{2,258},{258,2},{3,259},{259,3},{4... | collective-permute-start | bytes 2801672 | tf_op jit(solution)/shard_map/ppermute | solution.py:80
  91.3 12.9 %collective-permute-start.3 = (bf16[512,304]{1,0:T(8,128)(2,1)}, bf16[512,304]{1,0:T(8,128)(2,1)}, u32[]{:S(2)}, u32[]{:S(2)}) collective-permute-start(bf16[512,304]{1,0:T(8,128)(2,1)} %bitcast.15), channel_id=1, source_target_pairs={{0,128},{128,0},{1,129},{129,1},{2,130},{130,2},{3,131},{131,3},{4... | collective-permute-start | bytes 933896 | tf_op jit(solution)/shard_map/ppermute | solution.py:44
  98.2 16.0 %all-to-all-start.1 = ((bf16[8,256,256]{1,2,0:T(8,128)(2,1)}), bf16[8,256,256]{1,2,0:T(8,128)(2,1)S(1)}, u32[]{:S(2)}, u32[]{:S(2)}) async-start(bf16[8,256,256]{1,2,0:T(8,128)(2,1)} %broadcast_in_dim.25), calls=%async_computation.1 | async-start | bytes 2097152 | tf_op jit(solution)/shard_map/all_to_all | solution.py:40
  108.0 4.3 %collective-permute-start.4 = (bf16[1024,304]{0,1:T(8,128)(2,1)}, bf16[1024,304]{0,1:T(8,128)(2,1)}, u32[]{:S(2)}, u32[]{:S(2)}) collective-permute-start(bf16[1024,304]{0,1:T(8,128)(2,1)} %copy.65), channel_id=1, source_target_pairs={{0,256},{256,0},{1,257},{257,1},{2,258},{258,2},{3,259},{259,3},{4... | collective-permute-start | bytes 1867784 | tf_op jit(solution)/shard_map/ppermute | solution.py:44
  114.2 1.0 copy-start.4
  114.3 3.1 %copy-start.2 = (bf16[2,38,8,1024]{3,2,0,1:T(8,128)(2,1)}, bf16[2,38,8,1024]{3,2,0,1:T(8,128)(2,1)S(1)}, u32[]{:S(2)}) copy-start(bf16[2,38,8,1024]{3,2,0,1:T(8,128)(2,1)S(1)} %copy.80) | copy-start | bytes 3735556
  118.4 5.8 %copy-start.10 = (s32[64]{0:T(128)S(1)}, s32[64]{0:T(128)}, u32[]{:S(2)}) copy-start(s32[64]{0:T(128)} %param.15) | copy-start | bytes 772
  118.4 5.8 %copy-start.11 = (f32[64]{0:T(128)S(1)}, f32[64]{0:T(128)}, u32[]{:S(2)}) copy-start(f32[64]{0:T(128)} %param.14) | copy-start | bytes 772
  118.4 21.9 %all-to-all-start.3 = ((bf16[8,256,304]{1,2,0:T(8,128)(2,1)}), bf16[8,256,304]{1,2,0:T(8,128)(2,1)S(1)}, u32[]{:S(2)}, u32[]{:S(2)}) async-start(bf16[8,256,304]{1,2,0:T(8,128)(2,1)} %broadcast_in_dim.27), calls=%async_computation.3 | async-start | bytes 2490368 | tf_op jit(solution)/shard_map/all_to_all | solution.py:40
  140.3 0.7 copy-start.8
  150.6 5.7 %copy-start.13 = (f32[64]{0:T(128)S(1)}, f32[64]{0:T(128)}, u32[]{:S(2)}) copy-start(f32[64]{0:T(128)} %fusion.51) | copy-start | bytes 772
  150.6 5.8 %copy-start.12 = (f32[64]{0:T(128)S(1)}, f32[64]{0:T(128)}, u32[]{:S(2)}) copy-start(f32[64]{0:T(128)} %param.14) | copy-start | bytes 772
  150.6 6.0 %copy-start.14 = (f32[2,64]{1,0:T(2,128)S(1)}, f32[2,64]{1,0:T(2,128)}, u32[]{:S(2)}) copy-start(f32[2,64]{1,0:T(2,128)} %param.17) | copy-start | bytes 1540
  150.6 18.4 %all-to-all-start.4 = ((bf16[8,256,256]{1,2,0:T(8,128)(2,1)}), bf16[8,256,256]{1,2,0:T(8,128)(2,1)S(1)}, u32[]{:S(2)}, u32[]{:S(2)}) async-start(bf16[8,256,256]{1,2,0:T(8,128)(2,1)} %broadcast_in_dim.29), calls=%async_computation.4 | async-start | bytes 2097152 | tf_op jit(solution)/shard_map/all_to_all | solution.py:40
  169.1 3.8 %copy-start = (bf16[8,256,256]{1,2,0:T(8,128)(2,1)}, bf16[8,256,256]{1,2,0:T(8,128)(2,1)S(1)}, u32[]{:S(2)}) copy-start(bf16[8,256,256]{1,2,0:T(8,128)(2,1)S(1)} %all-to-all-done.4) | copy-start | bytes 3145732
  174.3 3.9 %collective-permute-start.5 = (bf16[1024,304]{0,1:T(8,128)(2,1)S(1)}, bf16[1024,304]{0,1:T(8,128)(2,1)S(1)}, u32[]{:S(2)}, u32[]{:S(2)}) collective-permute-start(bf16[1024,304]{0,1:T(8,128)(2,1)S(1)} %fusion.24), channel_id=1, source_target_pairs={{0,256},{256,0},{1,257},{257,1},{2,258},{258,2},{3,259},{259,3},{4... | collective-permute-start | bytes 1867784 | tf_op jit(solution)/shard_map/ppermute | solution.py:53
  181.4 12.9 %collective-permute-start.6 = (bf16[512,304]{0,1:T(8,128)(2,1)S(1)}, bf16[512,304]{0,1:T(8,128)(2,1)}, u32[]{:S(2)}, u32[]{:S(2)}) collective-permute-start(bf16[512,304]{0,1:T(8,128)(2,1)S(1)} %bitcast.180), channel_id=1, source_target_pairs={{0,128},{128,0},{1,129},{129,1},{2,130},{130,2},{3,131},{131,3},{4... | collective-permute-start | bytes 933896 | tf_op jit(solution)/shard_map/ppermute | solution.py:53
  186.6 17.0 %copy-start.1 = (bf16[8,256,256]{1,2,0:T(8,128)(2,1)S(1)}, bf16[8,256,256]{1,2,0:T(8,128)(2,1)}, u32[]{:S(2)}) copy-start(bf16[8,256,256]{1,2,0:T(8,128)(2,1)} %copy-done) | copy-start | bytes 3145732
  186.6 17.0 %copy-start.3 = (bf16[2,38,8,1024]{3,2,0,1:T(8,128)(2,1)S(1)}, bf16[2,38,8,1024]{3,2,0,1:T(8,128)(2,1)}, u32[]{:S(2)}) copy-start(bf16[2,38,8,1024]{3,2,0,1:T(8,128)(2,1)} %copy-done.2) | copy-start | bytes 3735556
  186.6 17.0 %copy-start.5 = (f32[1,256,304]{1,2,0:T(8,128)S(1)}, f32[1,256,304]{1,2,0:T(8,128)}, u32[]{:S(2)}) copy-start(f32[1,256,304]{1,2,0:T(8,128)} %param.9) | copy-start | bytes 933892
  196.3 29.3 %all-to-all-start.5 = ((bf16[16,32,304]{2,1,0:T(8,128)(2,1)}), bf16[16,32,304]{2,1,0:T(8,128)(2,1)S(1)}, u32[]{:S(2)}, u32[]{:S(2)}) async-start(bf16[16,32,304]{2,1,0:T(8,128)(2,1)} %bitcast.45), calls=%async_computation.5 | async-start | bytes 786432 | tf_op jit(solution)/shard_map/all_to_all | solution.py:171

commit v11 on v10

--- a/solution.py
+++ b/solution.py
@@ -85,9 +85,6 @@
         (((1 - me_g) * 2 + me_x) * block_rows, from_g),
         (((1 - me_g) * 2 + 1 - me_x) * block_rows, from_gx),
     ]
-    out_rows = out_z.reshape(-1, out_weight.shape[1])
-    out_rows = gather_pair(out_rows, "xh").reshape(-1, out_weight.shape[1])
-    out_rows = gather_pair(out_rows, "grp").reshape(-1, out_weight.shape[1])
 
     group_width = qkv_weight.shape[1]
     heads_here = group_width // HD
@@ -140,6 +137,11 @@
             "hqk,khe->qhe", probs, value_rows, preferred_element_type=jnp.float32
         ).astype(jnp.bfloat16)
         attn = attn_blocks.reshape(seq_len, group_width)
+        if section == 0:
+            out_z, attn = lax.optimization_barrier((out_z, attn))
+            out_rows = out_z.reshape(-1, out_weight.shape[1])
+            out_rows = gather_pair(out_rows, "xh").reshape(-1, out_weight.shape[1])
+            out_rows = gather_pair(out_rows, "grp").reshape(-1, out_weight.shape[1])
         attn_parts = gather_all_to_all(attn, FEATURE_AXES, seq_size)
         attn_all = jnp.transpose(attn_parts, (1, 0, 2)).reshape(seq_len, -1)
         velocity = jnp.dot(attn_all, out_rows, preferred_element_type=jnp.float32)

time: 231 us -> 228 us (0.987)
  matrix products: 21.4 us -> 15.3 us
  waiting for transfers between devices: 70.4 us -> 76.2 us
  starting transfers between devices: 59.4 us -> 56.9 us
    ppermute x2, waiting for transfers between devices: 1.2 us -> 7.8 us  [gather_pair(): other = lax.ppermute(x, axis_name, [(0, 1), (1, 0)])]
    dot_general x8, matrix products: 11.2 us -> 6.54 us  [on_device(): term = jnp.dot(columns, block, preferred_element_type=jnp.float32)]
    unnamed x32 -> x42, local copies, waits for them, and re-layouts: 1.03 us -> 4.7 us
  transfers between devices with their start and end apart: 13 -> 13, of which waited for: 9 -> 9; matrix products, arithmetic and copies ran while one was open for 12% -> 10% of each run, Pallas kernels for 0% -> 0%
where the time goes in v11:
time: 228 us; the launch traced here: 225 us
  waiting for transfers between devices  76.2 us (33%)
  starting transfers between devices  56.9 us (25%)
  blocking collectives  37.9 us (17%)
  local copies, waits for them, and re-layouts  17.1 us (8%)
  other arithmetic  16 us (7%)
  matrix products  15.3 us (7%)
  between operations  5.41 us (2%)
    all_gather x1, blocking collectives, on_device(): qkv_t = lax.all_gather(qkv_t, 'z', axis=0, tiled=True)  37.9 us
    all_to_all x5, waiting for transfers between devices, gather_all_to_all(): return lax.all_to_all(spread, axis_name, 0, 0, tiled=True)  34.1 us
    all_to_all x5, starting transfers between devices, gather_all_to_all(): return lax.all_to_all(spread, axis_name, 0, 0, tiled=True)  32.7 us
    all_to_all x1, waiting for transfers between devices, on_device(): part = lax.all_to_all(part.astype(jnp.bfloat16), 'z', 0, 0, tiled=True)  19.7 us
    ppermute x2, waiting for transfers between devices, reduce_pair(): sent = lax.ppermute(send.astype(jnp.bfloat16), axis_name, [(0, 1), (1, 0)])  10.6 us
    ppermute x2, waiting for transfers between devices, gather_pair(): other = lax.ppermute(x, axis_name, [(0, 1), (1, 0)])  7.8 us
    dot_general x8, matrix products, on_device(): term = jnp.dot(columns, block, preferred_element_type=jnp.float32)  6.54 us
    ppermute x2, starting transfers between devices, reduce_pair(): sent = lax.ppermute(send.astype(jnp.bfloat16), axis_name, [(0, 1), (1, 0)])  5.81 us
  transfers between devices with their start and end apart: 13, of which 9 were waited for; matrix products, arithmetic and copies ran while one was open for 10% of the time, Pallas kernels for 0%

profile of v11, /device:TPU:24, one launch (start us, length us, event | category | flops | bytes accessed | tf_op | source)
XLA Modules:
  0.0 224.8 jit_solution(3984821756734760131)
XLA Ops:
  0.6 1.0 convert_bitcast_fusion
  1.6 1.1 broadcast_in_dim.21
  2.7 9.2 %all-to-all-start = ((bf16[8,256,304]{1,2,0:T(8,128)(2,1)}), bf16[8,256,304]{1,2,0:T(8,128)(2,1)S(1)}, u32[]{:S(2)}, u32[]{:S(2)}) async-start(bf16[8,256,304]{1,2,0:T(8,128)(2,1)} %broadcast_in_dim.21), calls=%async_computation | async-start | bytes 2490368 | tf_op jit(solution)/shard_map/all_to_all | solution.py:40
  12.8 37.9 %all-gather = bf16[16,38,768]{2,1,0:T(8,128)(2,1)S(1)} all-gather(bf16[1,38,768]{2,1,0:T(8,128)(2,1)S(1)} %reshape.210), channel_id=1, replica_groups=mesh['grp'=2,'xh'=2,'z'=16,'y'=4,'xl'=2] {'z'}, dimensions={0}, use_global_device_ids=true | all-gather | bytes 992256 | tf_op jit(solution)/shard_map/all_gather | solution.py:72
  51.0 0.8 multiply_reduce_fusion.2
  51.8 4.8 %collective-permute-start = (bf16[608,768]{1,0:T(8,128)(2,1)S(1)}, bf16[608,768]{1,0:T(8,128)(2,1)S(1)}, u32[]{:S(2)}, u32[]{:S(2)}) collective-permute-start(bf16[608,768]{1,0:T(8,128)(2,1)S(1)} %reshape.211), channel_id=1, source_target_pairs={{0,128},{128,0},{1,129},{129,1},{2,130},{130,2},{3,131},{131,3},{4... | collective-permute-start | bytes 2801672 | tf_op jit(solution)/shard_map/ppermute | solution.py:78
  56.7 1.9 collective-permute-start.1
  58.7 0.8 broadcast_in_dim.22
  59.4 6.4 %all-to-all-start.1 = ((bf16[16,32,304]{2,1,0:T(8,128)(2,1)}), bf16[16,32,304]{2,1,0:T(8,128)(2,1)}, u32[]{:S(2)}, u32[]{:S(2)}) async-start(bf16[16,32,304]{2,1,0:T(8,128)(2,1)} %broadcast_in_dim.22), calls=%async_computation.1 | async-start | bytes 786432 | tf_op jit(solution)/shard_map/all_to_all | solution.py:40
  66.6 3.9 %collective-permute-done = bf16[608,768]{1,0:T(8,128)(2,1)S(1)} collective-permute-done((bf16[608,768]{1,0:T(8,128)(2,1)S(1)}, bf16[608,768]{1,0:T(8,128)(2,1)S(1)}, u32[]{:S(2)}, u32[]{:S(2)}) %collective-permute-start) | collective-permute-done | bytes 933920 | tf_op jit(solution)/shard_map/ppermute | solution.py:78
  70.5 1.9 collective-permute-start.2
  72.4 1.4 fusion.9
  73.8 0.5 fusion.47
  74.4 0.5 convolution_add_fusion.5
  74.9 1.7 convolution_add_fusion.4
  76.6 0.9 copy-done.4
  78.3 0.5 fusion.72
  79.5 11.8 %all-to-all-done.1 = bf16[16,32,304]{2,1,0:T(8,128)(2,1)} async-done(((bf16[16,32,304]{2,1,0:T(8,128)(2,1)}), bf16[16,32,304]{2,1,0:T(8,128)(2,1)}, u32[]{:S(2)}, u32[]{:S(2)}) %all-to-all-start.1) | async-done | bytes 311328 | tf_op jit(solution)/shard_map/all_to_all | solution.py:40
  91.3 2.7 %collective-permute-start.3 = (bf16[512,304]{1,0:T(8,128)(2,1)}, bf16[512,304]{1,0:T(8,128)(2,1)S(1)}, u32[]{:S(2)}, u32[]{:S(2)}) collective-permute-start(bf16[512,304]{1,0:T(8,128)(2,1)} %bitcast.15), channel_id=1, source_target_pairs={{0,128},{128,0},{1,129},{129,1},{2,130},{130,2},{3,131},{131,3},{4... | collective-permute-start | bytes 933896 | tf_op jit(solution)/shard_map/ppermute | solution.py:44
  94.0 1.0 broadcast_in_dim.23
  95.1 5.9 %all-to-all-start.2 = ((bf16[8,256,256]{1,2,0:T(8,128)(2,1)}), bf16[8,256,256]{1,2,0:T(8,128)(2,1)S(1)}, u32[]{:S(2)}, u32[]{:S(2)}) async-start(bf16[8,256,256]{1,2,0:T(8,128)(2,1)} %broadcast_in_dim.23), calls=%async_computation.2 | async-start | bytes 2097152 | tf_op jit(solution)/shard_map/all_to_all | solution.py:40
  101.0 5.9 %collective-permute-done.3 = bf16[512,304]{1,0:T(8,128)(2,1)S(1)} collective-permute-done((bf16[512,304]{1,0:T(8,128)(2,1)}, bf16[512,304]{1,0:T(8,128)(2,1)S(1)}, u32[]{:S(2)}, u32[]{:S(2)}) %collective-permute-start.3) | collective-permute-done | bytes 311328 | tf_op jit(solution)/shard_map/ppermute | solution.py:44
  107.2 1.4 maximum_select_fusion.1
  108.6 1.1 copy.65
  109.7 1.9 collective-permute-start.4
  112.0 1.9 collective-permute-done.4
  113.9 1.5 fusion.23
  115.6 0.8 copy-done.9
  116.4 2.2 fusion.70
  118.6 1.1 broadcast_in_dim.24
  119.7 5.4 %all-to-all-start.3 = ((bf16[8,256,304]{1,2,0:T(8,128)(2,1)}), bf16[8,256,304]{1,2,0:T(8,128)(2,1)S(1)}, u32[]{:S(2)}, u32[]{:S(2)}) async-start(bf16[8,256,304]{1,2,0:T(8,128)(2,1)} %broadcast_in_dim.24), calls=%async_computation.3 | async-start | bytes 2490368 | tf_op jit(solution)/shard_map/all_to_all | solution.py:40
  125.2 0.7 fusion.51
  125.9 1.4 fusion.53
  127.3 14.0 %all-to-all-done.3 = bf16[8,256,304]{1,2,0:T(8,128)(2,1)S(1)} async-done(((bf16[8,256,304]{1,2,0:T(8,128)(2,1)}), bf16[8,256,304]{1,2,0:T(8,128)(2,1)S(1)}, u32[]{:S(2)}, u32[]{:S(2)}) %all-to-all-start.3) | async-done | bytes 1245216 | tf_op jit(solution)/shard_map/all_to_all | solution.py:40
  142.0 1.4 fusion.5
  144.0 0.7 copy-done.3
  145.2 1.8 convolution_add_fusion.1
  146.9 0.5 fusion.22
  148.0 0.5 fusion.73
  148.9 1.1 broadcast_in_dim.26
  150.0 5.7 %all-to-all-start.4 = ((bf16[8,256,256]{1,2,0:T(8,128)(2,1)}), bf16[8,256,256]{1,2,0:T(8,128)(2,1)S(1)}, u32[]{:S(2)}, u32[]{:S(2)}) async-start(bf16[8,256,256]{1,2,0:T(8,128)(2,1)} %broadcast_in_dim.26), calls=%async_computation.4 | async-start | bytes 2097152 | tf_op jit(solution)/shard_map/all_to_all | solution.py:40
  156.0 0.7 fusion.64
  156.7 0.6 fusion.71
  158.8 0.8 fusion.50
  159.6 0.5 copy.71
  160.1 8.3 %all-to-all-done.4 = bf16[8,256,256]{1,2,0:T(8,128)(2,1)S(1)} async-done(((bf16[8,256,256]{1,2,0:T(8,128)(2,1)}), bf16[8,256,256]{1,2,0:T(8,128)(2,1)S(1)}, u32[]{:S(2)}, u32[]{:S(2)}) %all-to-all-start.4) | async-done | bytes 1048608 | tf_op jit(solution)/shard_map/all_to_all | solution.py:40
  168.4 0.5 copy.72
  169.0 1.8 fusion.14
  170.9 1.3 copy-done.6
  172.2 1.9 collective-permute-start.5
  174.1 2.0 collective-permute-done.5
  176.2 1.4 bitcast_add_fusion
  177.6 1.1 reshape.207
  178.7 0.6 constant_dynamic-slice_fusion
  179.2 0.8 copy.85
  180.0 3.9 %collective-permute-start.6 = (bf16[512,304]{0,1:T(8,128)(2,1)}, bf16[512,304]{0,1:T(8,128)(2,1)}, u32[]{:S(2)}, u32[]{:S(2)}) collective-permute-start(bf16[512,304]{0,1:T(8,128)(2,1)} %bitcast.161), channel_id=1, source_target_pairs={{0,128},{128,0},{1,129},{129,1},{2,130},{130,2},{3,131},{131,3},{4... | collective-permute-start | bytes 933896 | tf_op jit(solution)/shard_map/ppermute | solution.py:53
  183.9 0.5 constant_dynamic-slice_fusion.1
  184.5 8.6 %collective-permute-done.6 = bf16[512,304]{0,1:T(8,128)(2,1)} collective-permute-done((bf16[512,304]{0,1:T(8,128)(2,1)}, bf16[512,304]{0,1:T(8,128)(2,1)}, u32[]{:S(2)}, u32[]{:S(2)}) %collective-permute-start.6) | collective-permute-done | bytes 311328 | tf_op jit(solution)/shard_map/ppermute | solution.py:53
  193.1 1.1 fusion.25
  194.2 0.9 copy.74
  195.1 5.1 %all-to-all-start.5 = ((bf16[16,32,304]{2,1,0:T(8,128)(2,1)}), bf16[16,32,304]{2,1,0:T(8,128)(2,1)S(1)}, u32[]{:S(2)}, u32[]{:S(2)}) async-start(bf16[16,32,304]{2,1,0:T(8,128)(2,1)} %bitcast.45), calls=%async_computation.5 | async-start | bytes 786432 | tf_op jit(solution)/shard_map/all_to_all | solution.py:173
  201.0 2.2 fusion.31
  203.2 19.7 %all-to-all-done.5 = bf16[16,32,304]{2,1,0:T(8,128)(2,1)S(1)} async-done(((bf16[16,32,304]{2,1,0:T(8,128)(2,1)}), bf16[16,32,304]{2,1,0:T(8,128)(2,1)S(1)}, u32[]{:S(2)}, u32[]{:S(2)}) %all-to-all-start.5) | async-done | bytes 311328 | tf_op jit(solution)/shard_map/all_to_all | solution.py:173
  223.0 0.7 convert_reduce_fusion.2
  (71 shorter events, 6.3 us)
Async XLA Ops:
  2.7 9.9 %copy-start.12 = (bf16[3,256,38]{1,2,0:T(8,128)(2,1)S(1)}, bf16[3,256,38]{1,2,0:T(8,128)(2,1)}, u32[]{:S(2)}) copy-start(bf16[3,256,38]{1,2,0:T(8,128)(2,1)} %param.12) | copy-start | bytes 175108
  2.7 49.1 %all-to-all-start = ((bf16[8,256,304]{1,2,0:T(8,128)(2,1)}), bf16[8,256,304]{1,2,0:T(8,128)(2,1)S(1)}, u32[]{:S(2)}, u32[]{:S(2)}) async-start(bf16[8,256,304]{1,2,0:T(8,128)(2,1)} %broadcast_in_dim.21), calls=%async_computation | async-start | bytes 2490368 | tf_op jit(solution)/shard_map/all_to_all | solution.py:40
  12.7 38.2 %copy-start.11 = (f32[10,2,2432]{2,1,0:T(2,128)S(1)}, f32[10,2,2432]{2,1,0:T(2,128)}, u32[]{:S(2)}) copy-start(f32[10,2,2432]{2,1,0:T(2,128)} %param.11) | copy-start | bytes 583684
  50.7 8.0 %copy-start.14 = (bf16[32,304]{1,0:T(8,128)(2,1)S(1)}, bf16[32,304]{1,0:T(8,128)(2,1)}, u32[]{:S(2)}) copy-start(bf16[32,304]{1,0:T(8,128)(2,1)} %param.13) | copy-start | bytes 58372
  51.8 18.7 %collective-permute-start = (bf16[608,768]{1,0:T(8,128)(2,1)S(1)}, bf16[608,768]{1,0:T(8,128)(2,1)S(1)}, u32[]{:S(2)}, u32[]{:S(2)}) collective-permute-start(bf16[608,768]{1,0:T(8,128)(2,1)S(1)} %reshape.211), channel_id=1, source_target_pairs={{0,128},{128,0},{1,129},{129,1},{2,130},{130,2},{3,131},{131,3},{4... | collective-permute-start | bytes 2801672 | tf_op jit(solution)/shard_map/ppermute | solution.py:78
  56.7 18.2 %collective-permute-start.1 = (bf16[608,768]{1,0:T(8,128)(2,1)S(1)}, bf16[608,768]{1,0:T(8,128)(2,1)}, u32[]{:S(2)}, u32[]{:S(2)}) collective-permute-start(bf16[608,768]{1,0:T(8,128)(2,1)S(1)} %reshape.211), channel_id=1, source_target_pairs={{0,256},{256,0},{1,257},{257,1},{2,258},{258,2},{3,259},{259,3},{4... | collective-permute-start | bytes 2801672 | tf_op jit(solution)/shard_map/ppermute | solution.py:79
  59.4 31.9 %all-to-all-start.1 = ((bf16[16,32,304]{2,1,0:T(8,128)(2,1)}), bf16[16,32,304]{2,1,0:T(8,128)(2,1)}, u32[]{:S(2)}, u32[]{:S(2)}) async-start(bf16[16,32,304]{2,1,0:T(8,128)(2,1)} %broadcast_in_dim.22), calls=%async_computation.1 | async-start | bytes 786432 | tf_op jit(solution)/shard_map/all_to_all | solution.py:40
  70.5 3.9 %copy-start.2 = (bf16[608,768]{1,0:T(8,128)(2,1)}, bf16[608,768]{1,0:T(8,128)(2,1)S(1)}, u32[]{:S(2)}) copy-start(bf16[608,768]{1,0:T(8,128)(2,1)S(1)} %collective-permute-done) | copy-start | bytes 2801668
  70.5 6.1 %collective-permute-start.2 = (bf16[608,768]{1,0:T(8,128)(2,1)S(1)}, bf16[608,768]{1,0:T(8,128)(2,1)S(1)}, u32[]{:S(2)}, u32[]{:S(2)}) collective-permute-start(bf16[608,768]{1,0:T(8,128)(2,1)S(1)} %collective-permute-done), channel_id=1, source_target_pairs={{0,256},{256,0},{1,257},{257,1},{2,258},{258,2},{3,259},{259,3},{4... | collective-permute-start | bytes 2801672 | tf_op jit(solution)/shard_map/ppermute | solution.py:80
  76.6 0.9 copy-start.4
  91.3 15.5 %collective-permute-start.3 = (bf16[512,304]{1,0:T(8,128)(2,1)}, bf16[512,304]{1,0:T(8,128)(2,1)S(1)}, u32[]{:S(2)}, u32[]{:S(2)}) collective-permute-start(bf16[512,304]{1,0:T(8,128)(2,1)} %bitcast.15), channel_id=1, source_target_pairs={{0,128},{128,0},{1,129},{129,1},{2,130},{130,2},{3,131},{131,3},{4... | collective-permute-start | bytes 933896 | tf_op jit(solution)/shard_map/ppermute | solution.py:44
  95.1 20.5 %all-to-all-start.2 = ((bf16[8,256,256]{1,2,0:T(8,128)(2,1)}), bf16[8,256,256]{1,2,0:T(8,128)(2,1)S(1)}, u32[]{:S(2)}, u32[]{:S(2)}) async-start(bf16[8,256,256]{1,2,0:T(8,128)(2,1)} %broadcast_in_dim.23), calls=%async_computation.2 | async-start | bytes 2097152 | tf_op jit(solution)/shard_map/all_to_all | solution.py:40
  109.7 4.3 %collective-permute-start.4 = (bf16[1024,304]{0,1:T(8,128)(2,1)}, bf16[1024,304]{0,1:T(8,128)(2,1)}, u32[]{:S(2)}, u32[]{:S(2)}) collective-permute-start(bf16[1024,304]{0,1:T(8,128)(2,1)} %copy.65), channel_id=1, source_target_pairs={{0,256},{256,0},{1,257},{257,1},{2,258},{258,2},{3,259},{259,3},{4... | collective-permute-start | bytes 1867784 | tf_op jit(solution)/shard_map/ppermute | solution.py:44
  115.4 1.0 copy-start.9
  115.5 3.1 %copy-start.7 = (bf16[2,38,8,1024]{3,2,0,1:T(8,128)(2,1)}, bf16[2,38,8,1024]{3,2,0,1:T(8,128)(2,1)S(1)}, u32[]{:S(2)}) copy-start(bf16[2,38,8,1024]{3,2,0,1:T(8,128)(2,1)S(1)} %copy.80) | copy-start | bytes 3735556
  119.7 5.5 %copy-start.15 = (s32[64]{0:T(128)S(1)}, s32[64]{0:T(128)}, u32[]{:S(2)}) copy-start(s32[64]{0:T(128)} %param.15) | copy-start | bytes 772
  119.7 5.5 %copy-start.16 = (f32[64]{0:T(128)S(1)}, f32[64]{0:T(128)}, u32[]{:S(2)}) copy-start(f32[64]{0:T(128)} %param.14) | copy-start | bytes 772
  119.7 21.6 %all-to-all-start.3 = ((bf16[8,256,304]{1,2,0:T(8,128)(2,1)}), bf16[8,256,304]{1,2,0:T(8,128)(2,1)S(1)}, u32[]{:S(2)}, u32[]{:S(2)}) async-start(bf16[8,256,304]{1,2,0:T(8,128)(2,1)} %broadcast_in_dim.24), calls=%async_computation.3 | async-start | bytes 2490368 | tf_op jit(solution)/shard_map/all_to_all | solution.py:40
  141.3 0.7 copy-start.13
  143.4 1.2 copy-start.3
  145.1 1.8 copy-start.5
  150.0 5.7 %copy-start.18 = (f32[64]{0:T(128)S(1)}, f32[64]{0:T(128)}, u32[]{:S(2)}) copy-start(f32[64]{0:T(128)} %fusion.51) | copy-start | bytes 772
  150.0 5.8 %copy-start.17 = (f32[64]{0:T(128)S(1)}, f32[64]{0:T(128)}, u32[]{:S(2)}) copy-start(f32[64]{0:T(128)} %param.14) | copy-start | bytes 772
  150.0 6.0 %copy-start.19 = (f32[2,64]{1,0:T(2,128)S(1)}, f32[2,64]{1,0:T(2,128)}, u32[]{:S(2)}) copy-start(f32[2,64]{1,0:T(2,128)} %param.17) | copy-start | bytes 1540
  150.0 18.4 %all-to-all-start.4 = ((bf16[8,256,256]{1,2,0:T(8,128)(2,1)}), bf16[8,256,256]{1,2,0:T(8,128)(2,1)S(1)}, u32[]{:S(2)}, u32[]{:S(2)}) async-start(bf16[8,256,256]{1,2,0:T(8,128)(2,1)} %broadcast_in_dim.26), calls=%async_computation.4 | async-start | bytes 2097152 | tf_op jit(solution)/shard_map/all_to_all | solution.py:40
  168.4 2.3 %copy-start = (bf16[8,256,256]{1,2,0:T(8,128)(2,1)}, bf16[8,256,256]{1,2,0:T(8,128)(2,1)S(1)}, u32[]{:S(2)}) copy-start(bf16[8,256,256]{1,2,0:T(8,128)(2,1)S(1)} %all-to-all-done.4) | copy-start | bytes 3145732
  170.8 1.4 copy-start.6
  172.2 3.9 %collective-permute-start.5 = (bf16[1024,304]{0,1:T(8,128)(2,1)S(1)}, bf16[1024,304]{0,1:T(8,128)(2,1)S(1)}, u32[]{:S(2)}, u32[]{:S(2)}) collective-permute-start(bf16[1024,304]{0,1:T(8,128)(2,1)S(1)} %fusion.24), channel_id=1, source_target_pairs={{0,256},{256,0},{1,257},{257,1},{2,258},{258,2},{3,259},{259,3},{4... | collective-permute-start | bytes 1867784 | tf_op jit(solution)/shard_map/ppermute | solution.py:53
  180.0 13.1 %collective-permute-start.6 = (bf16[512,304]{0,1:T(8,128)(2,1)}, bf16[512,304]{0,1:T(8,128)(2,1)}, u32[]{:S(2)}, u32[]{:S(2)}) collective-permute-start(bf16[512,304]{0,1:T(8,128)(2,1)} %bitcast.161), channel_id=1, source_target_pairs={{0,128},{128,0},{1,129},{129,1},{2,130},{130,2},{3,131},{131,3},{4... | collective-permute-start | bytes 933896 | tf_op jit(solution)/shard_map/ppermute | solution.py:53
  184.5 16.5 %copy-start.1 = (bf16[8,256,256]{1,2,0:T(8,128)(2,1)S(1)}, bf16[8,256,256]{1,2,0:T(8,128)(2,1)}, u32[]{:S(2)}) copy-start(bf16[8,256,256]{1,2,0:T(8,128)(2,1)} %copy-done) | copy-start | bytes 3145732
  184.5 16.5 %copy-start.8 = (bf16[2,38,8,1024]{3,2,0,1:T(8,128)(2,1)S(1)}, bf16[2,38,8,1024]{3,2,0,1:T(8,128)(2,1)}, u32[]{:S(2)}) copy-start(bf16[2,38,8,1024]{3,2,0,1:T(8,128)(2,1)} %copy-done.7) | copy-start | bytes 3735556
  184.5 16.5 %copy-start.10 = (f32[1,256,304]{1,2,0:T(8,128)S(1)}, f32[1,256,304]{1,2,0:T(8,128)}, u32[]{:S(2)}) copy-start(f32[1,256,304]{1,2,0:T(8,128)} %param.9) | copy-start | bytes 933892
  195.1 27.8 %all-to-all-start.5 = ((bf16[16,32,304]{2,1,0:T(8,128)(2,1)}), bf16[16,32,304]{2,1,0:T(8,128)(2,1)S(1)}, u32[]{:S(2)}, u32[]{:S(2)}) async-start(bf16[16,32,304]{2,1,0:T(8,128)(2,1)} %bitcast.45), calls=%async_computation.5 | async-start | bytes 786432 | tf_op jit(solution)/shard_map/all_to_all | solution.py:173
